TPU v7x, 128 devices: a whole 4x4x4 slice. The times are simulated.
128 devices in a mesh: shard: 32 (over x, y, core), tensor: 4 (over z).
Axes of the slice: x: 4, y: 4, z: 4, core: 2. Of those that a mesh axis runs over, the one named last changes fastest.
Arguments:
- grads: bfloat16 [384, 256, 256], P('shard', 'tensor'), may hold values from -60 to 60
- owner: int32 [384], replicated, may hold values from 0 to 31, as said below
- slot: int32 [384], replicated, may hold values from 0 to 23, as said below
- stat_left: float32 [768, 256, 256], P('shard', 'tensor'), may hold values from -144 to 2704, as said below
- stat_right: float32 [768, 256, 256], P('shard', 'tensor'), may hold values from -144 to 2704, as said below
- root_left: float32 [768, 256, 256], P('shard', 'tensor'), may hold values from -0.72 to 2.72, as said below
- root_right: float32 [768, 256, 256], P('shard'), may hold values from -0.72 to 2.72, as said below
- moment: float32 [768, 256, 256], P('shard', 'tensor'), may hold values from 0.1 to 10
- momentum: float32 [768, 256, 256], P('shard', 'tensor'), may hold values from -6 to 6
- master: float32 [768, 256, 256], P('shard', 'tensor'), may hold values from -0.3 to 0.3
Outputs:
- stat_left_new: float32 [768, 256, 256], P('shard', 'tensor')
- stat_right_new: float32 [768, 256, 256], P('shard', 'tensor')
- moment_new: float32 [768, 256, 256], P('shard', 'tensor')
- momentum_new: float32 [768, 256, 256], P('shard', 'tensor')
- master_new: float32 [768, 256, 256], P('shard', 'tensor')
- weights_new: bfloat16 [384, 256, 256], P('shard', 'tensor')
Inputs may be any that keep to these rules, and one draw needn't show every extreme that they name: Each owner group holds at most 24 blocks, some exactly 24; no owner group holds two blocks of one shard group (blocks b with equal b // 12). `slot`: the blocks of one owner group have distinct slots. `stat_left`: Symmetric. `stat_right`: Symmetric. `root_left`: Symmetric. `root_right`: Symmetric.
All inputs are finite; a program needn't handle non-finite values.
Results may differ from a plain program's by a relative error of at most 0.001.
Values may be sent and summed in bfloat16 or wider, within the bound.
No kernel may reach another device: no remote copies, remote signals or barrier semaphores. Data moves between devices by JAX's collectives and lax.ppermute only.
A program may use at most 128 MiB of HBM per device.

v0:
```python
import jax
import jax.numpy as jnp
from jax import lax
from jax.sharding import PartitionSpec as P


beta_stat = 0.95
beta_mom = 0.9
learn_rate = 0.01
eps_root = 1e-08
eps_mean = 1e-06


def gather_rows(piece, far_right, splits, tensor_index):
    right = [(i, (i + 1) % splits) for i in range(splits)]
    left = [(i, (i - 1) % splits) for i in range(splits)]
    from_left = lax.ppermute(piece, "tensor", right)
    from_right = lax.ppermute(piece, "tensor", left)
    if far_right:
        far = lax.ppermute(from_left, "tensor", right)
    else:
        far = lax.ppermute(from_right, "tensor", left)
    by_shift = (piece, from_right, far, from_left)

    def ordered(first):
        return lambda: jnp.concatenate([by_shift[(p - first) % splits] for p in range(splits)], 1)

    return lax.switch(tensor_index, [ordered(first) for first in range(splits)])


def pick(source, index, valid):
    taken = jnp.take(source, index, axis=0, mode="clip")
    return jnp.where(valid[:, None, None], taken, jnp.zeros((), source.dtype))


def on_device(
    grads, owner, slot, stat_left, stat_right, root_left, root_right, moment, momentum, master
):
    groups = lax.axis_size("shard")
    splits = lax.axis_size("tensor")
    slots_dev = stat_left.shape[0]
    rows_dev = stat_left.shape[1]
    order = stat_left.shape[2]
    blocks_group = grads.shape[0]
    shard_index = lax.axis_index("shard")
    tensor_index = lax.axis_index("tensor")
    owner_grid = owner.reshape(groups, blocks_group)
    slot_grid = slot.reshape(groups, blocks_group)
    local_owner = lax.dynamic_index_in_dim(owner_grid, shard_index, 0, keepdims=False)
    hit_mask = owner_grid == shard_index
    slot_ids = jnp.arange(slots_dev, dtype=jnp.int32)
    group_ids = jnp.arange(groups, dtype=jnp.int32)
    slot_match = jnp.any(
        (slot_grid[None, :, :] == slot_ids[:, None, None]) & hit_mask[None, :, :], axis=2
    )
    src_of_slot = jnp.argmax(slot_match, axis=1).astype(jnp.int32)
    slot_filled = jnp.any(slot_match, axis=1)
    slot_of_src = jnp.argmax(slot_match, axis=0).astype(jnp.int32)
    src_sent = jnp.any(slot_match, axis=0)
    dest_match = local_owner[None, :] == group_ids[:, None]
    block_of_dest = jnp.argmax(dest_match, axis=1).astype(jnp.int32)
    dest_used = jnp.any(dest_match, axis=1)
    row_start = tensor_index * rows_dev
    outgoing = pick(grads, block_of_dest, dest_used)
    arrived = lax.all_to_all(outgoing, "shard", split_axis=0, concat_axis=0, tiled=True)
    half = slots_dev // 2
    first_half = pick(arrived, src_of_slot[:half], slot_filled[:half])
    second_half = pick(arrived, src_of_slot[half:], slot_filled[half:])
    grad_piece = jnp.concatenate([first_half, second_half], 0)
    whole_halves = [
        gather_rows(first_half, True, splits, tensor_index),
        gather_rows(second_half, False, splits, tensor_index),
    ]
    grad_whole = jnp.concatenate(whole_halves, 0)
    f32 = jnp.float32
    grad_cols = lax.dynamic_slice_in_dim(grad_whole, row_start, rows_dev, 2)
    left_new = beta_stat * stat_left + (1.0 - beta_stat) * jnp.einsum(
        "kij,klj->kil", grad_piece, grad_whole, preferred_element_type=f32
    )
    right_new = beta_stat * stat_right + (1.0 - beta_stat) * jnp.einsum(
        "kji,kjl->kil", grad_cols, grad_whole, preferred_element_type=f32
    )
    grad_rows = grad_piece.astype(f32)
    second_new = beta_stat * moment + (1.0 - beta_stat) * grad_rows * grad_rows
    adam_step = grad_rows / (jnp.sqrt(second_new) + eps_root)
    three_pass = lax.DotAlgorithmPreset.BF16_BF16_F32_X3
    precond_parts = []
    for part, whole in enumerate(whole_halves):
        lo = part * half
        mixed = jnp.einsum(
            "kij,kjl->kil", root_left[lo : lo + half], whole.astype(f32),
            precision=three_pass, preferred_element_type=f32,
        )
        precond_parts.append(jnp.einsum(
            "kij,kjl->kil", mixed, root_right[lo : lo + half], precision=three_pass,
            preferred_element_type=f32,
        ))
    precond = jnp.concatenate(precond_parts, 0)
    precond_sq = jnp.concatenate([jnp.sum(p * p, axis=(1, 2)) for p in precond_parts])
    sums = jnp.stack(
        [jnp.sum(adam_step * adam_step, axis=(1, 2)), precond_sq]
    )
    step = 1
    while step < splits:
        sums = sums + lax.ppermute(sums, "tensor", [(i, i ^ step) for i in range(splits)])
        step *= 2
    adam_sum, precond_sum = sums[0], sums[1]
    entries = float(rows_dev * splits * order)
    scale_ratio = jnp.sqrt(adam_sum / entries + eps_mean) / jnp.sqrt(
        precond_sum / entries + eps_mean
    )
    velocity_new = beta_mom * momentum + (1.0 - beta_mom) * scale_ratio[:, None, None] * precond
    weight_new = master - learn_rate * velocity_new
    weight_half = weight_new.astype(jnp.bfloat16)
    returning = pick(weight_half, slot_of_src, src_sent)
    back_rows = lax.all_to_all(returning, "shard", split_axis=0, concat_axis=0, tiled=True)
    weights_local = jnp.take(back_rows, local_owner, axis=0)
    return (left_new, right_new, second_new, velocity_new, weight_new, weights_local)


def solution(mesh):
    placed = (
        P("shard", "tensor", None),
        P(),
        P(),
        P("shard", "tensor", None),
        P("shard", "tensor", None),
        P("shard", "tensor", None),
        P("shard", None, None),
        P("shard", "tensor", None),
        P("shard", "tensor", None),
        P("shard", "tensor", None),
    )

    return jax.shard_map(
        on_device,
        mesh=mesh,
        in_specs=placed,
        out_specs=(
            P("shard", "tensor", None),
            P("shard", "tensor", None),
            P("shard", "tensor", None),
            P("shard", "tensor", None),
            P("shard", "tensor", None),
            P("shard", "tensor", None),
        ),
        check_vma=False,
    )
```

profile of v0, /device:TPU:1, one launch (start us, length us, event | category | flops | bytes accessed | tf_op | source)
XLA Modules:
  0.0 112.5 jit_solution(7108237873843504075)
XLA Ops:
  0.7 0.8 reshape.87
  3.3 1.1 broadcast_select_fusion.1
  4.5 8.7 %all-to-all-start = ((bf16[32,64,256]{2,1,0:T(8,128)(2,1)}), bf16[32,64,256]{2,1,0:T(8,128)(2,1)S(1)}, u32[]{:S(2)}, u32[]{:S(2)}) async-start(bf16[32,64,256]{2,1,0:T(8,128)(2,1)} %broadcast_select_fusion.1), calls=%async_computation | async-start | bytes 2097152 | tf_op jit(solution)/shard_map/all_to_all | solution.py:65
  13.5 0.7 fusion.23
  14.9 15.2 %all-to-all-done = bf16[32,64,256]{2,1,0:T(8,128)(2,1)S(1)} async-done(((bf16[32,64,256]{2,1,0:T(8,128)(2,1)}), bf16[32,64,256]{2,1,0:T(8,128)(2,1)S(1)}, u32[]{:S(2)}, u32[]{:S(2)}) %all-to-all-start) | async-done | bytes 1048608 | tf_op jit(solution)/shard_map/all_to_all | solution.py:65
  30.8 1.7 %collective-permute-start.1 = (bf16[12,64,256]{2,1,0:T(8,128)(2,1)S(1)}, bf16[12,64,256]{2,1,0:T(8,128)(2,1)S(1)}, u32[]{:S(2)}, u32[]{:S(2)}) collective-permute-start(bf16[12,64,256]{2,1,0:T(8,128)(2,1)S(1)} %broadcast_select_fusion.4), channel_id=1, source_target_pairs={{0,1},{1,2},{2,3},{3,0},{4,5},{5,6},{6,7},{7,4},{8,9},{9,10},{10,1... | collective-permute-start | bytes 1179656 | tf_op jit(solution)/shard_map/ppermute | solution.py:17
  33.2 2.2 %collective-permute-start.3 = (bf16[12,64,256]{2,1,0:T(8,128)(2,1)S(1)}, bf16[12,64,256]{2,1,0:T(8,128)(2,1)S(1)}, u32[]{:S(2)}, u32[]{:S(2)}) collective-permute-start(bf16[12,64,256]{2,1,0:T(8,128)(2,1)S(1)} %broadcast_select_fusion.3), channel_id=1, source_target_pairs={{0,3},{1,0},{2,1},{3,2},{4,7},{5,4},{6,5},{7,6},{8,11},{9,8},{10,9... | collective-permute-start | bytes 1179656 | tf_op jit(solution)/shard_map/ppermute | solution.py:18
  35.4 1.5 %collective-permute-start = (bf16[12,64,256]{2,1,0:T(8,128)(2,1)S(1)}, bf16[12,64,256]{2,1,0:T(8,128)(2,1)S(1)}, u32[]{:S(2)}, u32[]{:S(2)}) collective-permute-start(bf16[12,64,256]{2,1,0:T(8,128)(2,1)S(1)} %broadcast_select_fusion.4), channel_id=1, source_target_pairs={{0,3},{1,0},{2,1},{3,2},{4,7},{5,4},{6,5},{7,6},{8,11},{9,8},{10,9... | collective-permute-start | bytes 1179656 | tf_op jit(solution)/shard_map/ppermute | solution.py:18
  36.8 7.2 %collective-permute-done.1 = bf16[12,64,256]{2,1,0:T(8,128)(2,1)S(1)} collective-permute-done((bf16[12,64,256]{2,1,0:T(8,128)(2,1)S(1)}, bf16[12,64,256]{2,1,0:T(8,128)(2,1)S(1)}, u32[]{:S(2)}, u32[]{:S(2)}) %collective-permute-start.1) | collective-permute-done | bytes 393248 | tf_op jit(solution)/shard_map/ppermute | solution.py:17
  44.0 0.7 collective-permute-start.5
  44.7 2.5 %collective-permute-start.4 = (bf16[12,64,256]{2,1,0:T(8,128)(2,1)S(1)}, bf16[12,64,256]{2,1,0:T(8,128)(2,1)S(1)}, u32[]{:S(2)}, u32[]{:S(2)}) collective-permute-start(bf16[12,64,256]{2,1,0:T(8,128)(2,1)S(1)} %collective-permute-done.3), channel_id=1, source_target_pairs={{0,3},{1,0},{2,1},{3,2},{4,7},{5,4},{6,5},{7,6},{8,11},{9,8},{10,9... | collective-permute-start | bytes 1179656 | tf_op jit(solution)/shard_map/ppermute | solution.py:22
  47.1 3.9 %fusion.11 = (f32[24]{0:T(128)}, f32[24,64,256]{2,1,0:T(8,128)}) fusion(bf16[12,64,256]{2,1,0:T(8,128)(2,1)S(1)} %broadcast_select_fusion.3, bf16[12,64,256]{2,1,0:T(8,128)(2,1)S(1)} %broadcast_select_fusion.4, f32[24,64,256]{2,1,0:T(8,128)} %param.25), kind=kLoop, calls=%fused_computation.32 | loop fusion | flops 3932136 | bytes 3932256 | tf_op jit(solution)/shard_map/reduce_sum | solution.py:101
  51.1 1.2 %collective-permute-done = bf16[12,64,256]{2,1,0:T(8,128)(2,1)S(1)} collective-permute-done((bf16[12,64,256]{2,1,0:T(8,128)(2,1)S(1)}, bf16[12,64,256]{2,1,0:T(8,128)(2,1)S(1)}, u32[]{:S(2)}, u32[]{:S(2)}) %collective-permute-start) | collective-permute-done | bytes 393248 | tf_op jit(solution)/shard_map/ppermute | solution.py:18
  52.3 2.9 %collective-permute-done.2 = bf16[12,64,256]{2,1,0:T(8,128)(2,1)S(1)} collective-permute-done((bf16[12,64,256]{2,1,0:T(8,128)(2,1)S(1)}, bf16[12,64,256]{2,1,0:T(8,128)(2,1)S(1)}, u32[]{:S(2)}, u32[]{:S(2)}) %collective-permute-start.2) | collective-permute-done | bytes 393248 | tf_op jit(solution)/shard_map/ppermute | solution.py:20
  55.2 1.3 %conditional.2 = (bf16[12,256,256]{2,1,0:T(8,128)(2,1)}) conditional(s32[]{:T(128)} %clamp.4, (bf16[12,64,256]{2,1,0:T(8,128)(2,1)S(1)}, bf16[12,64,256]{2,1,0:T(8,128)(2,1)S(1)}, bf16[12,64,256]{2,1,0:T(8,128)(2,1)S(1)}, bf16[12,64,256]{2,1,0:T(8,128)(2,1)S(1)}) %tuple.38, (bf16[12,64,256]{2,1,0:T(8,128)(2,1)S(1)}, ...), branch_computations={%region_5.6_spmd, %region_6.7_spmd, %region_7.8_spmd, %region_8.9_... | conditional | flops 6291456 | bytes 3145736 | solution.py:28
  55.2 1.3 %pad_maximum_fusion = bf16[12,256,256]{2,1,0:T(8,128)(2,1)} fusion(bf16[12,64,256]{2,1,0:T(8,128)(2,1)S(1)} %get-tuple-element.72, bf16[12,64,256]{2,1,0:T(8,128)(2,1)S(1)} %get-tuple-element.71, bf16[12,64,256]{2,1,0:T(8,128)(2,1)S(1)} %get-tuple-element.70, bf16[12,64,256]{2,1,0:T(8,128)(2,1)S(1)} %get-tuple-element.64), kind=kLoop, calls=%fused_computation.5 | loop fusion | flops 6291456 | bytes 3145728 | tf_op jit(solution)/shard_map/cond/branch_0_fun/concatenate | solution.py:26
  56.4 4.9 %multiply_reduce_fusion.1 = (f32[12]{0:T(128)}, f32[12,64,256]{2,1,0:T(8,128)S(1)}) fusion(f32[24,256,256]{2,1,0:T(8,128)} %param.24, bf16[12,256,256]{2,1,0:T(8,128)(2,1)} %get-tuple-element.138, f32[24,64,256]{2,1,0:T(8,128)} %param.23), kind=kOutput, calls=%fused_computation.40 | convolution fusion | flops 604372992 | bytes 6291504 | tf_op jit(solution)/shard_map/kij,kjl->kil/dot_general | solution.py:94
  61.3 2.3 %collective-permute-done.5 = bf16[12,64,256]{2,1,0:T(8,128)(2,1)S(1)} collective-permute-done((bf16[12,64,256]{2,1,0:T(8,128)(2,1)S(1)}, bf16[12,64,256]{2,1,0:T(8,128)(2,1)S(1)}, u32[]{:S(2)}, u32[]{:S(2)}) %collective-permute-start.5) | collective-permute-done | bytes 393248 | tf_op jit(solution)/shard_map/ppermute | solution.py:17
  63.6 1.3 %conditional.3 = (bf16[12,256,256]{2,1,0:T(8,128)(2,1)}) conditional(s32[]{:T(128)} %clamp.4, (bf16[12,64,256]{2,1,0:T(8,128)(2,1)S(1)}, bf16[12,64,256]{2,1,0:T(8,128)(2,1)S(1)}, bf16[12,64,256]{2,1,0:T(8,128)(2,1)S(1)}, bf16[12,64,256]{2,1,0:T(8,128)(2,1)S(1)}) %tuple.42, (bf16[12,64,256]{2,1,0:T(8,128)(2,1)S(1)}, ...), branch_computations={%region_9.10_spmd, %region_10.11_spmd, %region_11.12_spmd, %region... | conditional | flops 6291456 | bytes 3145736 | solution.py:28
  63.6 1.3 %pad_maximum_fusion.4 = bf16[12,256,256]{2,1,0:T(8,128)(2,1)} fusion(bf16[12,64,256]{2,1,0:T(8,128)(2,1)S(1)} %get-tuple-element.93, bf16[12,64,256]{2,1,0:T(8,128)(2,1)S(1)} %get-tuple-element.92, bf16[12,64,256]{2,1,0:T(8,128)(2,1)S(1)} %get-tuple-element.91, bf16[12,64,256]{2,1,0:T(8,128)(2,1)S(1)} %get-tuple-element.90), kind=kLoop, calls=%fused_computation.9 | loop fusion | flops 6291456 | bytes 3145728 | tf_op jit(solution)/shard_map/cond/branch_0_fun/concatenate | solution.py:26
  64.9 4.4 %multiply_reduce_fusion = (f32[12]{0:T(128)S(1)}, f32[12,64,256]{2,1,0:T(8,128)S(1)}) fusion(f32[24,256,256]{2,1,0:T(8,128)} %param.24, bf16[12,256,256]{2,1,0:T(8,128)(2,1)} %get-tuple-element.139, f32[24,64,256]{2,1,0:T(8,128)} %param.23), kind=kOutput, calls=%fused_computation.38 | convolution fusion | flops 604372992 | bytes 6291504 | tf_op jit(solution)/shard_map/kij,kjl->kil/dot_general | solution.py:94
  70.0 1.9 %collective-permute-done.6 = f32[2,24]{1,0:T(2,128)S(1)} collective-permute-done((f32[2,24]{1,0:T(2,128)S(1)}, f32[2,24]{1,0:T(2,128)S(1)}, u32[]{:S(2)}, u32[]{:S(2)}) %collective-permute-start.6) | collective-permute-done | bytes 224 | tf_op jit(solution)/shard_map/ppermute | solution.py:105
  72.7 3.2 %collective-permute-done.7 = f32[2,24]{1,0:T(2,128)S(1)} collective-permute-done((f32[2,24]{1,0:T(2,128)S(1)}, f32[2,24]{1,0:T(2,128)S(1)}, u32[]{:S(2)}, u32[]{:S(2)}) %collective-permute-start.7) | collective-permute-done | bytes 224 | tf_op jit(solution)/shard_map/ppermute | solution.py:105
  75.9 4.3 %fusion.34 = (bf16[24,64,256]{2,1,0:T(8,128)(2,1)S(1)}, f32[24,64,256]{2,1,0:T(8,128)}, f32[24,64,256]{2,1,0:T(8,128)}) fusion(f32[24,64,256]{2,1,0:T(8,128)} %param.27, f32[12,64,256]{2,1,0:T(8,128)S(1)} %get-tuple-element.133, f32[12,64,256]{2,1,0:T(8,128)S(1)} %get-tuple-element.135, f32[24]{0:T(128)S(1)} %multiply_bitcast_fusion, f32[24,64,256]{2,1,0:T(8,128)} %param.26), kind=kLoop, calls=%fused_computation.74 | loop fusion | flops 2752512 | bytes 8650848 | tf_op jit(solution)/shard_map/convert_element_type | solution.py:114
  80.3 1.9 %gather_fusion.3 = bf16[32,64,256]{2,1,0:T(8,128)(2,1)} fusion(bf16[24,64,256]{2,1,0:T(8,128)(2,1)S(1)} %get-tuple-element.123, s32[1024]{0:T(1024)} %pad_clamp_fusion.1), kind=kCustom, calls=%fused_computation.3 | custom fusion | bytes 2097280 | tf_op jit(solution)/shard_map/jit(_take)/gather | solution.py:32
  82.2 2.4 %broadcast_select_fusion = bf16[32,64,256]{2,1,0:T(8,128)(2,1)} fusion(bf16[32,64,256]{2,1,0:T(8,128)(2,1)} %gather_fusion.3, pred[32]{0:T(512)(128)(4,1)S(1)} %copy-done.6), kind=kLoop, calls=%fused_computation.35 | loop fusion | flops 524288 | bytes 2097184 | tf_op jit(solution)/shard_map/jit(_where)/select_n | solution.py:33
  84.6 8.2 %all-to-all-start.1 = ((bf16[32,64,256]{2,1,0:T(8,128)(2,1)}), bf16[32,64,256]{2,1,0:T(8,128)(2,1)}, u32[]{:S(2)}, u32[]{:S(2)}) async-start(bf16[32,64,256]{2,1,0:T(8,128)(2,1)} %broadcast_select_fusion), calls=%async_computation.1 | async-start | bytes 2097152 | tf_op jit(solution)/shard_map/all_to_all | solution.py:116
  92.9 4.2 %multiply_add_fusion.1 = f32[24,64,256]{2,1,0:T(8,128)} fusion(f32[24,64,256]{2,1,0:T(8,128)} %param.21, bf16[12,256,256]{2,1,0:T(8,128)(2,1)} %get-tuple-element.139, bf16[12,256,256]{2,1,0:T(8,128)(2,1)S(1)} %copy-done.1, bf16[12,64,256]{2,1,0:T(8,128)(2,1)S(1)} %broadcast_select_fusion.3, bf16[12,64,256]{2,1,0:T(8,128)(2,1)S(1)} %broadcast_select_fusion.4), kind=kOutput, calls=%fused_computation.31 | convolution fusion | flops 204472320 | bytes 7077888 | tf_op jit(solution)/shard_map/kij,klj->kil/dot_general | solution.py:77
  97.1 2.5 %multiply_add_fusion = f32[24,64,256]{2,1,0:T(8,128)} fusion(f32[24,64,256]{2,1,0:T(8,128)S(1)} %copy-done.10, bf16[12,256,256]{2,1,0:T(8,128)(2,1)S(1)} %copy-done.2, bf16[12,256,256]{2,1,0:T(8,128)(2,1)S(1)} %copy-done.1, s32[]{:T(128)S(6)} %select_n.57), kind=kOutput, calls=%fused_computation.30 | convolution fusion | flops 205651968 | bytes 9437188 | tf_op jit(solution)/shard_map/kji,kjl->kil/dot_general | solution.py:80
  99.7 10.2 %all-to-all-done.1 = bf16[32,64,256]{2,1,0:T(8,128)(2,1)} async-done(((bf16[32,64,256]{2,1,0:T(8,128)(2,1)}), bf16[32,64,256]{2,1,0:T(8,128)(2,1)}, u32[]{:S(2)}, u32[]{:S(2)}) %all-to-all-start.1) | async-done | bytes 1048608 | tf_op jit(solution)/shard_map/all_to_all | solution.py:116
  109.8 1.8 %gather_fusion.4 = bf16[12,64,256]{2,1,0:T(8,128)(2,1)S(1)} fusion(bf16[32,64,256]{2,1,0:T(8,128)(2,1)} %all-to-all-done.1, s32[1024]{0:T(1024)S(1)} %pad_clamp_fusion), kind=kCustom, calls=%fused_computation.4 | custom fusion | bytes 786480 | tf_op jit(solution)/shard_map/jit(_take)/gather | solution.py:117
  111.7 0.9 broadcast_select_fusion.2
  (53 shorter events, 5.8 us)
Async XLA Ops:
  0.6 2.1 %copy-start = (bf16[12,64,256]{2,1,0:T(8,128)(2,1)S(1)}, bf16[12,64,256]{2,1,0:T(8,128)(2,1)}, u32[]{:S(2)}) copy-start(bf16[12,64,256]{2,1,0:T(8,128)(2,1)} %param.18) | copy-start | bytes 1179652
  4.5 8.8 %copy-start.7 = (s32[384]{0:T(512)S(1)}, s32[384]{0:T(512)}, u32[]{:S(2)}) copy-start(s32[384]{0:T(512)} %param.20) | copy-start | bytes 4612
  4.5 25.6 %all-to-all-start = ((bf16[32,64,256]{2,1,0:T(8,128)(2,1)}), bf16[32,64,256]{2,1,0:T(8,128)(2,1)S(1)}, u32[]{:S(2)}, u32[]{:S(2)}) async-start(bf16[32,64,256]{2,1,0:T(8,128)(2,1)} %broadcast_select_fusion.1), calls=%async_computation | async-start | bytes 2097152 | tf_op jit(solution)/shard_map/all_to_all | solution.py:65
  14.1 16.5 %copy-start.3 = (pred[24,32]{1,0:T(8,128)(4,1)}, pred[24,32]{1,0:T(8,128)(4,1)S(1)}, u32[]{:S(2)}) copy-start(pred[24,32]{1,0:T(8,128)(4,1)S(1)} %get-tuple-element.119) | copy-start | bytes 2308
  30.8 13.2 %collective-permute-start.1 = (bf16[12,64,256]{2,1,0:T(8,128)(2,1)S(1)}, bf16[12,64,256]{2,1,0:T(8,128)(2,1)S(1)}, u32[]{:S(2)}, u32[]{:S(2)}) collective-permute-start(bf16[12,64,256]{2,1,0:T(8,128)(2,1)S(1)} %broadcast_select_fusion.4), channel_id=1, source_target_pairs={{0,1},{1,2},{2,3},{3,0},{4,5},{5,6},{6,7},{7,4},{8,9},{9,10},{10,1... | collective-permute-start | bytes 1179656 | tf_op jit(solution)/shard_map/ppermute | solution.py:17
  33.2 11.5 %collective-permute-start.3 = (bf16[12,64,256]{2,1,0:T(8,128)(2,1)S(1)}, bf16[12,64,256]{2,1,0:T(8,128)(2,1)S(1)}, u32[]{:S(2)}, u32[]{:S(2)}) collective-permute-start(bf16[12,64,256]{2,1,0:T(8,128)(2,1)S(1)} %broadcast_select_fusion.3), channel_id=1, source_target_pairs={{0,3},{1,0},{2,1},{3,2},{4,7},{5,4},{6,5},{7,6},{8,11},{9,8},{10,9... | collective-permute-start | bytes 1179656 | tf_op jit(solution)/shard_map/ppermute | solution.py:18
  35.4 16.9 %collective-permute-start = (bf16[12,64,256]{2,1,0:T(8,128)(2,1)S(1)}, bf16[12,64,256]{2,1,0:T(8,128)(2,1)S(1)}, u32[]{:S(2)}, u32[]{:S(2)}) collective-permute-start(bf16[12,64,256]{2,1,0:T(8,128)(2,1)S(1)} %broadcast_select_fusion.4), channel_id=1, source_target_pairs={{0,3},{1,0},{2,1},{3,2},{4,7},{5,4},{6,5},{7,6},{8,11},{9,8},{10,9... | collective-permute-start | bytes 1179656 | tf_op jit(solution)/shard_map/ppermute | solution.py:18
  44.0 11.2 %collective-permute-start.2 = (bf16[12,64,256]{2,1,0:T(8,128)(2,1)S(1)}, bf16[12,64,256]{2,1,0:T(8,128)(2,1)S(1)}, u32[]{:S(2)}, u32[]{:S(2)}) collective-permute-start(bf16[12,64,256]{2,1,0:T(8,128)(2,1)S(1)} %collective-permute-done.1), channel_id=1, source_target_pairs={{0,1},{1,2},{2,3},{3,0},{4,5},{5,6},{6,7},{7,4},{8,9},{9,10},{10,1... | collective-permute-start | bytes 1179656 | tf_op jit(solution)/shard_map/ppermute | solution.py:20
  44.0 19.6 %collective-permute-start.5 = (bf16[12,64,256]{2,1,0:T(8,128)(2,1)S(1)}, bf16[12,64,256]{2,1,0:T(8,128)(2,1)S(1)}, u32[]{:S(2)}, u32[]{:S(2)}) collective-permute-start(bf16[12,64,256]{2,1,0:T(8,128)(2,1)S(1)} %broadcast_select_fusion.3), channel_id=1, source_target_pairs={{0,1},{1,2},{2,3},{3,0},{4,5},{5,6},{6,7},{7,4},{8,9},{9,10},{10,1... | collective-permute-start | bytes 1179656 | tf_op jit(solution)/shard_map/ppermute | solution.py:17
  44.7 18.9 %collective-permute-start.4 = (bf16[12,64,256]{2,1,0:T(8,128)(2,1)S(1)}, bf16[12,64,256]{2,1,0:T(8,128)(2,1)S(1)}, u32[]{:S(2)}, u32[]{:S(2)}) collective-permute-start(bf16[12,64,256]{2,1,0:T(8,128)(2,1)S(1)} %collective-permute-done.3), channel_id=1, source_target_pairs={{0,3},{1,0},{2,1},{3,2},{4,7},{5,4},{6,5},{7,6},{8,11},{9,8},{10,9... | collective-permute-start | bytes 1179656 | tf_op jit(solution)/shard_map/ppermute | solution.py:22
  64.9 4.4 %copy-start.9 = (f32[12]{0:T(128)S(1)}, f32[12]{0:T(128)}, u32[]{:S(2)}) copy-start(f32[12]{0:T(128)} %get-tuple-element.134) | copy-start | bytes 148
  64.9 4.5 %copy-start.5 = (f32[24]{0:T(128)S(1)}, f32[24]{0:T(128)}, u32[]{:S(2)}) copy-start(f32[24]{0:T(128)} %get-tuple-element.126) | copy-start | bytes 292
  64.9 4.6 %copy-start.4 = (pred[24,32]{1,0:T(8,128)(4,1)S(1)}, pred[24,32]{1,0:T(8,128)(4,1)}, u32[]{:S(2)}) copy-start(pred[24,32]{1,0:T(8,128)(4,1)} %copy-done.3) | copy-start | bytes 2308
  69.4 2.5 %collective-permute-start.6 = (f32[2,24]{1,0:T(2,128)S(1)}, f32[2,24]{1,0:T(2,128)S(1)}, u32[]{:S(2)}, u32[]{:S(2)}) collective-permute-start(f32[2,24]{1,0:T(2,128)S(1)} %pad_maximum_fusion.17), channel_id=1, source_target_pairs={{0,1},{1,0},{2,3},{3,2},{4,5},{5,4},{6,7},{7,6},{8,9},{9,8},{10,11... | collective-permute-start | bytes 584 | tf_op jit(solution)/shard_map/ppermute | solution.py:105
  71.9 4.0 %collective-permute-start.7 = (f32[2,24]{1,0:T(2,128)S(1)}, f32[2,24]{1,0:T(2,128)S(1)}, u32[]{:S(2)}, u32[]{:S(2)}) collective-permute-start(f32[2,24]{1,0:T(2,128)S(1)} %fusion.32), channel_id=1, source_target_pairs={{0,2},{1,3},{2,0},{3,1},{4,6},{5,7},{6,4},{7,5},{8,10},{9,11},{10,... | collective-permute-start | bytes 584 | tf_op jit(solution)/shard_map/ppermute | solution.py:105
  80.3 1.9 %copy-start.6 = (pred[32]{0:T(512)(128)(4,1)S(1)}, pred[32]{0:T(512)(128)(4,1)}, u32[]{:S(2)}) copy-start(pred[32]{0:T(512)(128)(4,1)} %get-tuple-element.118) | copy-start | bytes 100
  84.6 8.3 %copy-start.1 = (bf16[12,256,256]{2,1,0:T(8,128)(2,1)S(1)}, bf16[12,256,256]{2,1,0:T(8,128)(2,1)}, u32[]{:S(2)}) copy-start(bf16[12,256,256]{2,1,0:T(8,128)(2,1)} %get-tuple-element.138) | copy-start | bytes 4718596
  84.6 25.3 %all-to-all-start.1 = ((bf16[32,64,256]{2,1,0:T(8,128)(2,1)}), bf16[32,64,256]{2,1,0:T(8,128)(2,1)}, u32[]{:S(2)}, u32[]{:S(2)}) async-start(bf16[32,64,256]{2,1,0:T(8,128)(2,1)} %broadcast_select_fusion), calls=%async_computation.1 | async-start | bytes 2097152 | tf_op jit(solution)/shard_map/all_to_all | solution.py:116
  92.8 4.3 %copy-start.2 = (bf16[12,256,256]{2,1,0:T(8,128)(2,1)S(1)}, bf16[12,256,256]{2,1,0:T(8,128)(2,1)}, u32[]{:S(2)}) copy-start(bf16[12,256,256]{2,1,0:T(8,128)(2,1)} %get-tuple-element.139) | copy-start | bytes 4718596
  92.9 4.3 %copy-start.10 = (f32[24,64,256]{2,1,0:T(8,128)S(1)}, f32[24,64,256]{2,1,0:T(8,128)}, u32[]{:S(2)}) copy-start(f32[24,64,256]{2,1,0:T(8,128)} %param.22) | copy-start | bytes 4718596
  97.1 14.5 %copy-start.8 = (pred[12]{0:T(512)(128)(4,1)S(1)}, pred[12]{0:T(512)(128)(4,1)}, u32[]{:S(2)}) copy-start(pred[12]{0:T(512)(128)(4,1)} %get-tuple-element.121) | copy-start | bytes 40
where the time goes:
time: 113 us
  waiting for transfers between devices  44 us (39%)
  starting transfers between devices  25.7 us (23%)
  other arithmetic  19.1 us (17%)
  matrix products  16.1 us (14%)
  local copies, waits for them, and re-layouts  6.75 us (6%)
    all_to_all x1, waiting for transfers between devices, on_device(): lax.all_to_all(outgoing, 'shard', split_axis=0, concat_axis=0, tiled=True)  15.2 us
    all_to_all x1, waiting for transfers between devices, on_device(): lax.all_to_all(returning, 'shard', split_axis=0, concat_axis=0, tiled=True)  10.2 us
    ppermute x2, waiting for transfers between devices, gather_rows(): from_left = lax.ppermute(piece, 'tensor', right)  9.43 us
    dot_general x2, matrix products, on_device(): jnp.einsum('kij,kjl->kil', mixed, root_right[lo:lo + half], precision=thr...  9.33 us
    all_to_all x1, starting transfers between devices, on_device(): lax.all_to_all(outgoing, 'shard', split_axis=0, concat_axis=0, tiled=True)  8.71 us
    all_to_all x1, starting transfers between devices, on_device(): lax.all_to_all(returning, 'shard', split_axis=0, concat_axis=0, tiled=True)  8.22 us
    ppermute x2, waiting for transfers between devices, on_device(): lax.ppermute(sums, 'tensor', [(i, i ^ step) for i in range(splits)])  5.09 us
    convert_element_type x1, other arithmetic, on_device(): weight_half = weight_new.astype(jnp.bfloat16)  4.32 us
  transfers between devices with their start and end apart: 10, of which 8 were waited for; matrix products, arithmetic and copies ran while one was open for 18% of the time, Pallas kernels for 0%

commit v1 on v0

--- a/solution.py
+++ b/solution.py
@@ -29,7 +29,7 @@
 
 
 def pick(source, index, valid):
-    taken = jnp.take(source, index, axis=0, mode="clip")
+    taken = source.at[index].get(mode="promise_in_bounds")
     return jnp.where(valid[:, None, None], taken, jnp.zeros((), source.dtype))
 
 
@@ -56,7 +56,6 @@
     src_of_slot = jnp.argmax(slot_match, axis=1).astype(jnp.int32)
     slot_filled = jnp.any(slot_match, axis=1)
     slot_of_src = jnp.argmax(slot_match, axis=0).astype(jnp.int32)
-    src_sent = jnp.any(slot_match, axis=0)
     dest_match = local_owner[None, :] == group_ids[:, None]
     block_of_dest = jnp.argmax(dest_match, axis=1).astype(jnp.int32)
     dest_used = jnp.any(dest_match, axis=1)
@@ -112,9 +111,9 @@
     velocity_new = beta_mom * momentum + (1.0 - beta_mom) * scale_ratio[:, None, None] * precond
     weight_new = master - learn_rate * velocity_new
     weight_half = weight_new.astype(jnp.bfloat16)
-    returning = pick(weight_half, slot_of_src, src_sent)
+    returning = weight_half.at[slot_of_src].get(mode="promise_in_bounds")
     back_rows = lax.all_to_all(returning, "shard", split_axis=0, concat_axis=0, tiled=True)
-    weights_local = jnp.take(back_rows, local_owner, axis=0)
+    weights_local = back_rows.at[local_owner].get(mode="promise_in_bounds")
     return (left_new, right_new, second_new, velocity_new, weight_new, weights_local)
 
 

time: 113 us -> 113 us (level)
  other arithmetic: 19.1 us -> 15.1 us
  waiting for transfers between devices: 44 us -> 46.6 us
    select_n x4 -> x3, other arithmetic: 3.7 us -> 1.3 us  [pick(): return jnp.where(valid[:, None, None], taken, jnp.zeros((), source.dtype))]
    ppermute x2, waiting for transfers between devices: 5.09 us -> 6.22 us  [on_device(): lax.ppermute(sums, 'tensor', [(i, i ^ step) for i in range(splits)])]
  transfers between devices with their start and end apart: 10 -> 10, of which waited for: 8 -> 8; matrix products, arithmetic and copies ran while one was open for 18% -> 16% of each run, Pallas kernels for 0% -> 0%
where the time goes in v1:
time: 113 us; the launch traced here: 112 us
  waiting for transfers between devices  46.6 us (41%)
  starting transfers between devices  25.6 us (23%)
  matrix products  16.4 us (15%)
  other arithmetic  15.1 us (13%)
  local copies, waits for them, and re-layouts  7.85 us (7%)
    all_to_all x1, waiting for transfers between devices, on_device(): lax.all_to_all(outgoing, 'shard', split_axis=0, concat_axis=0, tiled=True)  16.1 us
    all_to_all x1, waiting for transfers between devices, on_device(): lax.all_to_all(returning, 'shard', split_axis=0, concat_axis=0, tiled=True)  10.2 us
    ppermute x2, waiting for transfers between devices, gather_rows(): from_left = lax.ppermute(piece, 'tensor', right)  9.93 us
    dot_general x2, matrix products, on_device(): jnp.einsum('kij,kjl->kil', mixed, root_right[lo:lo + half], precision=thr...  9.6 us
    all_to_all x1, starting transfers between devices, on_device(): lax.all_to_all(outgoing, 'shard', split_axis=0, concat_axis=0, tiled=True)  8.58 us
    all_to_all x1, starting transfers between devices, on_device(): lax.all_to_all(returning, 'shard', split_axis=0, concat_axis=0, tiled=True)  8.21 us
    ppermute x2, waiting for transfers between devices, on_device(): lax.ppermute(sums, 'tensor', [(i, i ^ step) for i in range(splits)])  6.22 us
    convert_element_type x1, other arithmetic, on_device(): weight_half = weight_new.astype(jnp.bfloat16)  4.55 us
  transfers between devices with their start and end apart: 10, of which 8 were waited for; matrix products, arithmetic and copies ran while one was open for 16% of the time, Pallas kernels for 0%

profile of v1, /device:TPU:1, one launch (start us, length us, event | category | flops | bytes accessed | tf_op | source)
XLA Modules:
  0.0 112.3 jit_solution(6900349508835884022)
XLA Ops:
  0.7 0.8 reshape.80
  2.3 0.8 eq.46
  4.4 0.6 gather_fusion
  5.0 1.1 broadcast_select_fusion
  6.1 8.6 %all-to-all-start = ((bf16[32,64,256]{2,1,0:T(8,128)(2,1)}), bf16[32,64,256]{2,1,0:T(8,128)(2,1)S(1)}, u32[]{:S(2)}, u32[]{:S(2)}) async-start(bf16[32,64,256]{2,1,0:T(8,128)(2,1)} %broadcast_select_fusion), calls=%async_computation | async-start | bytes 2097152 | tf_op jit(solution)/shard_map/all_to_all | solution.py:64
  14.7 0.6 iota_reduce_fusion.1
  15.5 16.1 %all-to-all-done = bf16[32,64,256]{2,1,0:T(8,128)(2,1)S(1)} async-done(((bf16[32,64,256]{2,1,0:T(8,128)(2,1)}), bf16[32,64,256]{2,1,0:T(8,128)(2,1)S(1)}, u32[]{:S(2)}, u32[]{:S(2)}) %all-to-all-start) | async-done | bytes 1048608 | tf_op jit(solution)/shard_map/all_to_all | solution.py:64
  32.3 1.7 %collective-permute-start.1 = (bf16[12,64,256]{2,1,0:T(8,128)(2,1)S(1)}, bf16[12,64,256]{2,1,0:T(8,128)(2,1)S(1)}, u32[]{:S(2)}, u32[]{:S(2)}) collective-permute-start(bf16[12,64,256]{2,1,0:T(8,128)(2,1)S(1)} %broadcast_select_fusion.2), channel_id=1, source_target_pairs={{0,1},{1,2},{2,3},{3,0},{4,5},{5,6},{6,7},{7,4},{8,9},{9,10},{10,1... | collective-permute-start | bytes 1179656 | tf_op jit(solution)/shard_map/ppermute | solution.py:17
  34.7 2.2 %collective-permute-start.3 = (bf16[12,64,256]{2,1,0:T(8,128)(2,1)S(1)}, bf16[12,64,256]{2,1,0:T(8,128)(2,1)S(1)}, u32[]{:S(2)}, u32[]{:S(2)}) collective-permute-start(bf16[12,64,256]{2,1,0:T(8,128)(2,1)S(1)} %broadcast_select_fusion.1), channel_id=1, source_target_pairs={{0,3},{1,0},{2,1},{3,2},{4,7},{5,4},{6,5},{7,6},{8,11},{9,8},{10,9... | collective-permute-start | bytes 1179656 | tf_op jit(solution)/shard_map/ppermute | solution.py:18
  36.9 1.5 %collective-permute-start = (bf16[12,64,256]{2,1,0:T(8,128)(2,1)S(1)}, bf16[12,64,256]{2,1,0:T(8,128)(2,1)S(1)}, u32[]{:S(2)}, u32[]{:S(2)}) collective-permute-start(bf16[12,64,256]{2,1,0:T(8,128)(2,1)S(1)} %broadcast_select_fusion.2), channel_id=1, source_target_pairs={{0,3},{1,0},{2,1},{3,2},{4,7},{5,4},{6,5},{7,6},{8,11},{9,8},{10,9... | collective-permute-start | bytes 1179656 | tf_op jit(solution)/shard_map/ppermute | solution.py:18
  38.3 7.2 %collective-permute-done.1 = bf16[12,64,256]{2,1,0:T(8,128)(2,1)S(1)} collective-permute-done((bf16[12,64,256]{2,1,0:T(8,128)(2,1)S(1)}, bf16[12,64,256]{2,1,0:T(8,128)(2,1)S(1)}, u32[]{:S(2)}, u32[]{:S(2)}) %collective-permute-start.1) | collective-permute-done | bytes 393248 | tf_op jit(solution)/shard_map/ppermute | solution.py:17
  45.5 0.7 collective-permute-start.5
  46.2 2.5 %collective-permute-start.4 = (bf16[12,64,256]{2,1,0:T(8,128)(2,1)S(1)}, bf16[12,64,256]{2,1,0:T(8,128)(2,1)S(1)}, u32[]{:S(2)}, u32[]{:S(2)}) collective-permute-start(bf16[12,64,256]{2,1,0:T(8,128)(2,1)S(1)} %collective-permute-done.3), channel_id=1, source_target_pairs={{0,3},{1,0},{2,1},{3,2},{4,7},{5,4},{6,5},{7,6},{8,11},{9,8},{10,9... | collective-permute-start | bytes 1179656 | tf_op jit(solution)/shard_map/ppermute | solution.py:22
  48.7 3.9 %fusion.11 = (f32[24]{0:T(128)}, f32[24,64,256]{2,1,0:T(8,128)}) fusion(bf16[12,64,256]{2,1,0:T(8,128)(2,1)S(1)} %broadcast_select_fusion.1, bf16[12,64,256]{2,1,0:T(8,128)(2,1)S(1)} %broadcast_select_fusion.2, f32[24,64,256]{2,1,0:T(8,128)} %param.25), kind=kLoop, calls=%fused_computation.32 | loop fusion | flops 3932136 | bytes 3932256 | tf_op jit(solution)/shard_map/reduce_sum | solution.py:100
  52.6 1.2 %collective-permute-done = bf16[12,64,256]{2,1,0:T(8,128)(2,1)S(1)} collective-permute-done((bf16[12,64,256]{2,1,0:T(8,128)(2,1)S(1)}, bf16[12,64,256]{2,1,0:T(8,128)(2,1)S(1)}, u32[]{:S(2)}, u32[]{:S(2)}) %collective-permute-start) | collective-permute-done | bytes 393248 | tf_op jit(solution)/shard_map/ppermute | solution.py:18
  53.8 2.9 %collective-permute-done.2 = bf16[12,64,256]{2,1,0:T(8,128)(2,1)S(1)} collective-permute-done((bf16[12,64,256]{2,1,0:T(8,128)(2,1)S(1)}, bf16[12,64,256]{2,1,0:T(8,128)(2,1)S(1)}, u32[]{:S(2)}, u32[]{:S(2)}) %collective-permute-start.2) | collective-permute-done | bytes 393248 | tf_op jit(solution)/shard_map/ppermute | solution.py:20
  56.7 1.3 %conditional.2 = (bf16[12,256,256]{2,1,0:T(8,128)(2,1)}) conditional(s32[]{:T(128)} %clamp.4, (bf16[12,64,256]{2,1,0:T(8,128)(2,1)S(1)}, bf16[12,64,256]{2,1,0:T(8,128)(2,1)S(1)}, bf16[12,64,256]{2,1,0:T(8,128)(2,1)S(1)}, bf16[12,64,256]{2,1,0:T(8,128)(2,1)S(1)}) %tuple.38, (bf16[12,64,256]{2,1,0:T(8,128)(2,1)S(1)}, ...), branch_computations={%region_5.6_spmd, %region_6.7_spmd, %region_7.8_spmd, %region_8.9_... | conditional | flops 6291456 | bytes 3145736 | solution.py:28
  56.7 1.3 %pad_maximum_fusion = bf16[12,256,256]{2,1,0:T(8,128)(2,1)} fusion(bf16[12,64,256]{2,1,0:T(8,128)(2,1)S(1)} %get-tuple-element.72, bf16[12,64,256]{2,1,0:T(8,128)(2,1)S(1)} %get-tuple-element.71, bf16[12,64,256]{2,1,0:T(8,128)(2,1)S(1)} %get-tuple-element.70, bf16[12,64,256]{2,1,0:T(8,128)(2,1)S(1)} %get-tuple-element.64), kind=kLoop, calls=%fused_computation.5 | loop fusion | flops 6291456 | bytes 3145728 | tf_op jit(solution)/shard_map/cond/branch_0_fun/concatenate | solution.py:26
  58.0 4.4 %multiply_reduce_fusion.1 = (f32[12]{0:T(128)S(1)}, f32[12,64,256]{2,1,0:T(8,128)S(1)}) fusion(f32[24,256,256]{2,1,0:T(8,128)} %param.24, bf16[12,256,256]{2,1,0:T(8,128)(2,1)} %get-tuple-element.137, f32[24,64,256]{2,1,0:T(8,128)} %param.23), kind=kOutput, calls=%fused_computation.39 | convolution fusion | flops 604372992 | bytes 6291504 | tf_op jit(solution)/shard_map/kij,kjl->kil/dot_general | solution.py:93
  62.4 2.8 %collective-permute-done.5 = bf16[12,64,256]{2,1,0:T(8,128)(2,1)S(1)} collective-permute-done((bf16[12,64,256]{2,1,0:T(8,128)(2,1)S(1)}, bf16[12,64,256]{2,1,0:T(8,128)(2,1)S(1)}, u32[]{:S(2)}, u32[]{:S(2)}) %collective-permute-start.5) | collective-permute-done | bytes 393248 | tf_op jit(solution)/shard_map/ppermute | solution.py:17
  65.1 1.3 %conditional.3 = (bf16[12,256,256]{2,1,0:T(8,128)(2,1)}) conditional(s32[]{:T(128)} %clamp.4, (bf16[12,64,256]{2,1,0:T(8,128)(2,1)S(1)}, bf16[12,64,256]{2,1,0:T(8,128)(2,1)S(1)}, bf16[12,64,256]{2,1,0:T(8,128)(2,1)S(1)}, bf16[12,64,256]{2,1,0:T(8,128)(2,1)S(1)}) %tuple.42, (bf16[12,64,256]{2,1,0:T(8,128)(2,1)S(1)}, ...), branch_computations={%region_9.10_spmd, %region_10.11_spmd, %region_11.12_spmd, %region... | conditional | flops 6291456 | bytes 3145736 | solution.py:28
  65.1 1.3 %pad_maximum_fusion.4 = bf16[12,256,256]{2,1,0:T(8,128)(2,1)} fusion(bf16[12,64,256]{2,1,0:T(8,128)(2,1)S(1)} %get-tuple-element.93, bf16[12,64,256]{2,1,0:T(8,128)(2,1)S(1)} %get-tuple-element.92, bf16[12,64,256]{2,1,0:T(8,128)(2,1)S(1)} %get-tuple-element.91, bf16[12,64,256]{2,1,0:T(8,128)(2,1)S(1)} %get-tuple-element.90), kind=kLoop, calls=%fused_computation.9 | loop fusion | flops 6291456 | bytes 3145728 | tf_op jit(solution)/shard_map/cond/branch_0_fun/concatenate | solution.py:26
  66.4 5.2 %multiply_reduce_fusion = (f32[12]{0:T(128)S(1)}, f32[12,64,256]{2,1,0:T(8,128)}) fusion(f32[24,256,256]{2,1,0:T(8,128)} %param.24, bf16[12,256,256]{2,1,0:T(8,128)(2,1)} %get-tuple-element.138, f32[24,64,256]{2,1,0:T(8,128)} %param.23), kind=kOutput, calls=%fused_computation.37 | convolution fusion | flops 604372992 | bytes 6291504 | tf_op jit(solution)/shard_map/kij,kjl->kil/dot_general | solution.py:93
  71.8 2.4 %collective-permute-done.6 = f32[2,24]{1,0:T(2,128)S(1)} collective-permute-done((f32[2,24]{1,0:T(2,128)S(1)}, f32[2,24]{1,0:T(2,128)S(1)}, u32[]{:S(2)}, u32[]{:S(2)}) %collective-permute-start.6) | collective-permute-done | bytes 224 | tf_op jit(solution)/shard_map/ppermute | solution.py:104
  74.4 3.8 %collective-permute-done.7 = f32[2,24]{1,0:T(2,128)S(1)} collective-permute-done((f32[2,24]{1,0:T(2,128)S(1)}, f32[2,24]{1,0:T(2,128)S(1)}, u32[]{:S(2)}, u32[]{:S(2)}) %collective-permute-start.7) | collective-permute-done | bytes 224 | tf_op jit(solution)/shard_map/ppermute | solution.py:104
  78.2 4.6 %fusion.32 = (bf16[24,64,256]{2,1,0:T(8,128)(2,1)S(1)}, f32[24,64,256]{2,1,0:T(8,128)}, f32[24,64,256]{2,1,0:T(8,128)}) fusion(f32[24,64,256]{2,1,0:T(8,128)} %param.27, f32[12,64,256]{2,1,0:T(8,128)} %get-tuple-element.130, f32[12,64,256]{2,1,0:T(8,128)S(1)} %get-tuple-element.132, f32[24]{0:T(128)S(1)} %multiply_bitcast_fusion, f32[24,64,256]{2,1,0:T(8,128)} %param.26), kind=kLoop, calls=%fused_computation.73 | loop fusion | flops 2752512 | bytes 8650848 | tf_op jit(solution)/shard_map/convert_element_type | solution.py:113
  82.8 1.6 %gather_fusion.3 = bf16[32,64,256]{2,1,0:T(8,128)(2,1)} fusion(bf16[24,64,256]{2,1,0:T(8,128)(2,1)S(1)} %get-tuple-element.120, s32[1024]{0:T(1024)S(1)} %pad_clamp_fusion.1), kind=kCustom, calls=%fused_computation.3 | custom fusion | bytes 2097280 | tf_op jit(solution)/shard_map/gather | solution.py:114
  84.4 8.2 %all-to-all-start.1 = ((bf16[32,64,256]{2,1,0:T(8,128)(2,1)}), bf16[32,64,256]{2,1,0:T(8,128)(2,1)}, u32[]{:S(2)}, u32[]{:S(2)}) async-start(bf16[32,64,256]{2,1,0:T(8,128)(2,1)} %gather_fusion.3), calls=%async_computation.1 | async-start | bytes 2097152 | tf_op jit(solution)/shard_map/all_to_all | solution.py:115
  92.7 4.2 %multiply_add_fusion.1 = f32[24,64,256]{2,1,0:T(8,128)} fusion(f32[24,64,256]{2,1,0:T(8,128)} %param.21, bf16[12,256,256]{2,1,0:T(8,128)(2,1)} %get-tuple-element.138, bf16[12,256,256]{2,1,0:T(8,128)(2,1)S(1)} %copy-done.1, bf16[12,64,256]{2,1,0:T(8,128)(2,1)S(1)} %broadcast_select_fusion.1, bf16[12,64,256]{2,1,0:T(8,128)(2,1)S(1)} %broadcast_select_fusion.2), kind=kOutput, calls=%fused_computation.31 | convolution fusion | flops 204472320 | bytes 7077888 | tf_op jit(solution)/shard_map/kij,klj->kil/dot_general | solution.py:76
  97.0 2.5 %multiply_add_fusion = f32[24,64,256]{2,1,0:T(8,128)} fusion(f32[24,64,256]{2,1,0:T(8,128)S(1)} %copy-done.5, bf16[12,256,256]{2,1,0:T(8,128)(2,1)S(1)} %copy-done.2, bf16[12,256,256]{2,1,0:T(8,128)(2,1)S(1)} %copy-done.1, s32[]{:T(128)S(6)} %select_n.59), kind=kOutput, calls=%fused_computation.30 | convolution fusion | flops 205651968 | bytes 9437188 | tf_op jit(solution)/shard_map/kji,kjl->kil/dot_general | solution.py:79
  99.5 10.2 %all-to-all-done.1 = bf16[32,64,256]{2,1,0:T(8,128)(2,1)} async-done(((bf16[32,64,256]{2,1,0:T(8,128)(2,1)}), bf16[32,64,256]{2,1,0:T(8,128)(2,1)}, u32[]{:S(2)}, u32[]{:S(2)}) %all-to-all-start.1) | async-done | bytes 1048608 | tf_op jit(solution)/shard_map/all_to_all | solution.py:115
  109.7 2.6 %gather_fusion.4 = bf16[12,64,256]{2,1,0:T(8,128)(2,1)} fusion(bf16[32,64,256]{2,1,0:T(8,128)(2,1)} %all-to-all-done.1, s32[1024]{0:T(1024)S(1)} %pad_clamp_fusion), kind=kCustom, calls=%fused_computation.4 | custom fusion | bytes 786480 | tf_op jit(solution)/shard_map/gather | solution.py:116
  (42 shorter events, 4.0 us)
Async XLA Ops:
  0.6 3.8 %copy-start = (bf16[12,64,256]{2,1,0:T(8,128)(2,1)S(1)}, bf16[12,64,256]{2,1,0:T(8,128)(2,1)}, u32[]{:S(2)}) copy-start(bf16[12,64,256]{2,1,0:T(8,128)(2,1)} %param.18) | copy-start | bytes 1179652
  6.1 25.5 %all-to-all-start = ((bf16[32,64,256]{2,1,0:T(8,128)(2,1)}), bf16[32,64,256]{2,1,0:T(8,128)(2,1)S(1)}, u32[]{:S(2)}, u32[]{:S(2)}) async-start(bf16[32,64,256]{2,1,0:T(8,128)(2,1)} %broadcast_select_fusion), calls=%async_computation | async-start | bytes 2097152 | tf_op jit(solution)/shard_map/all_to_all | solution.py:64
  32.3 13.2 %collective-permute-start.1 = (bf16[12,64,256]{2,1,0:T(8,128)(2,1)S(1)}, bf16[12,64,256]{2,1,0:T(8,128)(2,1)S(1)}, u32[]{:S(2)}, u32[]{:S(2)}) collective-permute-start(bf16[12,64,256]{2,1,0:T(8,128)(2,1)S(1)} %broadcast_select_fusion.2), channel_id=1, source_target_pairs={{0,1},{1,2},{2,3},{3,0},{4,5},{5,6},{6,7},{7,4},{8,9},{9,10},{10,1... | collective-permute-start | bytes 1179656 | tf_op jit(solution)/shard_map/ppermute | solution.py:17
  34.7 11.5 %collective-permute-start.3 = (bf16[12,64,256]{2,1,0:T(8,128)(2,1)S(1)}, bf16[12,64,256]{2,1,0:T(8,128)(2,1)S(1)}, u32[]{:S(2)}, u32[]{:S(2)}) collective-permute-start(bf16[12,64,256]{2,1,0:T(8,128)(2,1)S(1)} %broadcast_select_fusion.1), channel_id=1, source_target_pairs={{0,3},{1,0},{2,1},{3,2},{4,7},{5,4},{6,5},{7,6},{8,11},{9,8},{10,9... | collective-permute-start | bytes 1179656 | tf_op jit(solution)/shard_map/ppermute | solution.py:18
  36.9 16.9 %collective-permute-start = (bf16[12,64,256]{2,1,0:T(8,128)(2,1)S(1)}, bf16[12,64,256]{2,1,0:T(8,128)(2,1)S(1)}, u32[]{:S(2)}, u32[]{:S(2)}) collective-permute-start(bf16[12,64,256]{2,1,0:T(8,128)(2,1)S(1)} %broadcast_select_fusion.2), channel_id=1, source_target_pairs={{0,3},{1,0},{2,1},{3,2},{4,7},{5,4},{6,5},{7,6},{8,11},{9,8},{10,9... | collective-permute-start | bytes 1179656 | tf_op jit(solution)/shard_map/ppermute | solution.py:18
  45.5 11.2 %collective-permute-start.2 = (bf16[12,64,256]{2,1,0:T(8,128)(2,1)S(1)}, bf16[12,64,256]{2,1,0:T(8,128)(2,1)S(1)}, u32[]{:S(2)}, u32[]{:S(2)}) collective-permute-start(bf16[12,64,256]{2,1,0:T(8,128)(2,1)S(1)} %collective-permute-done.1), channel_id=1, source_target_pairs={{0,1},{1,2},{2,3},{3,0},{4,5},{5,6},{6,7},{7,4},{8,9},{9,10},{10,1... | collective-permute-start | bytes 1179656 | tf_op jit(solution)/shard_map/ppermute | solution.py:20
  45.5 19.6 %collective-permute-start.5 = (bf16[12,64,256]{2,1,0:T(8,128)(2,1)S(1)}, bf16[12,64,256]{2,1,0:T(8,128)(2,1)S(1)}, u32[]{:S(2)}, u32[]{:S(2)}) collective-permute-start(bf16[12,64,256]{2,1,0:T(8,128)(2,1)S(1)} %broadcast_select_fusion.1), channel_id=1, source_target_pairs={{0,1},{1,2},{2,3},{3,0},{4,5},{5,6},{6,7},{7,4},{8,9},{9,10},{10,1... | collective-permute-start | bytes 1179656 | tf_op jit(solution)/shard_map/ppermute | solution.py:17
  46.2 18.9 %collective-permute-start.4 = (bf16[12,64,256]{2,1,0:T(8,128)(2,1)S(1)}, bf16[12,64,256]{2,1,0:T(8,128)(2,1)S(1)}, u32[]{:S(2)}, u32[]{:S(2)}) collective-permute-start(bf16[12,64,256]{2,1,0:T(8,128)(2,1)S(1)} %collective-permute-done.3), channel_id=1, source_target_pairs={{0,3},{1,0},{2,1},{3,2},{4,7},{5,4},{6,5},{7,6},{8,11},{9,8},{10,9... | collective-permute-start | bytes 1179656 | tf_op jit(solution)/shard_map/ppermute | solution.py:22
  66.4 5.3 %copy-start.3 = (f32[24]{0:T(128)S(1)}, f32[24]{0:T(128)}, u32[]{:S(2)}) copy-start(f32[24]{0:T(128)} %get-tuple-element.123) | copy-start | bytes 292
  66.4 8.0 %copy-start.4 = (s32[32]{0:T(128)S(1)}, s32[32]{0:T(128)}, u32[]{:S(2)}) copy-start(s32[32]{0:T(128)} %get-tuple-element.133) | copy-start | bytes 388
  71.7 2.5 %collective-permute-start.6 = (f32[2,24]{1,0:T(2,128)S(1)}, f32[2,24]{1,0:T(2,128)S(1)}, u32[]{:S(2)}, u32[]{:S(2)}) collective-permute-start(f32[2,24]{1,0:T(2,128)S(1)} %pad_maximum_fusion.17), channel_id=1, source_target_pairs={{0,1},{1,0},{2,3},{3,2},{4,5},{5,4},{6,7},{7,6},{8,9},{9,8},{10,11... | collective-permute-start | bytes 584 | tf_op jit(solution)/shard_map/ppermute | solution.py:104
  74.2 4.0 %collective-permute-start.7 = (f32[2,24]{1,0:T(2,128)S(1)}, f32[2,24]{1,0:T(2,128)S(1)}, u32[]{:S(2)}, u32[]{:S(2)}) collective-permute-start(f32[2,24]{1,0:T(2,128)S(1)} %fusion.31), channel_id=1, source_target_pairs={{0,2},{1,3},{2,0},{3,1},{4,6},{5,7},{6,4},{7,5},{8,10},{9,11},{10,... | collective-permute-start | bytes 584 | tf_op jit(solution)/shard_map/ppermute | solution.py:104
  84.4 8.3 %copy-start.1 = (bf16[12,256,256]{2,1,0:T(8,128)(2,1)S(1)}, bf16[12,256,256]{2,1,0:T(8,128)(2,1)}, u32[]{:S(2)}) copy-start(bf16[12,256,256]{2,1,0:T(8,128)(2,1)} %get-tuple-element.137) | copy-start | bytes 4718596
  84.4 25.3 %all-to-all-start.1 = ((bf16[32,64,256]{2,1,0:T(8,128)(2,1)}), bf16[32,64,256]{2,1,0:T(8,128)(2,1)}, u32[]{:S(2)}, u32[]{:S(2)}) async-start(bf16[32,64,256]{2,1,0:T(8,128)(2,1)} %gather_fusion.3), calls=%async_computation.1 | async-start | bytes 2097152 | tf_op jit(solution)/shard_map/all_to_all | solution.py:115
  92.7 4.3 %copy-start.2 = (bf16[12,256,256]{2,1,0:T(8,128)(2,1)S(1)}, bf16[12,256,256]{2,1,0:T(8,128)(2,1)}, u32[]{:S(2)}) copy-start(bf16[12,256,256]{2,1,0:T(8,128)(2,1)} %get-tuple-element.138) | copy-start | bytes 4718596
  92.7 4.3 %copy-start.5 = (f32[24,64,256]{2,1,0:T(8,128)S(1)}, f32[24,64,256]{2,1,0:T(8,128)}, u32[]{:S(2)}) copy-start(f32[24,64,256]{2,1,0:T(8,128)} %param.22) | copy-start | bytes 4718596

commit v2 on v0

--- a/solution.py
+++ b/solution.py
@@ -11,15 +11,19 @@
 eps_mean = 1e-06
 
 
-def gather_rows(piece, far_right, splits, tensor_index):
+def gather_rows(piece, splits, tensor_index):
     right = [(i, (i + 1) % splits) for i in range(splits)]
     left = [(i, (i - 1) % splits) for i in range(splits)]
     from_left = lax.ppermute(piece, "tensor", right)
     from_right = lax.ppermute(piece, "tensor", left)
-    if far_right:
-        far = lax.ppermute(from_left, "tensor", right)
-    else:
-        far = lax.ppermute(from_right, "tensor", left)
+    cut = piece.shape[0] // 2
+    far = jnp.concatenate(
+        [
+            lax.ppermute(from_left[:cut], "tensor", right),
+            lax.ppermute(from_right[cut:], "tensor", left),
+        ],
+        0,
+    )
     by_shift = (piece, from_right, far, from_left)
 
     def ordered(first):
@@ -56,20 +60,19 @@
     src_of_slot = jnp.argmax(slot_match, axis=1).astype(jnp.int32)
     slot_filled = jnp.any(slot_match, axis=1)
     slot_of_src = jnp.argmax(slot_match, axis=0).astype(jnp.int32)
-    src_sent = jnp.any(slot_match, axis=0)
     dest_match = local_owner[None, :] == group_ids[:, None]
     block_of_dest = jnp.argmax(dest_match, axis=1).astype(jnp.int32)
     dest_used = jnp.any(dest_match, axis=1)
     row_start = tensor_index * rows_dev
     outgoing = pick(grads, block_of_dest, dest_used)
     arrived = lax.all_to_all(outgoing, "shard", split_axis=0, concat_axis=0, tiled=True)
-    half = slots_dev // 2
+    half = (2 * slots_dev) // 3
     first_half = pick(arrived, src_of_slot[:half], slot_filled[:half])
     second_half = pick(arrived, src_of_slot[half:], slot_filled[half:])
     grad_piece = jnp.concatenate([first_half, second_half], 0)
     whole_halves = [
-        gather_rows(first_half, True, splits, tensor_index),
-        gather_rows(second_half, False, splits, tensor_index),
+        gather_rows(first_half, splits, tensor_index),
+        gather_rows(second_half, splits, tensor_index),
     ]
     grad_whole = jnp.concatenate(whole_halves, 0)
     f32 = jnp.float32
@@ -87,12 +90,13 @@
     precond_parts = []
     for part, whole in enumerate(whole_halves):
         lo = part * half
+        hi = lo + whole.shape[0]
         mixed = jnp.einsum(
-            "kij,kjl->kil", root_left[lo : lo + half], whole.astype(f32),
+            "kij,kjl->kil", root_left[lo:hi], whole.astype(f32),
             precision=three_pass, preferred_element_type=f32,
         )
         precond_parts.append(jnp.einsum(
-            "kij,kjl->kil", mixed, root_right[lo : lo + half], precision=three_pass,
+            "kij,kjl->kil", mixed, root_right[lo:hi], precision=three_pass,
             preferred_element_type=f32,
         ))
     precond = jnp.concatenate(precond_parts, 0)
@@ -112,9 +116,9 @@
     velocity_new = beta_mom * momentum + (1.0 - beta_mom) * scale_ratio[:, None, None] * precond
     weight_new = master - learn_rate * velocity_new
     weight_half = weight_new.astype(jnp.bfloat16)
-    returning = pick(weight_half, slot_of_src, src_sent)
+    returning = jnp.take(weight_half, slot_of_src, axis=0, mode="clip")
     back_rows = lax.all_to_all(returning, "shard", split_axis=0, concat_axis=0, tiled=True)
-    weights_local = jnp.take(back_rows, local_owner, axis=0)
+    weights_local = jnp.take(back_rows, local_owner, axis=0, mode="clip")
     return (left_new, right_new, second_new, velocity_new, weight_new, weights_local)
 
 

time: 113 us -> 115 us (1.018)
  starting transfers between devices: 25.7 us -> 32.7 us
  other arithmetic: 19.1 us -> 12.5 us
  local copies, waits for them, and re-layouts: 6.75 us -> 9.96 us
    ppermute x2 -> x4, waiting for transfers between devices: 2.88 us -> 10.2 us  [the longest x2 10.2 us: gather_rows(): lax.ppermute(from_left[:cut], 'tensor', right)]
    ppermute x2, waiting for transfers between devices: 9.43 us -> 4.24 us  [gather_rows(): from_left = lax.ppermute(piece, 'tensor', right)]
    ppermute x2, starting transfers between devices: 0.27 us -> 4.56 us  [on_device(): lax.ppermute(sums, 'tensor', [(i, i ^ step) for i in range(splits)])]
    gather x1 -> x2, local copies, waits for them, and re-layouts: 1.79 us -> 5.43 us  [the longest x1 2.87 us: on_device(): returning = jnp.take(weight_half, slot_of_src, axis=0, mode='clip')]
    ppermute x2 -> x4, starting transfers between devices: 2.46 us -> 5.76 us  [the longest x2 4.8 us: gather_rows(): lax.ppermute(from_right[cut:], 'tensor', left)]
    ppermute x2, waiting for transfers between devices: 5.09 us -> 2.15 us  [on_device(): lax.ppermute(sums, 'tensor', [(i, i ^ step) for i in range(splits)])]
    select_n x4 -> x3, other arithmetic: 3.7 us -> 1.31 us  [pick(): return jnp.where(valid[:, None, None], taken, jnp.zeros((), source.dtype))]
    reduce_sum x1, other arithmetic: 3.93 us -> 2.02 us  [on_device(): sums = jnp.stack([jnp.sum(adam_step * adam_step, axis=(1, 2)), precond_sq])]
  transfers between devices with their start and end apart: 10 -> 12, of which waited for: 8 -> 7; matrix products, arithmetic and copies ran while one was open for 18% -> 13% of each run, Pallas kernels for 0% -> 0%
where the time goes in v2:
time: 115 us
  waiting for transfers between devices  43.1 us (37%)
  starting transfers between devices  32.7 us (28%)
  matrix products  15.5 us (13%)
  other arithmetic  12.5 us (11%)
  local copies, waits for them, and re-layouts  9.96 us (9%)
    all_to_all x1, waiting for transfers between devices, on_device(): lax.all_to_all(outgoing, 'shard', split_axis=0, concat_axis=0, tiled=True)  16.1 us
    all_to_all x1, waiting for transfers between devices, on_device(): lax.all_to_all(returning, 'shard', split_axis=0, concat_axis=0, tiled=True)  10.4 us
    ppermute x2, waiting for transfers between devices, gather_rows(): lax.ppermute(from_left[:cut], 'tensor', right)  10.2 us
    dot_general x2, matrix products, on_device(): jnp.einsum('kij,kjl->kil', mixed, root_right[lo:hi], precision=three_pass...  8.81 us
    all_to_all x1, starting transfers between devices, on_device(): lax.all_to_all(outgoing, 'shard', split_axis=0, concat_axis=0, tiled=True)  8.58 us
    all_to_all x1, starting transfers between devices, on_device(): lax.all_to_all(returning, 'shard', split_axis=0, concat_axis=0, tiled=True)  8.37 us
    ppermute x2, starting transfers between devices, gather_rows(): lax.ppermute(from_right[cut:], 'tensor', left)  4.8 us
    ppermute x2, starting transfers between devices, on_device(): lax.ppermute(sums, 'tensor', [(i, i ^ step) for i in range(splits)])  4.56 us
  transfers between devices with their start and end apart: 12, of which 7 were waited for; matrix products, arithmetic and copies ran while one was open for 13% of the time, Pallas kernels for 0%

profile of v2, /device:TPU:1, one launch (start us, length us, event | category | flops | bytes accessed | tf_op | source)
XLA Modules:
  0.0 114.6 jit_solution(16001413530367815452)
XLA Ops:
  0.7 0.8 reshape.53
  2.2 0.8 eq.46
  4.5 1.1 broadcast_select_fusion
  5.6 8.6 %all-to-all-start = ((bf16[32,64,256]{2,1,0:T(8,128)(2,1)}), bf16[32,64,256]{2,1,0:T(8,128)(2,1)S(1)}, u32[]{:S(2)}, u32[]{:S(2)}) async-start(bf16[32,64,256]{2,1,0:T(8,128)(2,1)} %broadcast_select_fusion), calls=%async_computation | async-start | bytes 2097152 | tf_op jit(solution)/shard_map/all_to_all | solution.py:68
  15.0 16.1 %all-to-all-done = bf16[32,64,256]{2,1,0:T(8,128)(2,1)S(1)} async-done(((bf16[32,64,256]{2,1,0:T(8,128)(2,1)}), bf16[32,64,256]{2,1,0:T(8,128)(2,1)S(1)}, u32[]{:S(2)}, u32[]{:S(2)}) %all-to-all-start) | async-done | bytes 1048608 | tf_op jit(solution)/shard_map/all_to_all | solution.py:68
  31.8 1.7 %collective-permute-start.5 = (bf16[8,64,256]{2,1,0:T(8,128)(2,1)S(1)}, bf16[8,64,256]{2,1,0:T(8,128)(2,1)S(1)}, u32[]{:S(2)}, u32[]{:S(2)}) collective-permute-start(bf16[8,64,256]{2,1,0:T(8,128)(2,1)S(1)} %broadcast_select_fusion.2), channel_id=1, source_target_pairs={{0,1},{1,2},{2,3},{3,0},{4,5},{5,6},{6,7},{7,4},{8,9},{9,10},{10,1... | collective-permute-start | bytes 786440 | tf_op jit(solution)/shard_map/ppermute | solution.py:17
  33.5 2.2 %collective-permute-start.4 = (bf16[8,64,256]{2,1,0:T(8,128)(2,1)S(1)}, bf16[8,64,256]{2,1,0:T(8,128)(2,1)S(1)}, u32[]{:S(2)}, u32[]{:S(2)}) collective-permute-start(bf16[8,64,256]{2,1,0:T(8,128)(2,1)S(1)} %broadcast_select_fusion.2), channel_id=1, source_target_pairs={{0,3},{1,0},{2,1},{3,2},{4,7},{5,4},{6,5},{7,6},{8,11},{9,8},{10,9... | collective-permute-start | bytes 786440 | tf_op jit(solution)/shard_map/ppermute | solution.py:18
  36.4 1.5 %collective-permute-start = (bf16[16,64,256]{2,1,0:T(8,128)(2,1)S(1)}, bf16[16,64,256]{2,1,0:T(8,128)(2,1)S(1)}, u32[]{:S(2)}, u32[]{:S(2)}) collective-permute-start(bf16[16,64,256]{2,1,0:T(8,128)(2,1)S(1)} %broadcast_select_fusion.1), channel_id=1, source_target_pairs={{0,3},{1,0},{2,1},{3,2},{4,7},{5,4},{6,5},{7,6},{8,11},{9,8},{10,9... | collective-permute-start | bytes 1572872 | tf_op jit(solution)/shard_map/ppermute | solution.py:18
  37.9 4.2 %collective-permute-done.5 = bf16[8,64,256]{2,1,0:T(8,128)(2,1)S(1)} collective-permute-done((bf16[8,64,256]{2,1,0:T(8,128)(2,1)S(1)}, bf16[8,64,256]{2,1,0:T(8,128)(2,1)S(1)}, u32[]{:S(2)}, u32[]{:S(2)}) %collective-permute-start.5) | collective-permute-done | bytes 262176 | tf_op jit(solution)/shard_map/ppermute | solution.py:17
  42.3 2.7 %collective-permute-start.7 = (bf16[4,64,256]{2,1,0:T(8,128)(2,1)S(1)}, bf16[4,64,256]{2,1,0:T(8,128)(2,1)S(1)}, u32[]{:S(2)}, u32[]{:S(2)}) collective-permute-start(bf16[4,64,256]{2,1,0:T(8,128)(2,1)S(1)} %slice.69), channel_id=1, source_target_pairs={{0,3},{1,0},{2,1},{3,2},{4,7},{5,4},{6,5},{7,6},{8,11},{9,8},{10,9... | collective-permute-start | bytes 393224 | tf_op jit(solution)/shard_map/ppermute | solution.py:23
  45.0 2.0 %fusion.11 = (f32[24]{0:T(128)S(1)}, f32[24,64,256]{2,1,0:T(8,128)}) fusion(bf16[8,64,256]{2,1,0:T(8,128)(2,1)S(1)} %broadcast_select_fusion.2, bf16[16,64,256]{2,1,0:T(8,128)(2,1)S(1)} %broadcast_select_fusion.1, f32[24,64,256]{2,1,0:T(8,128)S(1)} %copy-done.3), kind=kLoop, calls=%fused_computation.32 | loop fusion | flops 3932136 | bytes 3932256 | tf_op jit(solution)/shard_map/reduce_sum | solution.py:105
  47.0 8.8 %collective-permute-done.6 = bf16[4,64,256]{2,1,0:T(8,128)(2,1)S(1)} collective-permute-done((bf16[4,64,256]{2,1,0:T(8,128)(2,1)S(1)}, bf16[4,64,256]{2,1,0:T(8,128)(2,1)S(1)}, u32[]{:S(2)}, u32[]{:S(2)}) %collective-permute-start.6) | collective-permute-done | bytes 131104 | tf_op jit(solution)/shard_map/ppermute | solution.py:22
  55.8 1.1 conditional.3
  55.9 1.0 pad_maximum_fusion.4
  56.9 0.9 collective-permute-start.2
  58.5 2.1 %collective-permute-start.3 = (bf16[8,64,256]{2,1,0:T(8,128)(2,1)}, bf16[8,64,256]{2,1,0:T(8,128)(2,1)S(1)}, u32[]{:S(2)}, u32[]{:S(2)}) collective-permute-start(bf16[8,64,256]{2,1,0:T(8,128)(2,1)} %slice.67), channel_id=1, source_target_pairs={{0,3},{1,0},{2,1},{3,2},{4,7},{5,4},{6,5},{7,6},{8,11},{9,8},{10,9... | collective-permute-start | bytes 786440 | tf_op jit(solution)/shard_map/ppermute | solution.py:23
  60.6 3.3 %multiply_reduce_fusion.1 = (f32[8]{0:T(128)S(1)}, f32[8,64,256]{2,1,0:T(8,128)S(1)}) fusion(f32[24,256,256]{2,1,0:T(8,128)} %param.24, bf16[8,256,256]{2,1,0:T(8,128)(2,1)} %get-tuple-element.134, f32[24,64,256]{2,1,0:T(8,128)} %param.23), kind=kOutput, calls=%fused_computation.39 | convolution fusion | flops 402915328 | bytes 4194336 | tf_op jit(solution)/shard_map/kij,kjl->kil/dot_general | solution.py:98
  64.0 1.4 %collective-permute-done.2 = bf16[8,64,256]{2,1,0:T(8,128)(2,1)S(1)} collective-permute-done((bf16[8,64,256]{2,1,0:T(8,128)(2,1)S(1)}, bf16[8,64,256]{2,1,0:T(8,128)(2,1)S(1)}, u32[]{:S(2)}, u32[]{:S(2)}) %collective-permute-start.2) | collective-permute-done | bytes 262176 | tf_op jit(solution)/shard_map/ppermute | solution.py:22
  65.5 1.5 %conditional.2 = (bf16[16,256,256]{2,1,0:T(8,128)(2,1)}) conditional(s32[]{:T(128)} %clamp.4, (bf16[16,64,256]{2,1,0:T(8,128)(2,1)S(1)}, bf16[16,64,256]{2,1,0:T(8,128)(2,1)S(1)}, bf16[16,64,256]{2,1,0:T(8,128)(2,1)S(1)}, bf16[16,64,256]{2,1,0:T(8,128)(2,1)S(1)}) %tuple.38, (bf16[16,64,256]{2,1,0:T(8,128)(2,1)S(1)}, ...), branch_computations={%region_5.6_spmd, %region_6.7_spmd, %region_7.8_spmd, %region_8.9_... | conditional | flops 8388608 | bytes 4194312 | solution.py:32
  65.5 1.5 %pad_maximum_fusion = bf16[16,256,256]{2,1,0:T(8,128)(2,1)} fusion(bf16[16,64,256]{2,1,0:T(8,128)(2,1)S(1)} %get-tuple-element.72, bf16[16,64,256]{2,1,0:T(8,128)(2,1)S(1)} %get-tuple-element.71, bf16[16,64,256]{2,1,0:T(8,128)(2,1)S(1)} %get-tuple-element.70, bf16[16,64,256]{2,1,0:T(8,128)(2,1)S(1)} %get-tuple-element.64), kind=kLoop, calls=%fused_computation.5 | loop fusion | flops 8388608 | bytes 4194304 | tf_op jit(solution)/shard_map/cond/branch_0_fun/concatenate | solution.py:30
  67.0 5.5 %multiply_reduce_fusion = (f32[16]{0:T(128)S(1)}, f32[16,64,256]{2,1,0:T(8,128)S(1)}) fusion(f32[24,256,256]{2,1,0:T(8,128)} %param.24, bf16[16,256,256]{2,1,0:T(8,128)(2,1)} %get-tuple-element.133, f32[24,64,256]{2,1,0:T(8,128)} %param.23), kind=kOutput, calls=%fused_computation.35 | convolution fusion | flops 805830656 | bytes 8388672 | tf_op jit(solution)/shard_map/kij,kjl->kil/dot_general | solution.py:98
  72.5 1.3 %collective-permute-start.8 = (f32[2,24]{1,0:T(2,128)S(1)}, f32[2,24]{1,0:T(2,128)S(1)}, u32[]{:S(2)}, u32[]{:S(2)}) collective-permute-start(f32[2,24]{1,0:T(2,128)S(1)} %pad_maximum_fusion.17), channel_id=1, source_target_pairs={{0,1},{1,0},{2,3},{3,2},{4,5},{5,4},{6,7},{7,6},{8,9},{9,8},{10,11... | collective-permute-start | bytes 584 | tf_op jit(solution)/shard_map/ppermute | solution.py:109
  73.8 1.2 %collective-permute-done.8 = f32[2,24]{1,0:T(2,128)S(1)} collective-permute-done((f32[2,24]{1,0:T(2,128)S(1)}, f32[2,24]{1,0:T(2,128)S(1)}, u32[]{:S(2)}, u32[]{:S(2)}) %collective-permute-start.8) | collective-permute-done | bytes 224 | tf_op jit(solution)/shard_map/ppermute | solution.py:109
  75.0 3.3 %collective-permute-start.9 = (f32[2,24]{1,0:T(2,128)S(1)}, f32[2,24]{1,0:T(2,128)S(1)}, u32[]{:S(2)}, u32[]{:S(2)}) collective-permute-start(f32[2,24]{1,0:T(2,128)S(1)} %fusion.30), channel_id=1, source_target_pairs={{0,2},{1,3},{2,0},{3,1},{4,6},{5,7},{6,4},{7,5},{8,10},{9,11},{10,... | collective-permute-start | bytes 584 | tf_op jit(solution)/shard_map/ppermute | solution.py:109
  78.3 1.0 collective-permute-done.9
  79.3 4.5 %fusion.31 = (bf16[24,64,256]{2,1,0:T(8,128)(2,1)}, f32[24,64,256]{2,1,0:T(8,128)}, f32[24,64,256]{2,1,0:T(8,128)}) fusion(f32[24,64,256]{2,1,0:T(8,128)} %param.27, f32[8,64,256]{2,1,0:T(8,128)S(1)} %get-tuple-element.126, f32[16,64,256]{2,1,0:T(8,128)S(1)} %get-tuple-element.128, f32[24]{0:T(128)S(1)} %multiply_bitcast_fusion, f32[24,64,256]{2,1,0:T(8,128)} %param.26), kind=kLoop, calls=%fused_computation.71 | loop fusion | flops 2752512 | bytes 8650848 | tf_op jit(solution)/shard_map/convert_element_type | solution.py:118
  83.8 2.9 %gather_fusion.3 = bf16[32,64,256]{2,1,0:T(8,128)(2,1)} fusion(bf16[24,64,256]{2,1,0:T(8,128)(2,1)} %get-tuple-element.120, s32[1024]{0:T(1024)S(1)} %get-tuple-element.129), kind=kCustom, calls=%fused_computation.3 | custom fusion | bytes 2097280 | tf_op jit(solution)/shard_map/jit(_take)/gather | solution.py:119
  86.7 8.4 %all-to-all-start.1 = ((bf16[32,64,256]{2,1,0:T(8,128)(2,1)}), bf16[32,64,256]{2,1,0:T(8,128)(2,1)}, u32[]{:S(2)}, u32[]{:S(2)}) async-start(bf16[32,64,256]{2,1,0:T(8,128)(2,1)} %gather_fusion.3), calls=%async_computation.1 | async-start | bytes 2097152 | tf_op jit(solution)/shard_map/all_to_all | solution.py:120
  95.1 4.1 %multiply_add_fusion.1 = f32[24,64,256]{2,1,0:T(8,128)} fusion(f32[24,64,256]{2,1,0:T(8,128)} %param.21, bf16[8,256,256]{2,1,0:T(8,128)(2,1)} %get-tuple-element.134, bf16[16,256,256]{2,1,0:T(8,128)(2,1)S(1)} %copy-done.1, bf16[8,64,256]{2,1,0:T(8,128)(2,1)S(1)} %broadcast_select_fusion.2, bf16[16,64,256]{2,1,0:T(8,128)(2,1)S(1)} %broadcast_select_fusion.1), kind=kOutput, calls=%fused_computation.31 | convolution fusion | flops 204472320 | bytes 7077888 | tf_op jit(solution)/shard_map/kij,klj->kil/dot_general | solution.py:80
  99.2 2.6 %multiply_add_fusion = f32[24,64,256]{2,1,0:T(8,128)} fusion(f32[24,64,256]{2,1,0:T(8,128)S(1)} %copy-done.4, bf16[8,256,256]{2,1,0:T(8,128)(2,1)S(1)} %copy-done.2, bf16[16,256,256]{2,1,0:T(8,128)(2,1)S(1)} %copy-done.1, s32[]{:T(128)S(6)} %select_n.35), kind=kOutput, calls=%fused_computation.30 | convolution fusion | flops 205651968 | bytes 9437188 | tf_op jit(solution)/shard_map/kji,kjl->kil/dot_general | solution.py:83
  101.7 10.4 %all-to-all-done.1 = bf16[32,64,256]{2,1,0:T(8,128)(2,1)} async-done(((bf16[32,64,256]{2,1,0:T(8,128)(2,1)}), bf16[32,64,256]{2,1,0:T(8,128)(2,1)}, u32[]{:S(2)}, u32[]{:S(2)}) %all-to-all-start.1) | async-done | bytes 1048608 | tf_op jit(solution)/shard_map/all_to_all | solution.py:120
  112.1 2.6 %gather_fusion.4 = bf16[12,64,256]{2,1,0:T(8,128)(2,1)} fusion(bf16[32,64,256]{2,1,0:T(8,128)(2,1)} %all-to-all-done.1, s32[1024]{0:T(1024)S(1)} %pad_clamp_fusion), kind=kCustom, calls=%fused_computation.4 | custom fusion | bytes 786480 | tf_op jit(solution)/shard_map/jit(_take)/gather | solution.py:121
  (49 shorter events, 5.5 us)
Async XLA Ops:
  0.6 3.2 %copy-start = (bf16[12,64,256]{2,1,0:T(8,128)(2,1)S(1)}, bf16[12,64,256]{2,1,0:T(8,128)(2,1)}, u32[]{:S(2)}) copy-start(bf16[12,64,256]{2,1,0:T(8,128)(2,1)} %param.18) | copy-start | bytes 1179652
  5.6 25.5 %all-to-all-start = ((bf16[32,64,256]{2,1,0:T(8,128)(2,1)}), bf16[32,64,256]{2,1,0:T(8,128)(2,1)S(1)}, u32[]{:S(2)}, u32[]{:S(2)}) async-start(bf16[32,64,256]{2,1,0:T(8,128)(2,1)} %broadcast_select_fusion), calls=%async_computation | async-start | bytes 2097152 | tf_op jit(solution)/shard_map/all_to_all | solution.py:68
  31.8 10.4 %collective-permute-start.5 = (bf16[8,64,256]{2,1,0:T(8,128)(2,1)S(1)}, bf16[8,64,256]{2,1,0:T(8,128)(2,1)S(1)}, u32[]{:S(2)}, u32[]{:S(2)}) collective-permute-start(bf16[8,64,256]{2,1,0:T(8,128)(2,1)S(1)} %broadcast_select_fusion.2), channel_id=1, source_target_pairs={{0,1},{1,2},{2,3},{3,0},{4,5},{5,6},{6,7},{7,4},{8,9},{9,10},{10,1... | collective-permute-start | bytes 786440 | tf_op jit(solution)/shard_map/ppermute | solution.py:17
  33.5 8.8 %collective-permute-start.4 = (bf16[8,64,256]{2,1,0:T(8,128)(2,1)S(1)}, bf16[8,64,256]{2,1,0:T(8,128)(2,1)S(1)}, u32[]{:S(2)}, u32[]{:S(2)}) collective-permute-start(bf16[8,64,256]{2,1,0:T(8,128)(2,1)S(1)} %broadcast_select_fusion.2), channel_id=1, source_target_pairs={{0,3},{1,0},{2,1},{3,2},{4,7},{5,4},{6,5},{7,6},{8,11},{9,8},{10,9... | collective-permute-start | bytes 786440 | tf_op jit(solution)/shard_map/ppermute | solution.py:18
  36.3 8.7 %copy-start.3 = (f32[24,64,256]{2,1,0:T(8,128)S(1)}, f32[24,64,256]{2,1,0:T(8,128)}, u32[]{:S(2)}) copy-start(f32[24,64,256]{2,1,0:T(8,128)} %param.25) | copy-start | bytes 4718596
  36.4 21.4 %collective-permute-start = (bf16[16,64,256]{2,1,0:T(8,128)(2,1)S(1)}, bf16[16,64,256]{2,1,0:T(8,128)(2,1)S(1)}, u32[]{:S(2)}, u32[]{:S(2)}) collective-permute-start(bf16[16,64,256]{2,1,0:T(8,128)(2,1)S(1)} %broadcast_select_fusion.1), channel_id=1, source_target_pairs={{0,3},{1,0},{2,1},{3,2},{4,7},{5,4},{6,5},{7,6},{8,11},{9,8},{10,9... | collective-permute-start | bytes 1572872 | tf_op jit(solution)/shard_map/ppermute | solution.py:18
  37.8 19.1 %collective-permute-start.1 = (bf16[16,64,256]{2,1,0:T(8,128)(2,1)S(1)}, bf16[16,64,256]{2,1,0:T(8,128)(2,1)S(1)}, u32[]{:S(2)}, u32[]{:S(2)}) collective-permute-start(bf16[16,64,256]{2,1,0:T(8,128)(2,1)S(1)} %broadcast_select_fusion.1), channel_id=1, source_target_pairs={{0,1},{1,2},{2,3},{3,0},{4,5},{5,6},{6,7},{7,4},{8,9},{9,10},{10,1... | collective-permute-start | bytes 1572872 | tf_op jit(solution)/shard_map/ppermute | solution.py:17
  42.2 13.6 %collective-permute-start.6 = (bf16[4,64,256]{2,1,0:T(8,128)(2,1)S(1)}, bf16[4,64,256]{2,1,0:T(8,128)(2,1)S(1)}, u32[]{:S(2)}, u32[]{:S(2)}) collective-permute-start(bf16[4,64,256]{2,1,0:T(8,128)(2,1)S(1)} %slice.68), channel_id=1, source_target_pairs={{0,1},{1,2},{2,3},{3,0},{4,5},{5,6},{6,7},{7,4},{8,9},{9,10},{10,1... | collective-permute-start | bytes 393224 | tf_op jit(solution)/shard_map/ppermute | solution.py:22
  42.3 13.5 %collective-permute-start.7 = (bf16[4,64,256]{2,1,0:T(8,128)(2,1)S(1)}, bf16[4,64,256]{2,1,0:T(8,128)(2,1)S(1)}, u32[]{:S(2)}, u32[]{:S(2)}) collective-permute-start(bf16[4,64,256]{2,1,0:T(8,128)(2,1)S(1)} %slice.69), channel_id=1, source_target_pairs={{0,3},{1,0},{2,1},{3,2},{4,7},{5,4},{6,5},{7,6},{8,11},{9,8},{10,9... | collective-permute-start | bytes 393224 | tf_op jit(solution)/shard_map/ppermute | solution.py:23
  56.9 8.4 %collective-permute-start.2 = (bf16[8,64,256]{2,1,0:T(8,128)(2,1)S(1)}, bf16[8,64,256]{2,1,0:T(8,128)(2,1)S(1)}, u32[]{:S(2)}, u32[]{:S(2)}) collective-permute-start(bf16[8,64,256]{2,1,0:T(8,128)(2,1)S(1)} %slice.66), channel_id=1, source_target_pairs={{0,1},{1,2},{2,3},{3,0},{4,5},{5,6},{6,7},{7,4},{8,9},{9,10},{10,1... | collective-permute-start | bytes 786440 | tf_op jit(solution)/shard_map/ppermute | solution.py:22
  58.5 6.9 %collective-permute-start.3 = (bf16[8,64,256]{2,1,0:T(8,128)(2,1)}, bf16[8,64,256]{2,1,0:T(8,128)(2,1)S(1)}, u32[]{:S(2)}, u32[]{:S(2)}) collective-permute-start(bf16[8,64,256]{2,1,0:T(8,128)(2,1)} %slice.67), channel_id=1, source_target_pairs={{0,3},{1,0},{2,1},{3,2},{4,7},{5,4},{6,5},{7,6},{8,11},{9,8},{10,9... | collective-permute-start | bytes 786440 | tf_op jit(solution)/shard_map/ppermute | solution.py:23
  72.5 2.5 %collective-permute-start.8 = (f32[2,24]{1,0:T(2,128)S(1)}, f32[2,24]{1,0:T(2,128)S(1)}, u32[]{:S(2)}, u32[]{:S(2)}) collective-permute-start(f32[2,24]{1,0:T(2,128)S(1)} %pad_maximum_fusion.17), channel_id=1, source_target_pairs={{0,1},{1,0},{2,3},{3,2},{4,5},{5,4},{6,7},{7,6},{8,9},{9,8},{10,11... | collective-permute-start | bytes 584 | tf_op jit(solution)/shard_map/ppermute | solution.py:109
  75.0 4.2 %collective-permute-start.9 = (f32[2,24]{1,0:T(2,128)S(1)}, f32[2,24]{1,0:T(2,128)S(1)}, u32[]{:S(2)}, u32[]{:S(2)}) collective-permute-start(f32[2,24]{1,0:T(2,128)S(1)} %fusion.30), channel_id=1, source_target_pairs={{0,2},{1,3},{2,0},{3,1},{4,6},{5,7},{6,4},{7,5},{8,10},{9,11},{10,... | collective-permute-start | bytes 584 | tf_op jit(solution)/shard_map/ppermute | solution.py:109
  83.8 11.3 %copy-start.1 = (bf16[16,256,256]{2,1,0:T(8,128)(2,1)S(1)}, bf16[16,256,256]{2,1,0:T(8,128)(2,1)}, u32[]{:S(2)}) copy-start(bf16[16,256,256]{2,1,0:T(8,128)(2,1)} %get-tuple-element.133) | copy-start | bytes 6291460
  86.7 25.4 %all-to-all-start.1 = ((bf16[32,64,256]{2,1,0:T(8,128)(2,1)}), bf16[32,64,256]{2,1,0:T(8,128)(2,1)}, u32[]{:S(2)}, u32[]{:S(2)}) async-start(bf16[32,64,256]{2,1,0:T(8,128)(2,1)} %gather_fusion.3), calls=%async_computation.1 | async-start | bytes 2097152 | tf_op jit(solution)/shard_map/all_to_all | solution.py:120
  95.1 4.1 %copy-start.2 = (bf16[8,256,256]{2,1,0:T(8,128)(2,1)S(1)}, bf16[8,256,256]{2,1,0:T(8,128)(2,1)}, u32[]{:S(2)}) copy-start(bf16[8,256,256]{2,1,0:T(8,128)(2,1)} %get-tuple-element.134) | copy-start | bytes 3145732
  95.1 4.1 %copy-start.4 = (f32[24,64,256]{2,1,0:T(8,128)S(1)}, f32[24,64,256]{2,1,0:T(8,128)}, u32[]{:S(2)}) copy-start(f32[24,64,256]{2,1,0:T(8,128)} %param.22) | copy-start | bytes 4718596

commit v3 on v0

--- a/solution.py
+++ b/solution.py
@@ -56,7 +56,6 @@
     src_of_slot = jnp.argmax(slot_match, axis=1).astype(jnp.int32)
     slot_filled = jnp.any(slot_match, axis=1)
     slot_of_src = jnp.argmax(slot_match, axis=0).astype(jnp.int32)
-    src_sent = jnp.any(slot_match, axis=0)
     dest_match = local_owner[None, :] == group_ids[:, None]
     block_of_dest = jnp.argmax(dest_match, axis=1).astype(jnp.int32)
     dest_used = jnp.any(dest_match, axis=1)
@@ -87,9 +86,14 @@
     precond_parts = []
     for part, whole in enumerate(whole_halves):
         lo = part * half
-        mixed = jnp.einsum(
-            "kij,kjl->kil", root_left[lo : lo + half], whole.astype(f32),
-            precision=three_pass, preferred_element_type=f32,
+        root = root_left[lo : lo + half]
+        root_hi = root.astype(jnp.bfloat16)
+        rest = root - root_hi.astype(f32)
+        root_mid = rest.astype(jnp.bfloat16)
+        root_lo = (rest - root_mid.astype(f32)).astype(jnp.bfloat16)
+        mixed = sum(
+            jnp.einsum("kij,kjl->kil", part_bf, whole, preferred_element_type=f32)
+            for part_bf in (root_hi, root_mid, root_lo)
         )
         precond_parts.append(jnp.einsum(
             "kij,kjl->kil", mixed, root_right[lo : lo + half], precision=three_pass,
@@ -112,9 +116,9 @@
     velocity_new = beta_mom * momentum + (1.0 - beta_mom) * scale_ratio[:, None, None] * precond
     weight_new = master - learn_rate * velocity_new
     weight_half = weight_new.astype(jnp.bfloat16)
-    returning = pick(weight_half, slot_of_src, src_sent)
+    returning = jnp.take(weight_half, slot_of_src, axis=0, mode="clip")
     back_rows = lax.all_to_all(returning, "shard", split_axis=0, concat_axis=0, tiled=True)
-    weights_local = jnp.take(back_rows, local_owner, axis=0)
+    weights_local = jnp.take(back_rows, local_owner, axis=0, mode="clip")
     return (left_new, right_new, second_new, velocity_new, weight_new, weights_local)
 
 

time: 113 us -> 122 us (1.080)
  matrix products: 16.1 us -> 24 us
  other arithmetic: 19.1 us -> 14.6 us
  local copies, waits for them, and re-layouts: 6.75 us -> 9.26 us
  starting transfers between devices: 25.7 us -> 27.3 us
  waiting for transfers between devices: 44 us -> 45.3 us
    ppermute x2, waiting for transfers between devices: 1.23 us -> 9.41 us  [gather_rows(): from_right = lax.ppermute(piece, 'tensor', left)]
    dot_general x0 -> x4, matrix products: none -> 7.49 us  [on_device(): jnp.einsum('kij,kjl->kil', part_bf, whole, preferred_element_type=f32)]
    ppermute x2, waiting for transfers between devices: 9.43 us -> 4.12 us  [gather_rows(): from_left = lax.ppermute(piece, 'tensor', right)]
    gather x1 -> x2, local copies, waits for them, and re-layouts: 1.79 us -> 5.33 us  [the longest x1 2.78 us: on_device(): returning = jnp.take(weight_half, slot_of_src, axis=0, mode='clip')]
    select_n x4 -> x3, other arithmetic: 3.7 us -> 1.3 us  [pick(): return jnp.where(valid[:, None, None], taken, jnp.zeros((), source.dtype))]
    ppermute x2, starting transfers between devices: 2.4 us -> 0.15 us  [gather_rows(): from_left = lax.ppermute(piece, 'tensor', right)]
    gather x4 -> x3, local copies, waits for them, and re-layouts: 3.65 us -> 1.75 us  [pick(): taken = jnp.take(source, index, axis=0, mode='clip')]
    ppermute x2, starting transfers between devices: 0.27 us -> 1.86 us  [on_device(): lax.ppermute(sums, 'tensor', [(i, i ^ step) for i in range(splits)])]
  transfers between devices with their start and end apart: 10 -> 10, of which waited for: 8 -> 8; matrix products, arithmetic and copies ran while one was open for 18% -> 14% of each run, Pallas kernels for 0% -> 0%
where the time goes in v3:
time: 122 us; the launch traced here: 121 us
  waiting for transfers between devices  45.3 us (37%)
  starting transfers between devices  27.3 us (22%)
  matrix products  24 us (20%)
  other arithmetic  14.6 us (12%)
  local copies, waits for them, and re-layouts  9.26 us (8%)
    all_to_all x1, waiting for transfers between devices, on_device(): lax.all_to_all(outgoing, 'shard', split_axis=0, concat_axis=0, tiled=True)  15.7 us
    all_to_all x1, waiting for transfers between devices, on_device(): lax.all_to_all(returning, 'shard', split_axis=0, concat_axis=0, tiled=True)  10.5 us
    dot_general x2, matrix products, on_device(): jnp.einsum('kij,kjl->kil', mixed, root_right[lo:lo + half], precision=thr...  9.98 us
    ppermute x2, waiting for transfers between devices, gather_rows(): from_right = lax.ppermute(piece, 'tensor', left)  9.41 us
    all_to_all x1, starting transfers between devices, on_device(): lax.all_to_all(outgoing, 'shard', split_axis=0, concat_axis=0, tiled=True)  8.71 us
    all_to_all x1, starting transfers between devices, on_device(): lax.all_to_all(returning, 'shard', split_axis=0, concat_axis=0, tiled=True)  7.92 us
    dot_general x4, matrix products, on_device(): jnp.einsum('kij,kjl->kil', part_bf, whole, preferred_element_type=f32)  7.49 us
    convert_element_type x1, other arithmetic, on_device(): weight_half = weight_new.astype(jnp.bfloat16)  5.07 us
  transfers between devices with their start and end apart: 10, of which 8 were waited for; matrix products, arithmetic and copies ran while one was open for 14% of the time, Pallas kernels for 0%

profile of v3, /device:TPU:1, one launch (start us, length us, event | category | flops | bytes accessed | tf_op | source)
XLA Modules:
  0.0 121.4 jit_solution(14708637565019993268)
XLA Ops:
  0.7 0.8 reshape.53
  2.8 1.1 broadcast_select_fusion
  4.0 8.7 %all-to-all-start = ((bf16[32,64,256]{2,1,0:T(8,128)(2,1)}), bf16[32,64,256]{2,1,0:T(8,128)(2,1)S(1)}, u32[]{:S(2)}, u32[]{:S(2)}) async-start(bf16[32,64,256]{2,1,0:T(8,128)(2,1)} %broadcast_select_fusion), calls=%async_computation | async-start | bytes 2097152 | tf_op jit(solution)/shard_map/all_to_all | solution.py:64
  13.9 15.7 %all-to-all-done = bf16[32,64,256]{2,1,0:T(8,128)(2,1)S(1)} async-done(((bf16[32,64,256]{2,1,0:T(8,128)(2,1)}), bf16[32,64,256]{2,1,0:T(8,128)(2,1)S(1)}, u32[]{:S(2)}, u32[]{:S(2)}) %all-to-all-start) | async-done | bytes 1048608 | tf_op jit(solution)/shard_map/all_to_all | solution.py:64
  30.3 3.8 %collective-permute-start.3 = (bf16[12,64,256]{2,1,0:T(8,128)(2,1)S(1)}, bf16[12,64,256]{2,1,0:T(8,128)(2,1)S(1)}, u32[]{:S(2)}, u32[]{:S(2)}) collective-permute-start(bf16[12,64,256]{2,1,0:T(8,128)(2,1)S(1)} %broadcast_select_fusion.1), channel_id=1, source_target_pairs={{0,3},{1,0},{2,1},{3,2},{4,7},{5,4},{6,5},{7,6},{8,11},{9,8},{10,9... | collective-permute-start | bytes 1179656 | tf_op jit(solution)/shard_map/ppermute | solution.py:18
  35.0 7.5 %collective-permute-done.3 = bf16[12,64,256]{2,1,0:T(8,128)(2,1)S(1)} collective-permute-done((bf16[12,64,256]{2,1,0:T(8,128)(2,1)S(1)}, bf16[12,64,256]{2,1,0:T(8,128)(2,1)S(1)}, u32[]{:S(2)}, u32[]{:S(2)}) %collective-permute-start.3) | collective-permute-done | bytes 393248 | tf_op jit(solution)/shard_map/ppermute | solution.py:18
  42.5 3.4 %collective-permute-start.4 = (bf16[12,64,256]{2,1,0:T(8,128)(2,1)S(1)}, bf16[12,64,256]{2,1,0:T(8,128)(2,1)}, u32[]{:S(2)}, u32[]{:S(2)}) collective-permute-start(bf16[12,64,256]{2,1,0:T(8,128)(2,1)S(1)} %collective-permute-done.3), channel_id=1, source_target_pairs={{0,3},{1,0},{2,1},{3,2},{4,7},{5,4},{6,5},{7,6},{8,11},{9,8},{10,9... | collective-permute-start | bytes 1179656 | tf_op jit(solution)/shard_map/ppermute | solution.py:22
  45.9 3.4 %fusion.11 = (f32[24]{0:T(128)S(1)}, f32[24,64,256]{2,1,0:T(8,128)}) fusion(bf16[12,64,256]{2,1,0:T(8,128)(2,1)S(1)} %broadcast_select_fusion.1, bf16[12,64,256]{2,1,0:T(8,128)(2,1)S(1)} %broadcast_select_fusion.2, f32[24,64,256]{2,1,0:T(8,128)} %param.25), kind=kLoop, calls=%fused_computation.32 | loop fusion | flops 3932136 | bytes 3932256 | tf_op jit(solution)/shard_map/reduce_sum | solution.py:105
  49.3 1.4 %collective-permute-start.2 = (bf16[12,64,256]{2,1,0:T(8,128)(2,1)S(1)}, bf16[12,64,256]{2,1,0:T(8,128)(2,1)}, u32[]{:S(2)}, u32[]{:S(2)}) collective-permute-start(bf16[12,64,256]{2,1,0:T(8,128)(2,1)S(1)} %collective-permute-done.1), channel_id=1, source_target_pairs={{0,1},{1,2},{2,3},{3,0},{4,5},{5,6},{6,7},{7,4},{8,9},{9,10},{10,1... | collective-permute-start | bytes 1179656 | tf_op jit(solution)/shard_map/ppermute | solution.py:20
  50.8 4.1 %collective-permute-done.5 = bf16[12,64,256]{2,1,0:T(8,128)(2,1)} collective-permute-done((bf16[12,64,256]{2,1,0:T(8,128)(2,1)S(1)}, bf16[12,64,256]{2,1,0:T(8,128)(2,1)}, u32[]{:S(2)}, u32[]{:S(2)}) %collective-permute-start.5) | collective-permute-done | bytes 393248 | tf_op jit(solution)/shard_map/ppermute | solution.py:17
  54.9 1.2 %conditional.3 = (bf16[12,256,256]{2,1,0:T(8,128)(2,1)S(1)}) conditional(s32[]{:T(128)} %clamp.4, (bf16[12,64,256]{2,1,0:T(8,128)(2,1)S(1)}, bf16[12,64,256]{2,1,0:T(8,128)(2,1)S(1)}, bf16[12,64,256]{2,1,0:T(8,128)(2,1)}, bf16[12,64,256]{2,1,0:T(8,128)(2,1)}) %tuple.42, (bf16[12,64,256]{2,1,0:T(8,128)(2,1)}, ...), branch_computations={%region_9.10_spmd, %region_10.11_spmd, %region_11.12_spmd, %region... | conditional | flops 6291456 | bytes 3145736 | solution.py:28
  54.9 1.2 %pad_maximum_fusion.4 = bf16[12,256,256]{2,1,0:T(8,128)(2,1)S(1)} fusion(bf16[12,64,256]{2,1,0:T(8,128)(2,1)} %get-tuple-element.93, bf16[12,64,256]{2,1,0:T(8,128)(2,1)} %get-tuple-element.92, bf16[12,64,256]{2,1,0:T(8,128)(2,1)S(1)} %get-tuple-element.91, bf16[12,64,256]{2,1,0:T(8,128)(2,1)S(1)} %get-tuple-element.90), kind=kLoop, calls=%fused_computation.9 | loop fusion | flops 6291456 | bytes 3145728 | tf_op jit(solution)/shard_map/cond/branch_0_fun/concatenate | solution.py:26
  56.2 2.5 %fusion.21 = f32[12,64,256]{2,1,0:T(8,128)} fusion(bf16[12,256,256]{2,1,0:T(8,128)(2,1)S(1)} %get-tuple-element.136, f32[24,64,256]{2,1,0:T(8,128)} %param.23), kind=kOutput, calls=%fused_computation.52 | convolution fusion | flops 102039552 | bytes 3145728 | tf_op jit(solution)/shard_map/kij,kjl->kil/dot_general | solution.py:95
  58.7 1.2 %fusion.26 = f32[12,64,256]{2,1,0:T(8,128)} fusion(bf16[12,256,256]{2,1,0:T(8,128)(2,1)S(1)} %get-tuple-element.136, f32[24,64,256]{2,1,0:T(8,128)S(1)} %copy-done.7), kind=kOutput, calls=%fused_computation.59 | convolution fusion | flops 101449728 | bytes 3145728 | tf_op jit(solution)/shard_map/kij,kjl->kil/dot_general | solution.py:95
  59.9 1.9 %collective-permute-done = bf16[12,64,256]{2,1,0:T(8,128)(2,1)} collective-permute-done((bf16[12,64,256]{2,1,0:T(8,128)(2,1)S(1)}, bf16[12,64,256]{2,1,0:T(8,128)(2,1)}, u32[]{:S(2)}, u32[]{:S(2)}) %collective-permute-start) | collective-permute-done | bytes 393248 | tf_op jit(solution)/shard_map/ppermute | solution.py:18
  61.8 1.5 %collective-permute-done.2 = bf16[12,64,256]{2,1,0:T(8,128)(2,1)} collective-permute-done((bf16[12,64,256]{2,1,0:T(8,128)(2,1)S(1)}, bf16[12,64,256]{2,1,0:T(8,128)(2,1)}, u32[]{:S(2)}, u32[]{:S(2)}) %collective-permute-start.2) | collective-permute-done | bytes 393248 | tf_op jit(solution)/shard_map/ppermute | solution.py:20
  63.3 2.3 %conditional.2 = (bf16[12,256,256]{2,1,0:T(8,128)(2,1)S(1)}) conditional(s32[]{:T(128)} %clamp.4, (bf16[12,64,256]{2,1,0:T(8,128)(2,1)S(1)}, bf16[12,64,256]{2,1,0:T(8,128)(2,1)}, bf16[12,64,256]{2,1,0:T(8,128)(2,1)}, bf16[12,64,256]{2,1,0:T(8,128)(2,1)S(1)}) %tuple.38, (bf16[12,64,256]{2,1,0:T(8,128)(2,1)S(1)}, ...), branch_computations={%region_5.6_spmd, %region_6.7_spmd, %region_7.8_spmd, %region_8.9_... | conditional | flops 6291456 | bytes 6291520 | solution.py:28
  64.2 1.5 %pad_maximum_fusion = bf16[12,256,256]{2,1,0:T(8,128)(2,1)S(1)} fusion(bf16[12,64,256]{2,1,0:T(8,128)(2,1)} %copy-done.9, bf16[12,64,256]{2,1,0:T(8,128)(2,1)} %get-tuple-element.71, bf16[12,64,256]{2,1,0:T(8,128)(2,1)} %get-tuple-element.70, bf16[12,64,256]{2,1,0:T(8,128)(2,1)} %copy-done.3), kind=kLoop, calls=%fused_computation.5 | loop fusion | flops 6291456 | bytes 3145728 | tf_op jit(solution)/shard_map/cond/branch_0_fun/concatenate | solution.py:26
  65.7 2.5 %fusion.20 = f32[12,64,256]{2,1,0:T(8,128)} fusion(bf16[12,256,256]{2,1,0:T(8,128)(2,1)S(1)} %get-tuple-element.135, f32[24,64,256]{2,1,0:T(8,128)} %param.23), kind=kOutput, calls=%fused_computation.51 | convolution fusion | flops 102039552 | bytes 3145728 | tf_op jit(solution)/shard_map/kij,kjl->kil/dot_general | solution.py:95
  68.2 1.2 %fusion.29 = f32[12,64,256]{2,1,0:T(8,128)} fusion(bf16[12,256,256]{2,1,0:T(8,128)(2,1)S(1)} %get-tuple-element.135, f32[24,64,256]{2,1,0:T(8,128)S(1)} %copy-done.8), kind=kOutput, calls=%fused_computation.60 | convolution fusion | flops 101449728 | bytes 3145728 | tf_op jit(solution)/shard_map/kij,kjl->kil/dot_general | solution.py:95
  69.4 5.0 %multiply_reduce_fusion = (f32[12]{0:T(128)S(1)}, f32[12,64,256]{2,1,0:T(8,128)}) fusion(f32[24,256,256]{2,1,0:T(8,128)} %param.24, f32[12,64,256]{2,1,0:T(8,128)} %fusion.21, f32[12,64,256]{2,1,0:T(8,128)} %fusion.26, bf16[12,256,256]{2,1,0:T(8,128)(2,1)S(1)} %get-tuple-element.136, f32[24,64,256]{2,1,0:T(8,128)} %param.23), kind=kOutput, calls=%fused_computation.41 | convolution fusion | flops 403439616 | bytes 7471152 | tf_op jit(solution)/shard_map/kij,kjl->kil/dot_general | solution.py:98
  74.4 5.0 %multiply_reduce_fusion.1 = (f32[12]{0:T(128)S(1)}, f32[12,64,256]{2,1,0:T(8,128)}) fusion(f32[24,256,256]{2,1,0:T(8,128)} %param.24, f32[12,64,256]{2,1,0:T(8,128)} %fusion.20, f32[12,64,256]{2,1,0:T(8,128)} %fusion.29, bf16[12,256,256]{2,1,0:T(8,128)(2,1)S(1)} %get-tuple-element.135, f32[24,64,256]{2,1,0:T(8,128)} %param.23), kind=kOutput, calls=%fused_computation.44 | convolution fusion | flops 403439616 | bytes 7471152 | tf_op jit(solution)/shard_map/kij,kjl->kil/dot_general | solution.py:98
  80.1 1.9 %collective-permute-done.6 = f32[2,24]{1,0:T(2,128)S(1)} collective-permute-done((f32[2,24]{1,0:T(2,128)S(1)}, f32[2,24]{1,0:T(2,128)S(1)}, u32[]{:S(2)}, u32[]{:S(2)}) %collective-permute-start.6) | collective-permute-done | bytes 224 | tf_op jit(solution)/shard_map/ppermute | solution.py:109
  82.0 1.8 %collective-permute-start.7 = (f32[2,24]{1,0:T(2,128)S(1)}, f32[2,24]{1,0:T(2,128)S(1)}, u32[]{:S(2)}, u32[]{:S(2)}) collective-permute-start(f32[2,24]{1,0:T(2,128)S(1)} %fusion.36), channel_id=1, source_target_pairs={{0,2},{1,3},{2,0},{3,1},{4,6},{5,7},{6,4},{7,5},{8,10},{9,11},{10,... | collective-permute-start | bytes 584 | tf_op jit(solution)/shard_map/ppermute | solution.py:109
  83.8 2.2 %collective-permute-done.7 = f32[2,24]{1,0:T(2,128)S(1)} collective-permute-done((f32[2,24]{1,0:T(2,128)S(1)}, f32[2,24]{1,0:T(2,128)S(1)}, u32[]{:S(2)}, u32[]{:S(2)}) %collective-permute-start.7) | collective-permute-done | bytes 224 | tf_op jit(solution)/shard_map/ppermute | solution.py:109
  86.0 5.1 %fusion.37 = (bf16[24,64,256]{2,1,0:T(8,128)(2,1)}, f32[24,64,256]{2,1,0:T(8,128)}, f32[24,64,256]{2,1,0:T(8,128)}) fusion(f32[24,64,256]{2,1,0:T(8,128)} %param.27, f32[12,64,256]{2,1,0:T(8,128)} %get-tuple-element.130, f32[12,64,256]{2,1,0:T(8,128)} %get-tuple-element.132, f32[24]{0:T(128)S(1)} %multiply_bitcast_fusion, f32[24,64,256]{2,1,0:T(8,128)} %param.26), kind=kLoop, calls=%fused_computation.81 | loop fusion | flops 2752512 | bytes 8650848 | tf_op jit(solution)/shard_map/convert_element_type | solution.py:118
  91.1 2.8 %gather_fusion.3 = bf16[32,64,256]{2,1,0:T(8,128)(2,1)} fusion(bf16[24,64,256]{2,1,0:T(8,128)(2,1)} %get-tuple-element.120, s32[1024]{0:T(1024)S(1)} %pad_clamp_fusion.1), kind=kCustom, calls=%fused_computation.3 | custom fusion | bytes 2097280 | tf_op jit(solution)/shard_map/jit(_take)/gather | solution.py:119
  93.9 7.9 %all-to-all-start.1 = ((bf16[32,64,256]{2,1,0:T(8,128)(2,1)}), bf16[32,64,256]{2,1,0:T(8,128)(2,1)}, u32[]{:S(2)}, u32[]{:S(2)}) async-start(bf16[32,64,256]{2,1,0:T(8,128)(2,1)} %gather_fusion.3), calls=%async_computation.1 | async-start | bytes 2097152 | tf_op jit(solution)/shard_map/all_to_all | solution.py:120
  101.8 4.0 %multiply_add_fusion.1 = f32[24,64,256]{2,1,0:T(8,128)} fusion(f32[24,64,256]{2,1,0:T(8,128)} %param.21, bf16[12,256,256]{2,1,0:T(8,128)(2,1)S(1)} %get-tuple-element.136, bf16[12,256,256]{2,1,0:T(8,128)(2,1)S(1)} %get-tuple-element.135, bf16[12,64,256]{2,1,0:T(8,128)(2,1)} %copy-done.1, bf16[12,64,256]{2,1,0:T(8,128)(2,1)} %copy-done.2), kind=kOutput, calls=%fused_computation.31 | convolution fusion | flops 204472320 | bytes 7077888 | tf_op jit(solution)/shard_map/kij,klj->kil/dot_general | solution.py:76
  105.8 2.5 %multiply_add_fusion = f32[24,64,256]{2,1,0:T(8,128)} fusion(f32[24,64,256]{2,1,0:T(8,128)S(1)} %copy-done.16, bf16[12,256,256]{2,1,0:T(8,128)(2,1)S(1)} %get-tuple-element.136, bf16[12,256,256]{2,1,0:T(8,128)(2,1)S(1)} %get-tuple-element.135, s32[]{:T(128)S(6)} %select_n.34), kind=kOutput, calls=%fused_computation.30 | convolution fusion | flops 205651968 | bytes 9437188 | tf_op jit(solution)/shard_map/kji,kjl->kil/dot_general | solution.py:79
  108.4 10.5 %all-to-all-done.1 = bf16[32,64,256]{2,1,0:T(8,128)(2,1)} async-done(((bf16[32,64,256]{2,1,0:T(8,128)(2,1)}), bf16[32,64,256]{2,1,0:T(8,128)(2,1)}, u32[]{:S(2)}, u32[]{:S(2)}) %all-to-all-start.1) | async-done | bytes 1048608 | tf_op jit(solution)/shard_map/all_to_all | solution.py:120
  118.9 2.6 %gather_fusion.4 = bf16[12,64,256]{2,1,0:T(8,128)(2,1)} fusion(bf16[32,64,256]{2,1,0:T(8,128)(2,1)} %all-to-all-done.1, s32[1024]{0:T(1024)S(1)} %pad_clamp_fusion), kind=kCustom, calls=%fused_computation.4 | custom fusion | bytes 786480 | tf_op jit(solution)/shard_map/jit(_take)/gather | solution.py:121
  (54 shorter events, 5.7 us)
Async XLA Ops:
  0.6 1.6 %copy-start = (bf16[12,64,256]{2,1,0:T(8,128)(2,1)S(1)}, bf16[12,64,256]{2,1,0:T(8,128)(2,1)}, u32[]{:S(2)}) copy-start(bf16[12,64,256]{2,1,0:T(8,128)(2,1)} %param.18) | copy-start | bytes 1179652
  1.5 2.5 %copy-start.14 = (s32[12]{0:T(128)}, s32[12]{0:T(128)S(1)}, u32[]{:S(2)}) copy-start(s32[12]{0:T(128)S(1)} %fusion.33) | copy-start | bytes 148
  4.0 8.7 %copy-start.13 = (s32[384]{0:T(512)S(1)}, s32[384]{0:T(512)}, u32[]{:S(2)}) copy-start(s32[384]{0:T(512)} %param.20) | copy-start | bytes 4612
  4.0 25.6 %all-to-all-start = ((bf16[32,64,256]{2,1,0:T(8,128)(2,1)}), bf16[32,64,256]{2,1,0:T(8,128)(2,1)S(1)}, u32[]{:S(2)}, u32[]{:S(2)}) async-start(bf16[32,64,256]{2,1,0:T(8,128)(2,1)} %broadcast_select_fusion), calls=%async_computation | async-start | bytes 2097152 | tf_op jit(solution)/shard_map/all_to_all | solution.py:64
  30.3 24.6 %copy-start.1 = (bf16[12,64,256]{2,1,0:T(8,128)(2,1)}, bf16[12,64,256]{2,1,0:T(8,128)(2,1)S(1)}, u32[]{:S(2)}) copy-start(bf16[12,64,256]{2,1,0:T(8,128)(2,1)S(1)} %broadcast_select_fusion.1) | copy-start | bytes 1179652
  30.3 12.2 %collective-permute-start.3 = (bf16[12,64,256]{2,1,0:T(8,128)(2,1)S(1)}, bf16[12,64,256]{2,1,0:T(8,128)(2,1)S(1)}, u32[]{:S(2)}, u32[]{:S(2)}) collective-permute-start(bf16[12,64,256]{2,1,0:T(8,128)(2,1)S(1)} %broadcast_select_fusion.1), channel_id=1, source_target_pairs={{0,3},{1,0},{2,1},{3,2},{4,7},{5,4},{6,5},{7,6},{8,11},{9,8},{10,9... | collective-permute-start | bytes 1179656 | tf_op jit(solution)/shard_map/ppermute | solution.py:18
  34.8 28.5 %copy-start.2 = (bf16[12,64,256]{2,1,0:T(8,128)(2,1)}, bf16[12,64,256]{2,1,0:T(8,128)(2,1)S(1)}, u32[]{:S(2)}) copy-start(bf16[12,64,256]{2,1,0:T(8,128)(2,1)S(1)} %broadcast_select_fusion.2) | copy-start | bytes 1179652
  34.8 14.5 %collective-permute-start.1 = (bf16[12,64,256]{2,1,0:T(8,128)(2,1)S(1)}, bf16[12,64,256]{2,1,0:T(8,128)(2,1)S(1)}, u32[]{:S(2)}, u32[]{:S(2)}) collective-permute-start(bf16[12,64,256]{2,1,0:T(8,128)(2,1)S(1)} %broadcast_select_fusion.2), channel_id=1, source_target_pairs={{0,1},{1,2},{2,3},{3,0},{4,5},{5,6},{6,7},{7,4},{8,9},{9,10},{10,1... | collective-permute-start | bytes 1179656 | tf_op jit(solution)/shard_map/ppermute | solution.py:17
  34.9 20.0 %collective-permute-start.5 = (bf16[12,64,256]{2,1,0:T(8,128)(2,1)S(1)}, bf16[12,64,256]{2,1,0:T(8,128)(2,1)}, u32[]{:S(2)}, u32[]{:S(2)}) collective-permute-start(bf16[12,64,256]{2,1,0:T(8,128)(2,1)S(1)} %broadcast_select_fusion.1), channel_id=1, source_target_pairs={{0,1},{1,2},{2,3},{3,0},{4,5},{5,6},{6,7},{7,4},{8,9},{9,10},{10,1... | collective-permute-start | bytes 1179656 | tf_op jit(solution)/shard_map/ppermute | solution.py:17
  42.5 12.4 %collective-permute-start.4 = (bf16[12,64,256]{2,1,0:T(8,128)(2,1)S(1)}, bf16[12,64,256]{2,1,0:T(8,128)(2,1)}, u32[]{:S(2)}, u32[]{:S(2)}) collective-permute-start(bf16[12,64,256]{2,1,0:T(8,128)(2,1)S(1)} %collective-permute-done.3), channel_id=1, source_target_pairs={{0,3},{1,0},{2,1},{3,2},{4,7},{5,4},{6,5},{7,6},{8,11},{9,8},{10,9... | collective-permute-start | bytes 1179656 | tf_op jit(solution)/shard_map/ppermute | solution.py:22
  45.9 15.9 %collective-permute-start = (bf16[12,64,256]{2,1,0:T(8,128)(2,1)S(1)}, bf16[12,64,256]{2,1,0:T(8,128)(2,1)}, u32[]{:S(2)}, u32[]{:S(2)}) collective-permute-start(bf16[12,64,256]{2,1,0:T(8,128)(2,1)S(1)} %broadcast_select_fusion.2), channel_id=1, source_target_pairs={{0,3},{1,0},{2,1},{3,2},{4,7},{5,4},{6,5},{7,6},{8,11},{9,8},{10,9... | collective-permute-start | bytes 1179656 | tf_op jit(solution)/shard_map/ppermute | solution.py:18
  49.3 14.0 %collective-permute-start.2 = (bf16[12,64,256]{2,1,0:T(8,128)(2,1)S(1)}, bf16[12,64,256]{2,1,0:T(8,128)(2,1)}, u32[]{:S(2)}, u32[]{:S(2)}) collective-permute-start(bf16[12,64,256]{2,1,0:T(8,128)(2,1)S(1)} %collective-permute-done.1), channel_id=1, source_target_pairs={{0,1},{1,2},{2,3},{3,0},{4,5},{5,6},{6,7},{7,4},{8,9},{9,10},{10,1... | collective-permute-start | bytes 1179656 | tf_op jit(solution)/shard_map/ppermute | solution.py:20
  56.1 2.5 %copy-start.7 = (f32[24,64,256]{2,1,0:T(8,128)S(1)}, f32[24,64,256]{2,1,0:T(8,128)}, u32[]{:S(2)}) copy-start(f32[24,64,256]{2,1,0:T(8,128)} %param.23) | copy-start | bytes 4718596
  63.3 0.7 copy-start.3
  63.3 0.9 copy-start.9
  65.7 2.5 %copy-start.8 = (f32[24,64,256]{2,1,0:T(8,128)S(1)}, f32[24,64,256]{2,1,0:T(8,128)}, u32[]{:S(2)}) copy-start(f32[24,64,256]{2,1,0:T(8,128)} %param.23) | copy-start | bytes 4718596
  79.5 2.5 %collective-permute-start.6 = (f32[2,24]{1,0:T(2,128)S(1)}, f32[2,24]{1,0:T(2,128)S(1)}, u32[]{:S(2)}, u32[]{:S(2)}) collective-permute-start(f32[2,24]{1,0:T(2,128)S(1)} %pad_maximum_fusion.17), channel_id=1, source_target_pairs={{0,1},{1,0},{2,3},{3,2},{4,5},{5,4},{6,7},{7,6},{8,9},{9,8},{10,11... | collective-permute-start | bytes 584 | tf_op jit(solution)/shard_map/ppermute | solution.py:109
  82.0 4.0 %collective-permute-start.7 = (f32[2,24]{1,0:T(2,128)S(1)}, f32[2,24]{1,0:T(2,128)S(1)}, u32[]{:S(2)}, u32[]{:S(2)}) collective-permute-start(f32[2,24]{1,0:T(2,128)S(1)} %fusion.36), channel_id=1, source_target_pairs={{0,2},{1,3},{2,0},{3,1},{4,6},{5,7},{6,4},{7,5},{8,10},{9,11},{10,... | collective-permute-start | bytes 584 | tf_op jit(solution)/shard_map/ppermute | solution.py:109
  93.9 7.9 %copy-start.15 = (s32[12]{0:T(128)S(1)}, s32[12]{0:T(128)}, u32[]{:S(2)}) copy-start(s32[12]{0:T(128)} %copy-done.14) | copy-start | bytes 148
  93.9 25.0 %all-to-all-start.1 = ((bf16[32,64,256]{2,1,0:T(8,128)(2,1)}), bf16[32,64,256]{2,1,0:T(8,128)(2,1)}, u32[]{:S(2)}, u32[]{:S(2)}) async-start(bf16[32,64,256]{2,1,0:T(8,128)(2,1)} %gather_fusion.3), calls=%async_computation.1 | async-start | bytes 2097152 | tf_op jit(solution)/shard_map/all_to_all | solution.py:120
  101.8 4.0 %copy-start.16 = (f32[24,64,256]{2,1,0:T(8,128)S(1)}, f32[24,64,256]{2,1,0:T(8,128)}, u32[]{:S(2)}) copy-start(f32[24,64,256]{2,1,0:T(8,128)} %param.22) | copy-start | bytes 4718596

commit v4 on v1

--- a/solution.py
+++ b/solution.py
@@ -29,8 +29,11 @@
 
 
 def pick(source, index, valid):
-    taken = source.at[index].get(mode="promise_in_bounds")
-    return jnp.where(valid[:, None, None], taken, jnp.zeros((), source.dtype))
+    ids = jnp.arange(source.shape[0], dtype=jnp.int32)
+    chooser = ((index[:, None] == ids[None, :]) & valid[:, None]).astype(source.dtype)
+    flat = source.reshape(source.shape[0], -1)
+    taken = jnp.dot(chooser, flat, preferred_element_type=jnp.float32).astype(source.dtype)
+    return taken.reshape((index.shape[0],) + source.shape[1:])
 
 
 def on_device(
@@ -111,9 +114,9 @@
     velocity_new = beta_mom * momentum + (1.0 - beta_mom) * scale_ratio[:, None, None] * precond
     weight_new = master - learn_rate * velocity_new
     weight_half = weight_new.astype(jnp.bfloat16)
-    returning = weight_half.at[slot_of_src].get(mode="promise_in_bounds")
+    returning = pick(weight_half, slot_of_src, jnp.any(slot_match, axis=0))
     back_rows = lax.all_to_all(returning, "shard", split_axis=0, concat_axis=0, tiled=True)
-    weights_local = back_rows.at[local_owner].get(mode="promise_in_bounds")
+    weights_local = pick(back_rows, local_owner, jnp.ones(local_owner.shape, jnp.bool_))
     return (left_new, right_new, second_new, velocity_new, weight_new, weights_local)
 
 

time: 113 us -> 115 us (1.018)
  other arithmetic: 15.1 us -> 12.8 us
  matrix products: 16.4 us -> 18.5 us
  local copies, waits for them, and re-layouts: 7.85 us -> 9.9 us
    unnamed x12 -> x18, local copies, waits for them, and re-layouts: 0.03 us -> 7.01 us
    gather x5 -> x0, local copies, waits for them, and re-layouts: 5.95 us -> none  [the longest x1 2.55 us: on_device(): weights_local = back_rows.at[local_owner].get(mode='promise_in_bounds')]
    dot_general x0 -> x5, matrix products: none -> 2.01 us  [pick(): jnp.dot(chooser, flat, preferred_element_type=jnp.float32)]
    select_n x6 -> x0, other arithmetic: 1.9 us -> none  [the longest x3 1.3 us: pick(): return jnp.where(valid[:, None, None], taken, jnp.zeros((), source.dtype))]
where the time goes in v4:
time: 115 us; the launch traced here: 114 us
  waiting for transfers between devices  47 us (41%)
  starting transfers between devices  25.2 us (22%)
  matrix products  18.5 us (16%)
  other arithmetic  12.8 us (11%)
  local copies, waits for them, and re-layouts  9.9 us (9%)
    all_to_all x1, waiting for transfers between devices, on_device(): lax.all_to_all(outgoing, 'shard', split_axis=0, concat_axis=0, tiled=True)  15.7 us
    all_to_all x1, waiting for transfers between devices, on_device(): lax.all_to_all(returning, 'shard', split_axis=0, concat_axis=0, tiled=True)  10.5 us
    dot_general x2, matrix products, on_device(): jnp.einsum('kij,kjl->kil', mixed, root_right[lo:lo + half], precision=thr...  9.94 us
    ppermute x2, waiting for transfers between devices, gather_rows(): from_left = lax.ppermute(piece, 'tensor', right)  9.84 us
    all_to_all x1, starting transfers between devices, on_device(): lax.all_to_all(outgoing, 'shard', split_axis=0, concat_axis=0, tiled=True)  8.71 us
    all_to_all x1, starting transfers between devices, on_device(): lax.all_to_all(returning, 'shard', split_axis=0, concat_axis=0, tiled=True)  8.08 us
    unnamed x18, local copies, waits for them, and re-layouts  7.01 us
    ppermute x2, waiting for transfers between devices, on_device(): lax.ppermute(sums, 'tensor', [(i, i ^ step) for i in range(splits)])  5.79 us
  transfers between devices with their start and end apart: 10, of which 8 were waited for; matrix products, arithmetic and copies ran while one was open for 16% of the time, Pallas kernels for 0%

profile of v4, /device:TPU:1, one launch (start us, length us, event | category | flops | bytes accessed | tf_op | source)
XLA Modules:
  0.0 114.2 jit_solution(7591908264779018618)
XLA Ops:
  0.6 0.8 reshape.87
  2.1 1.0 pad.40
  4.0 1.2 %copy.23 = bf16[4,8,64,256]{3,2,1,0:T(8,128)(2,1)} copy(bf16[4,8,64,256]{3,1,2,0:T(8,128)(2,1)S(1)} %bitcast.41) | data formatting | bytes 2097152
  5.2 8.7 %all-to-all-start = ((bf16[32,64,256]{2,1,0:T(8,128)(2,1)}), bf16[32,64,256]{2,1,0:T(8,128)(2,1)S(1)}, u32[]{:S(2)}, u32[]{:S(2)}) async-start(bf16[32,64,256]{2,1,0:T(8,128)(2,1)} %bitcast.8), calls=%async_computation | async-start | bytes 2097152 | tf_op jit(solution)/shard_map/all_to_all | solution.py:67
  15.1 15.7 %all-to-all-done = bf16[32,64,256]{2,1,0:T(8,128)(2,1)S(1)} async-done(((bf16[32,64,256]{2,1,0:T(8,128)(2,1)}), bf16[32,64,256]{2,1,0:T(8,128)(2,1)S(1)}, u32[]{:S(2)}, u32[]{:S(2)}) %all-to-all-start) | async-done | bytes 1048608 | tf_op jit(solution)/shard_map/all_to_all | solution.py:67
  32.4 1.7 %collective-permute-start.1 = (bf16[12,64,256]{2,1,0:T(8,128)(2,1)S(1)}, bf16[12,64,256]{2,1,0:T(8,128)(2,1)S(1)}, u32[]{:S(2)}, u32[]{:S(2)}) collective-permute-start(bf16[12,64,256]{2,1,0:T(8,128)(2,1)S(1)} %get-tuple-element.126), channel_id=1, source_target_pairs={{0,1},{1,2},{2,3},{3,0},{4,5},{5,6},{6,7},{7,4},{8,9},{9,10},{10,1... | collective-permute-start | bytes 1179656 | tf_op jit(solution)/shard_map/ppermute | solution.py:17
  34.2 2.2 %collective-permute-start.3 = (bf16[12,64,256]{2,1,0:T(8,128)(2,1)S(1)}, bf16[12,64,256]{2,1,0:T(8,128)(2,1)S(1)}, u32[]{:S(2)}, u32[]{:S(2)}) collective-permute-start(bf16[12,64,256]{2,1,0:T(8,128)(2,1)S(1)} %get-tuple-element.128), channel_id=1, source_target_pairs={{0,3},{1,0},{2,1},{3,2},{4,7},{5,4},{6,5},{7,6},{8,11},{9,8},{10,9... | collective-permute-start | bytes 1179656 | tf_op jit(solution)/shard_map/ppermute | solution.py:18
  36.4 1.5 %collective-permute-start = (bf16[12,64,256]{2,1,0:T(8,128)(2,1)S(1)}, bf16[12,64,256]{2,1,0:T(8,128)(2,1)S(1)}, u32[]{:S(2)}, u32[]{:S(2)}) collective-permute-start(bf16[12,64,256]{2,1,0:T(8,128)(2,1)S(1)} %get-tuple-element.126), channel_id=1, source_target_pairs={{0,3},{1,0},{2,1},{3,2},{4,7},{5,4},{6,5},{7,6},{8,11},{9,8},{10,9... | collective-permute-start | bytes 1179656 | tf_op jit(solution)/shard_map/ppermute | solution.py:18
  37.9 7.8 %collective-permute-done.1 = bf16[12,64,256]{2,1,0:T(8,128)(2,1)S(1)} collective-permute-done((bf16[12,64,256]{2,1,0:T(8,128)(2,1)S(1)}, bf16[12,64,256]{2,1,0:T(8,128)(2,1)S(1)}, u32[]{:S(2)}, u32[]{:S(2)}) %collective-permute-start.1) | collective-permute-done | bytes 393248 | tf_op jit(solution)/shard_map/ppermute | solution.py:17
  45.6 0.7 collective-permute-start.5
  46.3 2.0 %collective-permute-start.4 = (bf16[12,64,256]{2,1,0:T(8,128)(2,1)S(1)}, bf16[12,64,256]{2,1,0:T(8,128)(2,1)}, u32[]{:S(2)}, u32[]{:S(2)}) collective-permute-start(bf16[12,64,256]{2,1,0:T(8,128)(2,1)S(1)} %collective-permute-done.3), channel_id=1, source_target_pairs={{0,3},{1,0},{2,1},{3,2},{4,7},{5,4},{6,5},{7,6},{8,11},{9,8},{10,9... | collective-permute-start | bytes 1179656 | tf_op jit(solution)/shard_map/ppermute | solution.py:22
  48.3 3.4 %fusion.11 = (f32[24]{0:T(128)S(1)}, f32[24,64,256]{2,1,0:T(8,128)}) fusion(bf16[24,64,256]{2,1,0:T(8,128)(2,1)S(1)} %get-tuple-element.129, f32[24,64,256]{2,1,0:T(8,128)} %param.25), kind=kLoop, calls=%fused_computation.32 | loop fusion | flops 3538920 | bytes 3932256 | tf_op jit(solution)/shard_map/reduce_sum | solution.py:103
  51.8 1.7 %collective-permute-done = bf16[12,64,256]{2,1,0:T(8,128)(2,1)S(1)} collective-permute-done((bf16[12,64,256]{2,1,0:T(8,128)(2,1)S(1)}, bf16[12,64,256]{2,1,0:T(8,128)(2,1)S(1)}, u32[]{:S(2)}, u32[]{:S(2)}) %collective-permute-start) | collective-permute-done | bytes 393248 | tf_op jit(solution)/shard_map/ppermute | solution.py:18
  53.5 3.5 %collective-permute-done.2 = bf16[12,64,256]{2,1,0:T(8,128)(2,1)} collective-permute-done((bf16[12,64,256]{2,1,0:T(8,128)(2,1)S(1)}, bf16[12,64,256]{2,1,0:T(8,128)(2,1)}, u32[]{:S(2)}, u32[]{:S(2)}) %collective-permute-start.2) | collective-permute-done | bytes 393248 | tf_op jit(solution)/shard_map/ppermute | solution.py:20
  56.9 1.1 conditional.2
  56.9 1.1 pad_maximum_fusion
  58.1 5.2 %multiply_reduce_fusion.1 = (f32[12]{0:T(128)}, f32[12,64,256]{2,1,0:T(8,128)}) fusion(f32[24,256,256]{2,1,0:T(8,128)} %param.24, bf16[12,256,256]{2,1,0:T(8,128)(2,1)S(1)} %get-tuple-element.138, f32[24,64,256]{2,1,0:T(8,128)} %param.23), kind=kOutput, calls=%fused_computation.37 | convolution fusion | flops 604372992 | bytes 6291504 | tf_op jit(solution)/shard_map/kij,kjl->kil/dot_general | solution.py:96
  63.3 2.1 %collective-permute-done.5 = bf16[12,64,256]{2,1,0:T(8,128)(2,1)} collective-permute-done((bf16[12,64,256]{2,1,0:T(8,128)(2,1)S(1)}, bf16[12,64,256]{2,1,0:T(8,128)(2,1)}, u32[]{:S(2)}, u32[]{:S(2)}) %collective-permute-start.5) | collective-permute-done | bytes 393248 | tf_op jit(solution)/shard_map/ppermute | solution.py:17
  65.4 2.1 %conditional.3 = (bf16[12,256,256]{2,1,0:T(8,128)(2,1)S(1)}) conditional(s32[]{:T(128)} %clamp.4, (bf16[12,64,256]{2,1,0:T(8,128)(2,1)S(1)}, bf16[12,64,256]{2,1,0:T(8,128)(2,1)S(1)}, bf16[12,64,256]{2,1,0:T(8,128)(2,1)}, bf16[12,64,256]{2,1,0:T(8,128)(2,1)}) %tuple.42, (bf16[12,64,256]{2,1,0:T(8,128)(2,1)}, ...), branch_computations={%region_9.10_spmd, %region_10.11_spmd, %region_11.12_spmd, %region... | conditional | flops 6291456 | bytes 4718628 | solution.py:28
  65.4 0.7 copy-done
  66.1 1.3 %pad_maximum_fusion.4 = bf16[12,256,256]{2,1,0:T(8,128)(2,1)S(1)} fusion(bf16[12,64,256]{2,1,0:T(8,128)(2,1)} %get-tuple-element.93, bf16[12,64,256]{2,1,0:T(8,128)(2,1)} %get-tuple-element.92, bf16[12,64,256]{2,1,0:T(8,128)(2,1)} %copy-done, bf16[12,64,256]{2,1,0:T(8,128)(2,1)S(1)} %get-tuple-element.90), kind=kLoop, calls=%fused_computation.4 | loop fusion | flops 6291456 | bytes 3145728 | tf_op jit(solution)/shard_map/cond/branch_0_fun/concatenate | solution.py:26
  67.5 4.7 %multiply_reduce_fusion = (f32[12]{0:T(128)S(1)}, f32[12,64,256]{2,1,0:T(8,128)}) fusion(f32[24,256,256]{2,1,0:T(8,128)} %param.24, bf16[12,256,256]{2,1,0:T(8,128)(2,1)S(1)} %get-tuple-element.139, f32[24,64,256]{2,1,0:T(8,128)} %param.23), kind=kOutput, calls=%fused_computation.35 | convolution fusion | flops 604372992 | bytes 6291504 | tf_op jit(solution)/shard_map/kij,kjl->kil/dot_general | solution.py:96
  72.4 2.4 %collective-permute-done.6 = f32[2,24]{1,0:T(2,128)S(1)} collective-permute-done((f32[2,24]{1,0:T(2,128)S(1)}, f32[2,24]{1,0:T(2,128)S(1)}, u32[]{:S(2)}, u32[]{:S(2)}) %collective-permute-start.6) | collective-permute-done | bytes 224 | tf_op jit(solution)/shard_map/ppermute | solution.py:107
  75.6 3.4 %collective-permute-done.7 = f32[2,24]{1,0:T(2,128)S(1)} collective-permute-done((f32[2,24]{1,0:T(2,128)S(1)}, f32[2,24]{1,0:T(2,128)S(1)}, u32[]{:S(2)}, u32[]{:S(2)}) %collective-permute-start.7) | collective-permute-done | bytes 224 | tf_op jit(solution)/shard_map/ppermute | solution.py:107
  79.0 4.8 %fusion.49 = (bf16[24,64,256]{2,1,0:T(8,128)(2,1)S(1)}, f32[24,64,256]{2,1,0:T(8,128)}, f32[24,64,256]{2,1,0:T(8,128)}) fusion(f32[24,64,256]{2,1,0:T(8,128)} %param.27, f32[12,64,256]{2,1,0:T(8,128)} %get-tuple-element.135, f32[12,64,256]{2,1,0:T(8,128)} %get-tuple-element.137, f32[24]{0:T(128)S(1)} %multiply_bitcast_fusion, f32[24,64,256]{2,1,0:T(8,128)} %param.26), kind=kLoop, calls=%fused_computation.79 | loop fusion | flops 2752512 | bytes 8650848 | tf_op jit(solution)/shard_map/convert_element_type | solution.py:116
  84.7 1.3 %copy.28 = bf16[4,8,64,256]{3,2,1,0:T(8,128)(2,1)} copy(bf16[4,8,64,256]{3,1,2,0:T(8,128)(2,1)S(1)} %bitcast.42) | data formatting | bytes 2097152
  86.0 8.1 %all-to-all-start.1 = ((bf16[32,64,256]{2,1,0:T(8,128)(2,1)}), bf16[32,64,256]{2,1,0:T(8,128)(2,1)}, u32[]{:S(2)}, u32[]{:S(2)}) async-start(bf16[32,64,256]{2,1,0:T(8,128)(2,1)} %bitcast.40), calls=%async_computation.1 | async-start | bytes 2097152 | tf_op jit(solution)/shard_map/all_to_all | solution.py:118
  94.1 4.0 %multiply_add_fusion.1 = f32[24,64,256]{2,1,0:T(8,128)} fusion(f32[24,64,256]{2,1,0:T(8,128)} %param.21, bf16[24,64,256]{2,1,0:T(8,128)(2,1)} %copy-done.4, bf16[12,256,256]{2,1,0:T(8,128)(2,1)S(1)} %get-tuple-element.139, bf16[12,256,256]{2,1,0:T(8,128)(2,1)S(1)} %get-tuple-element.138), kind=kOutput, calls=%fused_computation.31 | convolution fusion | flops 204079104 | bytes 7077888 | tf_op jit(solution)/shard_map/kij,klj->kil/dot_general | solution.py:79
  98.1 2.5 %multiply_add_fusion = f32[24,64,256]{2,1,0:T(8,128)} fusion(f32[24,64,256]{2,1,0:T(8,128)S(1)} %copy-done.7, bf16[12,256,256]{2,1,0:T(8,128)(2,1)S(1)} %get-tuple-element.139, bf16[12,256,256]{2,1,0:T(8,128)(2,1)S(1)} %get-tuple-element.138, s32[]{:T(128)S(6)} %select_n.20), kind=kOutput, calls=%fused_computation.30 | convolution fusion | flops 205651968 | bytes 9437188 | tf_op jit(solution)/shard_map/kji,kjl->kil/dot_general | solution.py:82
  100.6 10.5 %all-to-all-done.1 = bf16[32,64,256]{2,1,0:T(8,128)(2,1)} async-done(((bf16[32,64,256]{2,1,0:T(8,128)(2,1)}), bf16[32,64,256]{2,1,0:T(8,128)(2,1)}, u32[]{:S(2)}, u32[]{:S(2)}) %all-to-all-start.1) | async-done | bytes 1048608 | tf_op jit(solution)/shard_map/all_to_all | solution.py:118
  111.2 1.8 %copy.29 = bf16[4,8,64,256]{3,1,2,0:T(8,128)(2,1)S(1)} copy(bf16[4,8,64,256]{3,2,1,0:T(8,128)(2,1)} %bitcast.21) | data formatting | bytes 2097152
  113.4 0.8 slice.42
  (44 shorter events, 6.8 us)
Async XLA Ops:
  5.2 8.8 %copy-start.5 = (s32[384]{0:T(512)S(1)}, s32[384]{0:T(512)}, u32[]{:S(2)}) copy-start(s32[384]{0:T(512)} %param.20) | copy-start | bytes 4612
  5.2 25.6 %all-to-all-start = ((bf16[32,64,256]{2,1,0:T(8,128)(2,1)}), bf16[32,64,256]{2,1,0:T(8,128)(2,1)S(1)}, u32[]{:S(2)}, u32[]{:S(2)}) async-start(bf16[32,64,256]{2,1,0:T(8,128)(2,1)} %bitcast.8), calls=%async_computation | async-start | bytes 2097152 | tf_op jit(solution)/shard_map/all_to_all | solution.py:67
  32.4 13.2 %collective-permute-start.1 = (bf16[12,64,256]{2,1,0:T(8,128)(2,1)S(1)}, bf16[12,64,256]{2,1,0:T(8,128)(2,1)S(1)}, u32[]{:S(2)}, u32[]{:S(2)}) collective-permute-start(bf16[12,64,256]{2,1,0:T(8,128)(2,1)S(1)} %get-tuple-element.126), channel_id=1, source_target_pairs={{0,1},{1,2},{2,3},{3,0},{4,5},{5,6},{6,7},{7,4},{8,9},{9,10},{10,1... | collective-permute-start | bytes 1179656 | tf_op jit(solution)/shard_map/ppermute | solution.py:17
  34.2 17.5 %copy-start.4 = (bf16[24,64,256]{2,1,0:T(8,128)(2,1)}, bf16[24,64,256]{2,1,0:T(8,128)(2,1)S(1)}, u32[]{:S(2)}) copy-start(bf16[24,64,256]{2,1,0:T(8,128)(2,1)S(1)} %get-tuple-element.129) | copy-start | bytes 2359300
  34.2 12.1 %collective-permute-start.3 = (bf16[12,64,256]{2,1,0:T(8,128)(2,1)S(1)}, bf16[12,64,256]{2,1,0:T(8,128)(2,1)S(1)}, u32[]{:S(2)}, u32[]{:S(2)}) collective-permute-start(bf16[12,64,256]{2,1,0:T(8,128)(2,1)S(1)} %get-tuple-element.128), channel_id=1, source_target_pairs={{0,3},{1,0},{2,1},{3,2},{4,7},{5,4},{6,5},{7,6},{8,11},{9,8},{10,9... | collective-permute-start | bytes 1179656 | tf_op jit(solution)/shard_map/ppermute | solution.py:18
  36.4 17.0 %collective-permute-start = (bf16[12,64,256]{2,1,0:T(8,128)(2,1)S(1)}, bf16[12,64,256]{2,1,0:T(8,128)(2,1)S(1)}, u32[]{:S(2)}, u32[]{:S(2)}) collective-permute-start(bf16[12,64,256]{2,1,0:T(8,128)(2,1)S(1)} %get-tuple-element.126), channel_id=1, source_target_pairs={{0,3},{1,0},{2,1},{3,2},{4,7},{5,4},{6,5},{7,6},{8,11},{9,8},{10,9... | collective-permute-start | bytes 1179656 | tf_op jit(solution)/shard_map/ppermute | solution.py:18
  45.6 11.3 %collective-permute-start.2 = (bf16[12,64,256]{2,1,0:T(8,128)(2,1)S(1)}, bf16[12,64,256]{2,1,0:T(8,128)(2,1)}, u32[]{:S(2)}, u32[]{:S(2)}) collective-permute-start(bf16[12,64,256]{2,1,0:T(8,128)(2,1)S(1)} %collective-permute-done.1), channel_id=1, source_target_pairs={{0,1},{1,2},{2,3},{3,0},{4,5},{5,6},{6,7},{7,4},{8,9},{9,10},{10,1... | collective-permute-start | bytes 1179656 | tf_op jit(solution)/shard_map/ppermute | solution.py:20
  45.6 19.7 %collective-permute-start.5 = (bf16[12,64,256]{2,1,0:T(8,128)(2,1)S(1)}, bf16[12,64,256]{2,1,0:T(8,128)(2,1)}, u32[]{:S(2)}, u32[]{:S(2)}) collective-permute-start(bf16[12,64,256]{2,1,0:T(8,128)(2,1)S(1)} %get-tuple-element.128), channel_id=1, source_target_pairs={{0,1},{1,2},{2,3},{3,0},{4,5},{5,6},{6,7},{7,4},{8,9},{9,10},{10,1... | collective-permute-start | bytes 1179656 | tf_op jit(solution)/shard_map/ppermute | solution.py:17
  46.3 19.0 %collective-permute-start.4 = (bf16[12,64,256]{2,1,0:T(8,128)(2,1)S(1)}, bf16[12,64,256]{2,1,0:T(8,128)(2,1)}, u32[]{:S(2)}, u32[]{:S(2)}) collective-permute-start(bf16[12,64,256]{2,1,0:T(8,128)(2,1)S(1)} %collective-permute-done.3), channel_id=1, source_target_pairs={{0,3},{1,0},{2,1},{3,2},{4,7},{5,4},{6,5},{7,6},{8,11},{9,8},{10,9... | collective-permute-start | bytes 1179656 | tf_op jit(solution)/shard_map/ppermute | solution.py:22
  65.4 0.7 copy-start
  67.5 4.7 %copy-start.6 = (f32[12]{0:T(128)S(1)}, f32[12]{0:T(128)}, u32[]{:S(2)}) copy-start(f32[12]{0:T(128)} %get-tuple-element.136) | copy-start | bytes 148
  72.3 2.5 %collective-permute-start.6 = (f32[2,24]{1,0:T(2,128)S(1)}, f32[2,24]{1,0:T(2,128)S(1)}, u32[]{:S(2)}, u32[]{:S(2)}) collective-permute-start(f32[2,24]{1,0:T(2,128)S(1)} %pad_maximum_fusion.15), channel_id=1, source_target_pairs={{0,1},{1,0},{2,3},{3,2},{4,5},{5,4},{6,7},{7,6},{8,9},{9,8},{10,11... | collective-permute-start | bytes 584 | tf_op jit(solution)/shard_map/ppermute | solution.py:107
  74.8 4.2 %collective-permute-start.7 = (f32[2,24]{1,0:T(2,128)S(1)}, f32[2,24]{1,0:T(2,128)S(1)}, u32[]{:S(2)}, u32[]{:S(2)}) collective-permute-start(f32[2,24]{1,0:T(2,128)S(1)} %fusion.48), channel_id=1, source_target_pairs={{0,2},{1,3},{2,0},{3,1},{4,6},{5,7},{6,4},{7,5},{8,10},{9,11},{10,... | collective-permute-start | bytes 584 | tf_op jit(solution)/shard_map/ppermute | solution.py:107
  86.0 25.1 %all-to-all-start.1 = ((bf16[32,64,256]{2,1,0:T(8,128)(2,1)}), bf16[32,64,256]{2,1,0:T(8,128)(2,1)}, u32[]{:S(2)}, u32[]{:S(2)}) async-start(bf16[32,64,256]{2,1,0:T(8,128)(2,1)} %bitcast.40), calls=%async_computation.1 | async-start | bytes 2097152 | tf_op jit(solution)/shard_map/all_to_all | solution.py:118
  94.1 4.0 %copy-start.7 = (f32[24,64,256]{2,1,0:T(8,128)S(1)}, f32[24,64,256]{2,1,0:T(8,128)}, u32[]{:S(2)}) copy-start(f32[24,64,256]{2,1,0:T(8,128)} %param.22) | copy-start | bytes 4718596

commit v5 on v2

--- a/solution.py
+++ b/solution.py
@@ -70,10 +70,9 @@
     first_half = pick(arrived, src_of_slot[:half], slot_filled[:half])
     second_half = pick(arrived, src_of_slot[half:], slot_filled[half:])
     grad_piece = jnp.concatenate([first_half, second_half], 0)
-    whole_halves = [
-        gather_rows(first_half, splits, tensor_index),
-        gather_rows(second_half, splits, tensor_index),
-    ]
+    whole_halves = []
+    for piece in (first_half, second_half):
+        whole_halves.append(gather_rows(piece, splits, tensor_index))
     grad_whole = jnp.concatenate(whole_halves, 0)
     f32 = jnp.float32
     grad_cols = lax.dynamic_slice_in_dim(grad_whole, row_start, rows_dev, 2)

time: 115 us -> 115 us (level)
  no operation moved by 1% of the time
where the time goes in v5:
time: 115 us
  waiting for transfers between devices  43.1 us (37%)
  starting transfers between devices  32.7 us (28%)
  matrix products  15.5 us (13%)
  other arithmetic  12.5 us (11%)
  local copies, waits for them, and re-layouts  9.96 us (9%)
    all_to_all x1, waiting for transfers between devices, on_device(): lax.all_to_all(outgoing, 'shard', split_axis=0, concat_axis=0, tiled=True)  16.1 us
    all_to_all x1, waiting for transfers between devices, on_device(): lax.all_to_all(returning, 'shard', split_axis=0, concat_axis=0, tiled=True)  10.4 us
    ppermute x2, waiting for transfers between devices, gather_rows(): lax.ppermute(from_left[:cut], 'tensor', right)  10.2 us
    dot_general x2, matrix products, on_device(): jnp.einsum('kij,kjl->kil', mixed, root_right[lo:hi], precision=three_pass...  8.81 us
    all_to_all x1, starting transfers between devices, on_device(): lax.all_to_all(outgoing, 'shard', split_axis=0, concat_axis=0, tiled=True)  8.58 us
    all_to_all x1, starting transfers between devices, on_device(): lax.all_to_all(returning, 'shard', split_axis=0, concat_axis=0, tiled=True)  8.37 us
    ppermute x2, starting transfers between devices, gather_rows(): lax.ppermute(from_right[cut:], 'tensor', left)  4.8 us
    ppermute x2, starting transfers between devices, on_device(): lax.ppermute(sums, 'tensor', [(i, i ^ step) for i in range(splits)])  4.56 us
  transfers between devices with their start and end apart: 12, of which 7 were waited for; matrix products, arithmetic and copies ran while one was open for 13% of the time, Pallas kernels for 0%

profile of v5, /device:TPU:1, one launch (start us, length us, event | category | flops | bytes accessed | tf_op | source)
XLA Modules:
  0.0 114.6 jit_solution(16001413530367815452)
XLA Ops:
  0.7 0.8 reshape.53
  2.2 0.8 eq.46
  4.5 1.1 broadcast_select_fusion
  5.6 8.6 %all-to-all-start = ((bf16[32,64,256]{2,1,0:T(8,128)(2,1)}), bf16[32,64,256]{2,1,0:T(8,128)(2,1)S(1)}, u32[]{:S(2)}, u32[]{:S(2)}) async-start(bf16[32,64,256]{2,1,0:T(8,128)(2,1)} %broadcast_select_fusion), calls=%async_computation | async-start | bytes 2097152 | tf_op jit(solution)/shard_map/all_to_all | solution.py:68
  15.0 16.1 %all-to-all-done = bf16[32,64,256]{2,1,0:T(8,128)(2,1)S(1)} async-done(((bf16[32,64,256]{2,1,0:T(8,128)(2,1)}), bf16[32,64,256]{2,1,0:T(8,128)(2,1)S(1)}, u32[]{:S(2)}, u32[]{:S(2)}) %all-to-all-start) | async-done | bytes 1048608 | tf_op jit(solution)/shard_map/all_to_all | solution.py:68
  31.8 1.7 %collective-permute-start.5 = (bf16[8,64,256]{2,1,0:T(8,128)(2,1)S(1)}, bf16[8,64,256]{2,1,0:T(8,128)(2,1)S(1)}, u32[]{:S(2)}, u32[]{:S(2)}) collective-permute-start(bf16[8,64,256]{2,1,0:T(8,128)(2,1)S(1)} %broadcast_select_fusion.2), channel_id=1, source_target_pairs={{0,1},{1,2},{2,3},{3,0},{4,5},{5,6},{6,7},{7,4},{8,9},{9,10},{10,1... | collective-permute-start | bytes 786440 | tf_op jit(solution)/shard_map/ppermute | solution.py:17
  33.5 2.2 %collective-permute-start.4 = (bf16[8,64,256]{2,1,0:T(8,128)(2,1)S(1)}, bf16[8,64,256]{2,1,0:T(8,128)(2,1)S(1)}, u32[]{:S(2)}, u32[]{:S(2)}) collective-permute-start(bf16[8,64,256]{2,1,0:T(8,128)(2,1)S(1)} %broadcast_select_fusion.2), channel_id=1, source_target_pairs={{0,3},{1,0},{2,1},{3,2},{4,7},{5,4},{6,5},{7,6},{8,11},{9,8},{10,9... | collective-permute-start | bytes 786440 | tf_op jit(solution)/shard_map/ppermute | solution.py:18
  36.4 1.5 %collective-permute-start = (bf16[16,64,256]{2,1,0:T(8,128)(2,1)S(1)}, bf16[16,64,256]{2,1,0:T(8,128)(2,1)S(1)}, u32[]{:S(2)}, u32[]{:S(2)}) collective-permute-start(bf16[16,64,256]{2,1,0:T(8,128)(2,1)S(1)} %broadcast_select_fusion.1), channel_id=1, source_target_pairs={{0,3},{1,0},{2,1},{3,2},{4,7},{5,4},{6,5},{7,6},{8,11},{9,8},{10,9... | collective-permute-start | bytes 1572872 | tf_op jit(solution)/shard_map/ppermute | solution.py:18
  37.9 4.2 %collective-permute-done.5 = bf16[8,64,256]{2,1,0:T(8,128)(2,1)S(1)} collective-permute-done((bf16[8,64,256]{2,1,0:T(8,128)(2,1)S(1)}, bf16[8,64,256]{2,1,0:T(8,128)(2,1)S(1)}, u32[]{:S(2)}, u32[]{:S(2)}) %collective-permute-start.5) | collective-permute-done | bytes 262176 | tf_op jit(solution)/shard_map/ppermute | solution.py:17
  42.3 2.7 %collective-permute-start.7 = (bf16[4,64,256]{2,1,0:T(8,128)(2,1)S(1)}, bf16[4,64,256]{2,1,0:T(8,128)(2,1)S(1)}, u32[]{:S(2)}, u32[]{:S(2)}) collective-permute-start(bf16[4,64,256]{2,1,0:T(8,128)(2,1)S(1)} %slice.69), channel_id=1, source_target_pairs={{0,3},{1,0},{2,1},{3,2},{4,7},{5,4},{6,5},{7,6},{8,11},{9,8},{10,9... | collective-permute-start | bytes 393224 | tf_op jit(solution)/shard_map/ppermute | solution.py:23
  45.0 2.0 %fusion.11 = (f32[24]{0:T(128)S(1)}, f32[24,64,256]{2,1,0:T(8,128)}) fusion(bf16[8,64,256]{2,1,0:T(8,128)(2,1)S(1)} %broadcast_select_fusion.2, bf16[16,64,256]{2,1,0:T(8,128)(2,1)S(1)} %broadcast_select_fusion.1, f32[24,64,256]{2,1,0:T(8,128)S(1)} %copy-done.3), kind=kLoop, calls=%fused_computation.32 | loop fusion | flops 3932136 | bytes 3932256 | tf_op jit(solution)/shard_map/reduce_sum | solution.py:104
  47.0 8.8 %collective-permute-done.6 = bf16[4,64,256]{2,1,0:T(8,128)(2,1)S(1)} collective-permute-done((bf16[4,64,256]{2,1,0:T(8,128)(2,1)S(1)}, bf16[4,64,256]{2,1,0:T(8,128)(2,1)S(1)}, u32[]{:S(2)}, u32[]{:S(2)}) %collective-permute-start.6) | collective-permute-done | bytes 131104 | tf_op jit(solution)/shard_map/ppermute | solution.py:22
  55.8 1.1 conditional.3
  55.9 1.0 pad_maximum_fusion.4
  56.9 0.9 collective-permute-start.2
  58.5 2.1 %collective-permute-start.3 = (bf16[8,64,256]{2,1,0:T(8,128)(2,1)}, bf16[8,64,256]{2,1,0:T(8,128)(2,1)S(1)}, u32[]{:S(2)}, u32[]{:S(2)}) collective-permute-start(bf16[8,64,256]{2,1,0:T(8,128)(2,1)} %slice.67), channel_id=1, source_target_pairs={{0,3},{1,0},{2,1},{3,2},{4,7},{5,4},{6,5},{7,6},{8,11},{9,8},{10,9... | collective-permute-start | bytes 786440 | tf_op jit(solution)/shard_map/ppermute | solution.py:23
  60.6 3.3 %multiply_reduce_fusion.1 = (f32[8]{0:T(128)S(1)}, f32[8,64,256]{2,1,0:T(8,128)S(1)}) fusion(f32[24,256,256]{2,1,0:T(8,128)} %param.24, bf16[8,256,256]{2,1,0:T(8,128)(2,1)} %get-tuple-element.134, f32[24,64,256]{2,1,0:T(8,128)} %param.23), kind=kOutput, calls=%fused_computation.39 | convolution fusion | flops 402915328 | bytes 4194336 | tf_op jit(solution)/shard_map/kij,kjl->kil/dot_general | solution.py:97
  64.0 1.4 %collective-permute-done.2 = bf16[8,64,256]{2,1,0:T(8,128)(2,1)S(1)} collective-permute-done((bf16[8,64,256]{2,1,0:T(8,128)(2,1)S(1)}, bf16[8,64,256]{2,1,0:T(8,128)(2,1)S(1)}, u32[]{:S(2)}, u32[]{:S(2)}) %collective-permute-start.2) | collective-permute-done | bytes 262176 | tf_op jit(solution)/shard_map/ppermute | solution.py:22
  65.5 1.5 %conditional.2 = (bf16[16,256,256]{2,1,0:T(8,128)(2,1)}) conditional(s32[]{:T(128)} %clamp.4, (bf16[16,64,256]{2,1,0:T(8,128)(2,1)S(1)}, bf16[16,64,256]{2,1,0:T(8,128)(2,1)S(1)}, bf16[16,64,256]{2,1,0:T(8,128)(2,1)S(1)}, bf16[16,64,256]{2,1,0:T(8,128)(2,1)S(1)}) %tuple.38, (bf16[16,64,256]{2,1,0:T(8,128)(2,1)S(1)}, ...), branch_computations={%region_5.6_spmd, %region_6.7_spmd, %region_7.8_spmd, %region_8.9_... | conditional | flops 8388608 | bytes 4194312 | solution.py:32
  65.5 1.5 %pad_maximum_fusion = bf16[16,256,256]{2,1,0:T(8,128)(2,1)} fusion(bf16[16,64,256]{2,1,0:T(8,128)(2,1)S(1)} %get-tuple-element.72, bf16[16,64,256]{2,1,0:T(8,128)(2,1)S(1)} %get-tuple-element.71, bf16[16,64,256]{2,1,0:T(8,128)(2,1)S(1)} %get-tuple-element.70, bf16[16,64,256]{2,1,0:T(8,128)(2,1)S(1)} %get-tuple-element.64), kind=kLoop, calls=%fused_computation.5 | loop fusion | flops 8388608 | bytes 4194304 | tf_op jit(solution)/shard_map/cond/branch_0_fun/concatenate | solution.py:30
  67.0 5.5 %multiply_reduce_fusion = (f32[16]{0:T(128)S(1)}, f32[16,64,256]{2,1,0:T(8,128)S(1)}) fusion(f32[24,256,256]{2,1,0:T(8,128)} %param.24, bf16[16,256,256]{2,1,0:T(8,128)(2,1)} %get-tuple-element.133, f32[24,64,256]{2,1,0:T(8,128)} %param.23), kind=kOutput, calls=%fused_computation.35 | convolution fusion | flops 805830656 | bytes 8388672 | tf_op jit(solution)/shard_map/kij,kjl->kil/dot_general | solution.py:97
  72.5 1.3 %collective-permute-start.8 = (f32[2,24]{1,0:T(2,128)S(1)}, f32[2,24]{1,0:T(2,128)S(1)}, u32[]{:S(2)}, u32[]{:S(2)}) collective-permute-start(f32[2,24]{1,0:T(2,128)S(1)} %pad_maximum_fusion.17), channel_id=1, source_target_pairs={{0,1},{1,0},{2,3},{3,2},{4,5},{5,4},{6,7},{7,6},{8,9},{9,8},{10,11... | collective-permute-start | bytes 584 | tf_op jit(solution)/shard_map/ppermute | solution.py:108
  73.8 1.2 %collective-permute-done.8 = f32[2,24]{1,0:T(2,128)S(1)} collective-permute-done((f32[2,24]{1,0:T(2,128)S(1)}, f32[2,24]{1,0:T(2,128)S(1)}, u32[]{:S(2)}, u32[]{:S(2)}) %collective-permute-start.8) | collective-permute-done | bytes 224 | tf_op jit(solution)/shard_map/ppermute | solution.py:108
  75.0 3.3 %collective-permute-start.9 = (f32[2,24]{1,0:T(2,128)S(1)}, f32[2,24]{1,0:T(2,128)S(1)}, u32[]{:S(2)}, u32[]{:S(2)}) collective-permute-start(f32[2,24]{1,0:T(2,128)S(1)} %fusion.30), channel_id=1, source_target_pairs={{0,2},{1,3},{2,0},{3,1},{4,6},{5,7},{6,4},{7,5},{8,10},{9,11},{10,... | collective-permute-start | bytes 584 | tf_op jit(solution)/shard_map/ppermute | solution.py:108
  78.3 1.0 collective-permute-done.9
  79.3 4.5 %fusion.31 = (bf16[24,64,256]{2,1,0:T(8,128)(2,1)}, f32[24,64,256]{2,1,0:T(8,128)}, f32[24,64,256]{2,1,0:T(8,128)}) fusion(f32[24,64,256]{2,1,0:T(8,128)} %param.27, f32[8,64,256]{2,1,0:T(8,128)S(1)} %get-tuple-element.126, f32[16,64,256]{2,1,0:T(8,128)S(1)} %get-tuple-element.128, f32[24]{0:T(128)S(1)} %multiply_bitcast_fusion, f32[24,64,256]{2,1,0:T(8,128)} %param.26), kind=kLoop, calls=%fused_computation.71 | loop fusion | flops 2752512 | bytes 8650848 | tf_op jit(solution)/shard_map/convert_element_type | solution.py:117
  83.8 2.9 %gather_fusion.3 = bf16[32,64,256]{2,1,0:T(8,128)(2,1)} fusion(bf16[24,64,256]{2,1,0:T(8,128)(2,1)} %get-tuple-element.120, s32[1024]{0:T(1024)S(1)} %get-tuple-element.129), kind=kCustom, calls=%fused_computation.3 | custom fusion | bytes 2097280 | tf_op jit(solution)/shard_map/jit(_take)/gather | solution.py:118
  86.7 8.4 %all-to-all-start.1 = ((bf16[32,64,256]{2,1,0:T(8,128)(2,1)}), bf16[32,64,256]{2,1,0:T(8,128)(2,1)}, u32[]{:S(2)}, u32[]{:S(2)}) async-start(bf16[32,64,256]{2,1,0:T(8,128)(2,1)} %gather_fusion.3), calls=%async_computation.1 | async-start | bytes 2097152 | tf_op jit(solution)/shard_map/all_to_all | solution.py:119
  95.1 4.1 %multiply_add_fusion.1 = f32[24,64,256]{2,1,0:T(8,128)} fusion(f32[24,64,256]{2,1,0:T(8,128)} %param.21, bf16[8,256,256]{2,1,0:T(8,128)(2,1)} %get-tuple-element.134, bf16[16,256,256]{2,1,0:T(8,128)(2,1)S(1)} %copy-done.1, bf16[8,64,256]{2,1,0:T(8,128)(2,1)S(1)} %broadcast_select_fusion.2, bf16[16,64,256]{2,1,0:T(8,128)(2,1)S(1)} %broadcast_select_fusion.1), kind=kOutput, calls=%fused_computation.31 | convolution fusion | flops 204472320 | bytes 7077888 | tf_op jit(solution)/shard_map/kij,klj->kil/dot_general | solution.py:79
  99.2 2.6 %multiply_add_fusion = f32[24,64,256]{2,1,0:T(8,128)} fusion(f32[24,64,256]{2,1,0:T(8,128)S(1)} %copy-done.4, bf16[8,256,256]{2,1,0:T(8,128)(2,1)S(1)} %copy-done.2, bf16[16,256,256]{2,1,0:T(8,128)(2,1)S(1)} %copy-done.1, s32[]{:T(128)S(6)} %select_n.35), kind=kOutput, calls=%fused_computation.30 | convolution fusion | flops 205651968 | bytes 9437188 | tf_op jit(solution)/shard_map/kji,kjl->kil/dot_general | solution.py:82
  101.7 10.4 %all-to-all-done.1 = bf16[32,64,256]{2,1,0:T(8,128)(2,1)} async-done(((bf16[32,64,256]{2,1,0:T(8,128)(2,1)}), bf16[32,64,256]{2,1,0:T(8,128)(2,1)}, u32[]{:S(2)}, u32[]{:S(2)}) %all-to-all-start.1) | async-done | bytes 1048608 | tf_op jit(solution)/shard_map/all_to_all | solution.py:119
  112.1 2.6 %gather_fusion.4 = bf16[12,64,256]{2,1,0:T(8,128)(2,1)} fusion(bf16[32,64,256]{2,1,0:T(8,128)(2,1)} %all-to-all-done.1, s32[1024]{0:T(1024)S(1)} %pad_clamp_fusion), kind=kCustom, calls=%fused_computation.4 | custom fusion | bytes 786480 | tf_op jit(solution)/shard_map/jit(_take)/gather | solution.py:120
  (49 shorter events, 5.5 us)
Async XLA Ops:
  0.6 3.2 %copy-start = (bf16[12,64,256]{2,1,0:T(8,128)(2,1)S(1)}, bf16[12,64,256]{2,1,0:T(8,128)(2,1)}, u32[]{:S(2)}) copy-start(bf16[12,64,256]{2,1,0:T(8,128)(2,1)} %param.18) | copy-start | bytes 1179652
  5.6 25.5 %all-to-all-start = ((bf16[32,64,256]{2,1,0:T(8,128)(2,1)}), bf16[32,64,256]{2,1,0:T(8,128)(2,1)S(1)}, u32[]{:S(2)}, u32[]{:S(2)}) async-start(bf16[32,64,256]{2,1,0:T(8,128)(2,1)} %broadcast_select_fusion), calls=%async_computation | async-start | bytes 2097152 | tf_op jit(solution)/shard_map/all_to_all | solution.py:68
  31.8 10.4 %collective-permute-start.5 = (bf16[8,64,256]{2,1,0:T(8,128)(2,1)S(1)}, bf16[8,64,256]{2,1,0:T(8,128)(2,1)S(1)}, u32[]{:S(2)}, u32[]{:S(2)}) collective-permute-start(bf16[8,64,256]{2,1,0:T(8,128)(2,1)S(1)} %broadcast_select_fusion.2), channel_id=1, source_target_pairs={{0,1},{1,2},{2,3},{3,0},{4,5},{5,6},{6,7},{7,4},{8,9},{9,10},{10,1... | collective-permute-start | bytes 786440 | tf_op jit(solution)/shard_map/ppermute | solution.py:17
  33.5 8.8 %collective-permute-start.4 = (bf16[8,64,256]{2,1,0:T(8,128)(2,1)S(1)}, bf16[8,64,256]{2,1,0:T(8,128)(2,1)S(1)}, u32[]{:S(2)}, u32[]{:S(2)}) collective-permute-start(bf16[8,64,256]{2,1,0:T(8,128)(2,1)S(1)} %broadcast_select_fusion.2), channel_id=1, source_target_pairs={{0,3},{1,0},{2,1},{3,2},{4,7},{5,4},{6,5},{7,6},{8,11},{9,8},{10,9... | collective-permute-start | bytes 786440 | tf_op jit(solution)/shard_map/ppermute | solution.py:18
  36.3 8.7 %copy-start.3 = (f32[24,64,256]{2,1,0:T(8,128)S(1)}, f32[24,64,256]{2,1,0:T(8,128)}, u32[]{:S(2)}) copy-start(f32[24,64,256]{2,1,0:T(8,128)} %param.25) | copy-start | bytes 4718596
  36.4 21.4 %collective-permute-start = (bf16[16,64,256]{2,1,0:T(8,128)(2,1)S(1)}, bf16[16,64,256]{2,1,0:T(8,128)(2,1)S(1)}, u32[]{:S(2)}, u32[]{:S(2)}) collective-permute-start(bf16[16,64,256]{2,1,0:T(8,128)(2,1)S(1)} %broadcast_select_fusion.1), channel_id=1, source_target_pairs={{0,3},{1,0},{2,1},{3,2},{4,7},{5,4},{6,5},{7,6},{8,11},{9,8},{10,9... | collective-permute-start | bytes 1572872 | tf_op jit(solution)/shard_map/ppermute | solution.py:18
  37.8 19.1 %collective-permute-start.1 = (bf16[16,64,256]{2,1,0:T(8,128)(2,1)S(1)}, bf16[16,64,256]{2,1,0:T(8,128)(2,1)S(1)}, u32[]{:S(2)}, u32[]{:S(2)}) collective-permute-start(bf16[16,64,256]{2,1,0:T(8,128)(2,1)S(1)} %broadcast_select_fusion.1), channel_id=1, source_target_pairs={{0,1},{1,2},{2,3},{3,0},{4,5},{5,6},{6,7},{7,4},{8,9},{9,10},{10,1... | collective-permute-start | bytes 1572872 | tf_op jit(solution)/shard_map/ppermute | solution.py:17
  42.2 13.6 %collective-permute-start.6 = (bf16[4,64,256]{2,1,0:T(8,128)(2,1)S(1)}, bf16[4,64,256]{2,1,0:T(8,128)(2,1)S(1)}, u32[]{:S(2)}, u32[]{:S(2)}) collective-permute-start(bf16[4,64,256]{2,1,0:T(8,128)(2,1)S(1)} %slice.68), channel_id=1, source_target_pairs={{0,1},{1,2},{2,3},{3,0},{4,5},{5,6},{6,7},{7,4},{8,9},{9,10},{10,1... | collective-permute-start | bytes 393224 | tf_op jit(solution)/shard_map/ppermute | solution.py:22
  42.3 13.5 %collective-permute-start.7 = (bf16[4,64,256]{2,1,0:T(8,128)(2,1)S(1)}, bf16[4,64,256]{2,1,0:T(8,128)(2,1)S(1)}, u32[]{:S(2)}, u32[]{:S(2)}) collective-permute-start(bf16[4,64,256]{2,1,0:T(8,128)(2,1)S(1)} %slice.69), channel_id=1, source_target_pairs={{0,3},{1,0},{2,1},{3,2},{4,7},{5,4},{6,5},{7,6},{8,11},{9,8},{10,9... | collective-permute-start | bytes 393224 | tf_op jit(solution)/shard_map/ppermute | solution.py:23
  56.9 8.4 %collective-permute-start.2 = (bf16[8,64,256]{2,1,0:T(8,128)(2,1)S(1)}, bf16[8,64,256]{2,1,0:T(8,128)(2,1)S(1)}, u32[]{:S(2)}, u32[]{:S(2)}) collective-permute-start(bf16[8,64,256]{2,1,0:T(8,128)(2,1)S(1)} %slice.66), channel_id=1, source_target_pairs={{0,1},{1,2},{2,3},{3,0},{4,5},{5,6},{6,7},{7,4},{8,9},{9,10},{10,1... | collective-permute-start | bytes 786440 | tf_op jit(solution)/shard_map/ppermute | solution.py:22
  58.5 6.9 %collective-permute-start.3 = (bf16[8,64,256]{2,1,0:T(8,128)(2,1)}, bf16[8,64,256]{2,1,0:T(8,128)(2,1)S(1)}, u32[]{:S(2)}, u32[]{:S(2)}) collective-permute-start(bf16[8,64,256]{2,1,0:T(8,128)(2,1)} %slice.67), channel_id=1, source_target_pairs={{0,3},{1,0},{2,1},{3,2},{4,7},{5,4},{6,5},{7,6},{8,11},{9,8},{10,9... | collective-permute-start | bytes 786440 | tf_op jit(solution)/shard_map/ppermute | solution.py:23
  72.5 2.5 %collective-permute-start.8 = (f32[2,24]{1,0:T(2,128)S(1)}, f32[2,24]{1,0:T(2,128)S(1)}, u32[]{:S(2)}, u32[]{:S(2)}) collective-permute-start(f32[2,24]{1,0:T(2,128)S(1)} %pad_maximum_fusion.17), channel_id=1, source_target_pairs={{0,1},{1,0},{2,3},{3,2},{4,5},{5,4},{6,7},{7,6},{8,9},{9,8},{10,11... | collective-permute-start | bytes 584 | tf_op jit(solution)/shard_map/ppermute | solution.py:108
  75.0 4.2 %collective-permute-start.9 = (f32[2,24]{1,0:T(2,128)S(1)}, f32[2,24]{1,0:T(2,128)S(1)}, u32[]{:S(2)}, u32[]{:S(2)}) collective-permute-start(f32[2,24]{1,0:T(2,128)S(1)} %fusion.30), channel_id=1, source_target_pairs={{0,2},{1,3},{2,0},{3,1},{4,6},{5,7},{6,4},{7,5},{8,10},{9,11},{10,... | collective-permute-start | bytes 584 | tf_op jit(solution)/shard_map/ppermute | solution.py:108
  83.8 11.3 %copy-start.1 = (bf16[16,256,256]{2,1,0:T(8,128)(2,1)S(1)}, bf16[16,256,256]{2,1,0:T(8,128)(2,1)}, u32[]{:S(2)}) copy-start(bf16[16,256,256]{2,1,0:T(8,128)(2,1)} %get-tuple-element.133) | copy-start | bytes 6291460
  86.7 25.4 %all-to-all-start.1 = ((bf16[32,64,256]{2,1,0:T(8,128)(2,1)}), bf16[32,64,256]{2,1,0:T(8,128)(2,1)}, u32[]{:S(2)}, u32[]{:S(2)}) async-start(bf16[32,64,256]{2,1,0:T(8,128)(2,1)} %gather_fusion.3), calls=%async_computation.1 | async-start | bytes 2097152 | tf_op jit(solution)/shard_map/all_to_all | solution.py:119
  95.1 4.1 %copy-start.2 = (bf16[8,256,256]{2,1,0:T(8,128)(2,1)S(1)}, bf16[8,256,256]{2,1,0:T(8,128)(2,1)}, u32[]{:S(2)}) copy-start(bf16[8,256,256]{2,1,0:T(8,128)(2,1)} %get-tuple-element.134) | copy-start | bytes 3145732
  95.1 4.1 %copy-start.4 = (f32[24,64,256]{2,1,0:T(8,128)S(1)}, f32[24,64,256]{2,1,0:T(8,128)}, u32[]{:S(2)}) copy-start(f32[24,64,256]{2,1,0:T(8,128)} %param.22) | copy-start | bytes 4718596

commit v6 on v0

--- a/solution.py
+++ b/solution.py
@@ -44,19 +44,18 @@
     blocks_group = grads.shape[0]
     shard_index = lax.axis_index("shard")
     tensor_index = lax.axis_index("tensor")
+    local_owner = lax.dynamic_slice_in_dim(owner, shard_index * blocks_group, blocks_group)
+    slot_ids = jnp.arange(slots_dev, dtype=jnp.int32)
+    group_ids = jnp.arange(groups, dtype=jnp.int32)
     owner_grid = owner.reshape(groups, blocks_group)
     slot_grid = slot.reshape(groups, blocks_group)
-    local_owner = lax.dynamic_index_in_dim(owner_grid, shard_index, 0, keepdims=False)
     hit_mask = owner_grid == shard_index
-    slot_ids = jnp.arange(slots_dev, dtype=jnp.int32)
-    group_ids = jnp.arange(groups, dtype=jnp.int32)
     slot_match = jnp.any(
         (slot_grid[None, :, :] == slot_ids[:, None, None]) & hit_mask[None, :, :], axis=2
     )
     src_of_slot = jnp.argmax(slot_match, axis=1).astype(jnp.int32)
     slot_filled = jnp.any(slot_match, axis=1)
     slot_of_src = jnp.argmax(slot_match, axis=0).astype(jnp.int32)
-    src_sent = jnp.any(slot_match, axis=0)
     dest_match = local_owner[None, :] == group_ids[:, None]
     block_of_dest = jnp.argmax(dest_match, axis=1).astype(jnp.int32)
     dest_used = jnp.any(dest_match, axis=1)
@@ -112,9 +111,9 @@
     velocity_new = beta_mom * momentum + (1.0 - beta_mom) * scale_ratio[:, None, None] * precond
     weight_new = master - learn_rate * velocity_new
     weight_half = weight_new.astype(jnp.bfloat16)
-    returning = pick(weight_half, slot_of_src, src_sent)
+    returning = jnp.take(weight_half, slot_of_src, axis=0, mode="clip")
     back_rows = lax.all_to_all(returning, "shard", split_axis=0, concat_axis=0, tiled=True)
-    weights_local = jnp.take(back_rows, local_owner, axis=0)
+    weights_local = jnp.take(back_rows, local_owner, axis=0, mode="clip")
     return (left_new, right_new, second_new, velocity_new, weight_new, weights_local)
 
 

time: 113 us -> 110 us (0.973)
  other arithmetic: 19.1 us -> 13.9 us
  starting transfers between devices: 25.7 us -> 26.9 us
    ppermute x2, waiting for transfers between devices: 1.23 us -> 8.89 us  [gather_rows(): from_right = lax.ppermute(piece, 'tensor', left)]
    ppermute x2, waiting for transfers between devices: 9.43 us -> 4.46 us  [gather_rows(): from_left = lax.ppermute(piece, 'tensor', right)]
    select_n x4 -> x3, other arithmetic: 3.7 us -> 1.3 us  [pick(): return jnp.where(valid[:, None, None], taken, jnp.zeros((), source.dtype))]
    gather x1 -> x2, local copies, waits for them, and re-layouts: 1.79 us -> 4.16 us  [the longest x1 2.55 us: on_device(): weights_local = jnp.take(back_rows, local_owner, axis=0, mode='clip')]
    ppermute x2, starting transfers between devices: 2.4 us -> 0.15 us  [gather_rows(): from_left = lax.ppermute(piece, 'tensor', right)]
    gather x4 -> x3, local copies, waits for them, and re-layouts: 3.65 us -> 1.75 us  [pick(): taken = jnp.take(source, index, axis=0, mode='clip')]
    ppermute x2, starting transfers between devices: 0.27 us -> 1.88 us  [on_device(): lax.ppermute(sums, 'tensor', [(i, i ^ step) for i in range(splits)])]
    ppermute x1, waiting for transfers between devices: 2.88 us -> 1.39 us  [gather_rows(): far = lax.ppermute(from_left, 'tensor', right)]
  transfers between devices with their start and end apart: 10 -> 10, of which waited for: 8 -> 9; matrix products, arithmetic and copies ran while one was open for 18% -> 17% of each run, Pallas kernels for 0% -> 0%
where the time goes in v6:
time: 110 us
  waiting for transfers between devices  44.6 us (41%)
  starting transfers between devices  26.9 us (24%)
  matrix products  16.4 us (15%)
  other arithmetic  13.9 us (13%)
  local copies, waits for them, and re-layouts  7.28 us (7%)
    all_to_all x1, waiting for transfers between devices, on_device(): lax.all_to_all(outgoing, 'shard', split_axis=0, concat_axis=0, tiled=True)  15.5 us
    all_to_all x1, waiting for transfers between devices, on_device(): lax.all_to_all(returning, 'shard', split_axis=0, concat_axis=0, tiled=True)  10.2 us
    dot_general x2, matrix products, on_device(): jnp.einsum('kij,kjl->kil', mixed, root_right[lo:lo + half], precision=thr...  9.58 us
    ppermute x2, waiting for transfers between devices, gather_rows(): from_right = lax.ppermute(piece, 'tensor', left)  8.89 us
    all_to_all x1, starting transfers between devices, on_device(): lax.all_to_all(outgoing, 'shard', split_axis=0, concat_axis=0, tiled=True)  8.71 us
    all_to_all x1, starting transfers between devices, on_device(): lax.all_to_all(returning, 'shard', split_axis=0, concat_axis=0, tiled=True)  7.9 us
    convert_element_type x1, other arithmetic, on_device(): weight_half = weight_new.astype(jnp.bfloat16)  4.49 us
    ppermute x2, waiting for transfers between devices, gather_rows(): from_left = lax.ppermute(piece, 'tensor', right)  4.46 us
  transfers between devices with their start and end apart: 10, of which 9 were waited for; matrix products, arithmetic and copies ran while one was open for 17% of the time, Pallas kernels for 0%

profile of v6, /device:TPU:1, one launch (start us, length us, event | category | flops | bytes accessed | tf_op | source)
XLA Modules:
  0.0 109.8 jit_solution(9810548632407535723)
XLA Ops:
  0.7 0.8 dynamic_slice.6
  1.5 0.6 iota_reduce_fusion.2
  2.2 0.6 gather_fusion
  2.8 1.1 %broadcast_select_fusion = bf16[32,64,256]{2,1,0:T(8,128)(2,1)} fusion(bf16[32,64,256]{2,1,0:T(8,128)(2,1)S(1)} %gather_fusion, pred[32]{0:T(512)(128)(4,1)S(1)} %fusion.25), kind=kLoop, calls=%fused_computation.35 | loop fusion | flops 524288 | bytes 2097184 | tf_op jit(solution)/shard_map/jit(_where)/select_n | solution.py:33
  3.9 8.7 %all-to-all-start = ((bf16[32,64,256]{2,1,0:T(8,128)(2,1)}), bf16[32,64,256]{2,1,0:T(8,128)(2,1)S(1)}, u32[]{:S(2)}, u32[]{:S(2)}) async-start(bf16[32,64,256]{2,1,0:T(8,128)(2,1)} %broadcast_select_fusion), calls=%async_computation | async-start | bytes 2097152 | tf_op jit(solution)/shard_map/all_to_all | solution.py:64
  13.2 0.6 iota_reduce_fusion.1
  14.0 15.5 %all-to-all-done = bf16[32,64,256]{2,1,0:T(8,128)(2,1)S(1)} async-done(((bf16[32,64,256]{2,1,0:T(8,128)(2,1)}), bf16[32,64,256]{2,1,0:T(8,128)(2,1)S(1)}, u32[]{:S(2)}, u32[]{:S(2)}) %all-to-all-start) | async-done | bytes 1048608 | tf_op jit(solution)/shard_map/all_to_all | solution.py:64
  29.5 0.6 gather_fusion.2
  30.2 3.8 %collective-permute-start.3 = (bf16[12,64,256]{2,1,0:T(8,128)(2,1)S(1)}, bf16[12,64,256]{2,1,0:T(8,128)(2,1)S(1)}, u32[]{:S(2)}, u32[]{:S(2)}) collective-permute-start(bf16[12,64,256]{2,1,0:T(8,128)(2,1)S(1)} %broadcast_select_fusion.1), channel_id=1, source_target_pairs={{0,3},{1,0},{2,1},{3,2},{4,7},{5,4},{6,5},{7,6},{8,11},{9,8},{10,9... | collective-permute-start | bytes 1179656 | tf_op jit(solution)/shard_map/ppermute | solution.py:18
  34.9 7.5 %collective-permute-done.3 = bf16[12,64,256]{2,1,0:T(8,128)(2,1)S(1)} collective-permute-done((bf16[12,64,256]{2,1,0:T(8,128)(2,1)S(1)}, bf16[12,64,256]{2,1,0:T(8,128)(2,1)S(1)}, u32[]{:S(2)}, u32[]{:S(2)}) %collective-permute-start.3) | collective-permute-done | bytes 393248 | tf_op jit(solution)/shard_map/ppermute | solution.py:18
  42.4 3.4 %collective-permute-start.4 = (bf16[12,64,256]{2,1,0:T(8,128)(2,1)S(1)}, bf16[12,64,256]{2,1,0:T(8,128)(2,1)S(1)}, u32[]{:S(2)}, u32[]{:S(2)}) collective-permute-start(bf16[12,64,256]{2,1,0:T(8,128)(2,1)S(1)} %collective-permute-done.3), channel_id=1, source_target_pairs={{0,3},{1,0},{2,1},{3,2},{4,7},{5,4},{6,5},{7,6},{8,11},{9,8},{10,9... | collective-permute-start | bytes 1179656 | tf_op jit(solution)/shard_map/ppermute | solution.py:22
  46.3 1.0 collective-permute-start.2
  47.3 3.4 %fusion.11 = (f32[24]{0:T(128)S(1)}, f32[24,64,256]{2,1,0:T(8,128)}) fusion(bf16[12,64,256]{2,1,0:T(8,128)(2,1)S(1)} %broadcast_select_fusion.1, bf16[12,64,256]{2,1,0:T(8,128)(2,1)S(1)} %broadcast_select_fusion.2, f32[24,64,256]{2,1,0:T(8,128)} %param.25), kind=kLoop, calls=%fused_computation.32 | loop fusion | flops 3932136 | bytes 3932256 | tf_op jit(solution)/shard_map/reduce_sum | solution.py:100
  50.7 4.0 %collective-permute-done.5 = bf16[12,64,256]{2,1,0:T(8,128)(2,1)S(1)} collective-permute-done((bf16[12,64,256]{2,1,0:T(8,128)(2,1)S(1)}, bf16[12,64,256]{2,1,0:T(8,128)(2,1)S(1)}, u32[]{:S(2)}, u32[]{:S(2)}) %collective-permute-start.5) | collective-permute-done | bytes 393248 | tf_op jit(solution)/shard_map/ppermute | solution.py:17
  54.7 1.3 %conditional.3 = (bf16[12,256,256]{2,1,0:T(8,128)(2,1)}) conditional(s32[]{:T(128)} %clamp.4, (bf16[12,64,256]{2,1,0:T(8,128)(2,1)S(1)}, bf16[12,64,256]{2,1,0:T(8,128)(2,1)S(1)}, bf16[12,64,256]{2,1,0:T(8,128)(2,1)S(1)}, bf16[12,64,256]{2,1,0:T(8,128)(2,1)S(1)}) %tuple.42, (bf16[12,64,256]{2,1,0:T(8,128)(2,1)S(1)}, ...), branch_computations={%region_9.10_spmd, %region_10.11_spmd, %region_11.12_spmd, %region... | conditional | flops 6291456 | bytes 3145736 | solution.py:28
  54.7 1.3 %pad_maximum_fusion.4 = bf16[12,256,256]{2,1,0:T(8,128)(2,1)} fusion(bf16[12,64,256]{2,1,0:T(8,128)(2,1)S(1)} %get-tuple-element.93, bf16[12,64,256]{2,1,0:T(8,128)(2,1)S(1)} %get-tuple-element.92, bf16[12,64,256]{2,1,0:T(8,128)(2,1)S(1)} %get-tuple-element.91, bf16[12,64,256]{2,1,0:T(8,128)(2,1)S(1)} %get-tuple-element.90), kind=kLoop, calls=%fused_computation.9 | loop fusion | flops 6291456 | bytes 3145728 | tf_op jit(solution)/shard_map/cond/branch_0_fun/concatenate | solution.py:26
  56.0 4.4 %multiply_reduce_fusion = (f32[12]{0:T(128)S(1)}, f32[12,64,256]{2,1,0:T(8,128)S(1)}) fusion(f32[24,256,256]{2,1,0:T(8,128)} %param.24, bf16[12,256,256]{2,1,0:T(8,128)(2,1)} %get-tuple-element.136, f32[24,64,256]{2,1,0:T(8,128)} %param.23), kind=kOutput, calls=%fused_computation.37 | convolution fusion | flops 604372992 | bytes 6291504 | tf_op jit(solution)/shard_map/kij,kjl->kil/dot_general | solution.py:93
  60.4 1.4 %collective-permute-done = bf16[12,64,256]{2,1,0:T(8,128)(2,1)S(1)} collective-permute-done((bf16[12,64,256]{2,1,0:T(8,128)(2,1)S(1)}, bf16[12,64,256]{2,1,0:T(8,128)(2,1)S(1)}, u32[]{:S(2)}, u32[]{:S(2)}) %collective-permute-start) | collective-permute-done | bytes 393248 | tf_op jit(solution)/shard_map/ppermute | solution.py:18
  61.7 1.4 %collective-permute-done.2 = bf16[12,64,256]{2,1,0:T(8,128)(2,1)S(1)} collective-permute-done((bf16[12,64,256]{2,1,0:T(8,128)(2,1)S(1)}, bf16[12,64,256]{2,1,0:T(8,128)(2,1)S(1)}, u32[]{:S(2)}, u32[]{:S(2)}) %collective-permute-start.2) | collective-permute-done | bytes 393248 | tf_op jit(solution)/shard_map/ppermute | solution.py:20
  63.1 1.3 %conditional.2 = (bf16[12,256,256]{2,1,0:T(8,128)(2,1)}) conditional(s32[]{:T(128)} %clamp.4, (bf16[12,64,256]{2,1,0:T(8,128)(2,1)S(1)}, bf16[12,64,256]{2,1,0:T(8,128)(2,1)S(1)}, bf16[12,64,256]{2,1,0:T(8,128)(2,1)S(1)}, bf16[12,64,256]{2,1,0:T(8,128)(2,1)S(1)}) %tuple.38, (bf16[12,64,256]{2,1,0:T(8,128)(2,1)S(1)}, ...), branch_computations={%region_5.6_spmd, %region_6.7_spmd, %region_7.8_spmd, %region_8.9_... | conditional | flops 6291456 | bytes 3145736 | solution.py:28
  63.1 1.3 %pad_maximum_fusion = bf16[12,256,256]{2,1,0:T(8,128)(2,1)} fusion(bf16[12,64,256]{2,1,0:T(8,128)(2,1)S(1)} %get-tuple-element.72, bf16[12,64,256]{2,1,0:T(8,128)(2,1)S(1)} %get-tuple-element.71, bf16[12,64,256]{2,1,0:T(8,128)(2,1)S(1)} %get-tuple-element.70, bf16[12,64,256]{2,1,0:T(8,128)(2,1)S(1)} %get-tuple-element.64), kind=kLoop, calls=%fused_computation.5 | loop fusion | flops 6291456 | bytes 3145728 | tf_op jit(solution)/shard_map/cond/branch_0_fun/concatenate | solution.py:26
  64.4 5.2 %multiply_reduce_fusion.1 = (f32[12]{0:T(128)S(1)}, f32[12,64,256]{2,1,0:T(8,128)}) fusion(f32[24,256,256]{2,1,0:T(8,128)} %param.24, bf16[12,256,256]{2,1,0:T(8,128)(2,1)} %get-tuple-element.135, f32[24,64,256]{2,1,0:T(8,128)} %param.23), kind=kOutput, calls=%fused_computation.39 | convolution fusion | flops 604372992 | bytes 6291504 | tf_op jit(solution)/shard_map/kij,kjl->kil/dot_general | solution.py:93
  70.3 1.9 %collective-permute-done.6 = f32[2,24]{1,0:T(2,128)S(1)} collective-permute-done((f32[2,24]{1,0:T(2,128)S(1)}, f32[2,24]{1,0:T(2,128)S(1)}, u32[]{:S(2)}, u32[]{:S(2)}) %collective-permute-start.6) | collective-permute-done | bytes 224 | tf_op jit(solution)/shard_map/ppermute | solution.py:104
  72.2 1.8 %collective-permute-start.7 = (f32[2,24]{1,0:T(2,128)S(1)}, f32[2,24]{1,0:T(2,128)S(1)}, u32[]{:S(2)}, u32[]{:S(2)}) collective-permute-start(f32[2,24]{1,0:T(2,128)S(1)} %fusion.29), channel_id=1, source_target_pairs={{0,2},{1,3},{2,0},{3,1},{4,6},{5,7},{6,4},{7,5},{8,10},{9,11},{10,... | collective-permute-start | bytes 584 | tf_op jit(solution)/shard_map/ppermute | solution.py:104
  74.0 2.2 %collective-permute-done.7 = f32[2,24]{1,0:T(2,128)S(1)} collective-permute-done((f32[2,24]{1,0:T(2,128)S(1)}, f32[2,24]{1,0:T(2,128)S(1)}, u32[]{:S(2)}, u32[]{:S(2)}) %collective-permute-start.7) | collective-permute-done | bytes 224 | tf_op jit(solution)/shard_map/ppermute | solution.py:104
  76.2 4.5 %fusion.30 = (bf16[24,64,256]{2,1,0:T(8,128)(2,1)S(1)}, f32[24,64,256]{2,1,0:T(8,128)}, f32[24,64,256]{2,1,0:T(8,128)}) fusion(f32[24,64,256]{2,1,0:T(8,128)} %param.27, f32[12,64,256]{2,1,0:T(8,128)S(1)} %get-tuple-element.130, f32[12,64,256]{2,1,0:T(8,128)} %get-tuple-element.132, f32[24]{0:T(128)S(1)} %multiply_bitcast_fusion, f32[24,64,256]{2,1,0:T(8,128)} %param.26), kind=kLoop, calls=%fused_computation.65 | loop fusion | flops 2752512 | bytes 8650848 | tf_op jit(solution)/shard_map/convert_element_type | solution.py:113
  80.7 1.6 %gather_fusion.3 = bf16[32,64,256]{2,1,0:T(8,128)(2,1)} fusion(bf16[24,64,256]{2,1,0:T(8,128)(2,1)S(1)} %get-tuple-element.120, s32[1024]{0:T(1024)S(1)} %pad_clamp_fusion.1), kind=kCustom, calls=%fused_computation.3 | custom fusion | bytes 2097280 | tf_op jit(solution)/shard_map/jit(_take)/gather | solution.py:114
  82.3 7.9 %all-to-all-start.1 = ((bf16[32,64,256]{2,1,0:T(8,128)(2,1)}), bf16[32,64,256]{2,1,0:T(8,128)(2,1)}, u32[]{:S(2)}, u32[]{:S(2)}) async-start(bf16[32,64,256]{2,1,0:T(8,128)(2,1)} %gather_fusion.3), calls=%async_computation.1 | async-start | bytes 2097152 | tf_op jit(solution)/shard_map/all_to_all | solution.py:115
  90.3 4.2 %multiply_add_fusion.1 = f32[24,64,256]{2,1,0:T(8,128)} fusion(f32[24,64,256]{2,1,0:T(8,128)} %param.21, bf16[12,256,256]{2,1,0:T(8,128)(2,1)S(1)} %copy-done.1, bf16[12,256,256]{2,1,0:T(8,128)(2,1)} %get-tuple-element.135, bf16[12,64,256]{2,1,0:T(8,128)(2,1)S(1)} %broadcast_select_fusion.1, bf16[12,64,256]{2,1,0:T(8,128)(2,1)S(1)} %broadcast_select_fusion.2), kind=kOutput, calls=%fused_computation.31 | convolution fusion | flops 204472320 | bytes 7077888 | tf_op jit(solution)/shard_map/kij,klj->kil/dot_general | solution.py:76
  94.5 2.5 %multiply_add_fusion = f32[24,64,256]{2,1,0:T(8,128)} fusion(f32[24,64,256]{2,1,0:T(8,128)S(1)} %copy-done.5, bf16[12,256,256]{2,1,0:T(8,128)(2,1)S(1)} %copy-done.1, bf16[12,256,256]{2,1,0:T(8,128)(2,1)S(1)} %copy-done.2, s32[]{:T(128)S(6)} %select_n.33), kind=kOutput, calls=%fused_computation.30 | convolution fusion | flops 205651968 | bytes 9437188 | tf_op jit(solution)/shard_map/kji,kjl->kil/dot_general | solution.py:79
  97.1 10.2 %all-to-all-done.1 = bf16[32,64,256]{2,1,0:T(8,128)(2,1)} async-done(((bf16[32,64,256]{2,1,0:T(8,128)(2,1)}), bf16[32,64,256]{2,1,0:T(8,128)(2,1)}, u32[]{:S(2)}, u32[]{:S(2)}) %all-to-all-start.1) | async-done | bytes 1048608 | tf_op jit(solution)/shard_map/all_to_all | solution.py:115
  107.3 2.6 %gather_fusion.4 = bf16[12,64,256]{2,1,0:T(8,128)(2,1)} fusion(bf16[32,64,256]{2,1,0:T(8,128)(2,1)} %all-to-all-done.1, s32[1024]{0:T(1024)S(1)} %pad_clamp_fusion), kind=kCustom, calls=%fused_computation.4 | custom fusion | bytes 786480 | tf_op jit(solution)/shard_map/jit(_take)/gather | solution.py:116
  (40 shorter events, 2.9 us)
Async XLA Ops:
  0.6 1.5 %copy-start = (bf16[12,64,256]{2,1,0:T(8,128)(2,1)S(1)}, bf16[12,64,256]{2,1,0:T(8,128)(2,1)}, u32[]{:S(2)}) copy-start(bf16[12,64,256]{2,1,0:T(8,128)(2,1)} %param.18) | copy-start | bytes 1179652
  3.9 8.7 %copy-start.3 = (s32[384]{0:T(512)S(1)}, s32[384]{0:T(512)}, u32[]{:S(2)}) copy-start(s32[384]{0:T(512)} %param.20) | copy-start | bytes 4612
  3.9 8.9 %copy-start.4 = (s32[384]{0:T(512)S(1)}, s32[384]{0:T(512)}, u32[]{:S(2)}) copy-start(s32[384]{0:T(512)} %param.19) | copy-start | bytes 4612
  3.9 25.6 %all-to-all-start = ((bf16[32,64,256]{2,1,0:T(8,128)(2,1)}), bf16[32,64,256]{2,1,0:T(8,128)(2,1)S(1)}, u32[]{:S(2)}, u32[]{:S(2)}) async-start(bf16[32,64,256]{2,1,0:T(8,128)(2,1)} %broadcast_select_fusion), calls=%async_computation | async-start | bytes 2097152 | tf_op jit(solution)/shard_map/all_to_all | solution.py:64
  30.2 12.2 %collective-permute-start.3 = (bf16[12,64,256]{2,1,0:T(8,128)(2,1)S(1)}, bf16[12,64,256]{2,1,0:T(8,128)(2,1)S(1)}, u32[]{:S(2)}, u32[]{:S(2)}) collective-permute-start(bf16[12,64,256]{2,1,0:T(8,128)(2,1)S(1)} %broadcast_select_fusion.1), channel_id=1, source_target_pairs={{0,3},{1,0},{2,1},{3,2},{4,7},{5,4},{6,5},{7,6},{8,11},{9,8},{10,9... | collective-permute-start | bytes 1179656 | tf_op jit(solution)/shard_map/ppermute | solution.py:18
  34.7 11.6 %collective-permute-start.1 = (bf16[12,64,256]{2,1,0:T(8,128)(2,1)S(1)}, bf16[12,64,256]{2,1,0:T(8,128)(2,1)S(1)}, u32[]{:S(2)}, u32[]{:S(2)}) collective-permute-start(bf16[12,64,256]{2,1,0:T(8,128)(2,1)S(1)} %broadcast_select_fusion.2), channel_id=1, source_target_pairs={{0,1},{1,2},{2,3},{3,0},{4,5},{5,6},{6,7},{7,4},{8,9},{9,10},{10,1... | collective-permute-start | bytes 1179656 | tf_op jit(solution)/shard_map/ppermute | solution.py:17
  34.8 19.9 %collective-permute-start.5 = (bf16[12,64,256]{2,1,0:T(8,128)(2,1)S(1)}, bf16[12,64,256]{2,1,0:T(8,128)(2,1)S(1)}, u32[]{:S(2)}, u32[]{:S(2)}) collective-permute-start(bf16[12,64,256]{2,1,0:T(8,128)(2,1)S(1)} %broadcast_select_fusion.1), channel_id=1, source_target_pairs={{0,1},{1,2},{2,3},{3,0},{4,5},{5,6},{6,7},{7,4},{8,9},{9,10},{10,1... | collective-permute-start | bytes 1179656 | tf_op jit(solution)/shard_map/ppermute | solution.py:17
  42.4 12.3 %collective-permute-start.4 = (bf16[12,64,256]{2,1,0:T(8,128)(2,1)S(1)}, bf16[12,64,256]{2,1,0:T(8,128)(2,1)S(1)}, u32[]{:S(2)}, u32[]{:S(2)}) collective-permute-start(bf16[12,64,256]{2,1,0:T(8,128)(2,1)S(1)} %collective-permute-done.3), channel_id=1, source_target_pairs={{0,3},{1,0},{2,1},{3,2},{4,7},{5,4},{6,5},{7,6},{8,11},{9,8},{10,9... | collective-permute-start | bytes 1179656 | tf_op jit(solution)/shard_map/ppermute | solution.py:22
  45.8 15.9 %collective-permute-start = (bf16[12,64,256]{2,1,0:T(8,128)(2,1)S(1)}, bf16[12,64,256]{2,1,0:T(8,128)(2,1)S(1)}, u32[]{:S(2)}, u32[]{:S(2)}) collective-permute-start(bf16[12,64,256]{2,1,0:T(8,128)(2,1)S(1)} %broadcast_select_fusion.2), channel_id=1, source_target_pairs={{0,3},{1,0},{2,1},{3,2},{4,7},{5,4},{6,5},{7,6},{8,11},{9,8},{10,9... | collective-permute-start | bytes 1179656 | tf_op jit(solution)/shard_map/ppermute | solution.py:18
  46.3 16.9 %collective-permute-start.2 = (bf16[12,64,256]{2,1,0:T(8,128)(2,1)S(1)}, bf16[12,64,256]{2,1,0:T(8,128)(2,1)S(1)}, u32[]{:S(2)}, u32[]{:S(2)}) collective-permute-start(bf16[12,64,256]{2,1,0:T(8,128)(2,1)S(1)} %collective-permute-done.1), channel_id=1, source_target_pairs={{0,1},{1,2},{2,3},{3,0},{4,5},{5,6},{6,7},{7,4},{8,9},{9,10},{10,1... | collective-permute-start | bytes 1179656 | tf_op jit(solution)/shard_map/ppermute | solution.py:20
  69.7 2.5 %collective-permute-start.6 = (f32[2,24]{1,0:T(2,128)S(1)}, f32[2,24]{1,0:T(2,128)S(1)}, u32[]{:S(2)}, u32[]{:S(2)}) collective-permute-start(f32[2,24]{1,0:T(2,128)S(1)} %pad_maximum_fusion.17), channel_id=1, source_target_pairs={{0,1},{1,0},{2,3},{3,2},{4,5},{5,4},{6,7},{7,6},{8,9},{9,8},{10,11... | collective-permute-start | bytes 584 | tf_op jit(solution)/shard_map/ppermute | solution.py:104
  72.2 4.0 %collective-permute-start.7 = (f32[2,24]{1,0:T(2,128)S(1)}, f32[2,24]{1,0:T(2,128)S(1)}, u32[]{:S(2)}, u32[]{:S(2)}) collective-permute-start(f32[2,24]{1,0:T(2,128)S(1)} %fusion.29), channel_id=1, source_target_pairs={{0,2},{1,3},{2,0},{3,1},{4,6},{5,7},{6,4},{7,5},{8,10},{9,11},{10,... | collective-permute-start | bytes 584 | tf_op jit(solution)/shard_map/ppermute | solution.py:104
  82.3 7.9 %copy-start.1 = (bf16[12,256,256]{2,1,0:T(8,128)(2,1)S(1)}, bf16[12,256,256]{2,1,0:T(8,128)(2,1)}, u32[]{:S(2)}) copy-start(bf16[12,256,256]{2,1,0:T(8,128)(2,1)} %get-tuple-element.136) | copy-start | bytes 4718596
  82.3 25.0 %all-to-all-start.1 = ((bf16[32,64,256]{2,1,0:T(8,128)(2,1)}), bf16[32,64,256]{2,1,0:T(8,128)(2,1)}, u32[]{:S(2)}, u32[]{:S(2)}) async-start(bf16[32,64,256]{2,1,0:T(8,128)(2,1)} %gather_fusion.3), calls=%async_computation.1 | async-start | bytes 2097152 | tf_op jit(solution)/shard_map/all_to_all | solution.py:115
  90.3 4.3 %copy-start.2 = (bf16[12,256,256]{2,1,0:T(8,128)(2,1)S(1)}, bf16[12,256,256]{2,1,0:T(8,128)(2,1)}, u32[]{:S(2)}) copy-start(bf16[12,256,256]{2,1,0:T(8,128)(2,1)} %get-tuple-element.135) | copy-start | bytes 4718596
  90.3 4.3 %copy-start.5 = (f32[24,64,256]{2,1,0:T(8,128)S(1)}, f32[24,64,256]{2,1,0:T(8,128)}, u32[]{:S(2)}) copy-start(f32[24,64,256]{2,1,0:T(8,128)} %param.22) | copy-start | bytes 4718596

commit v7 on v0

--- a/solution.py
+++ b/solution.py
@@ -56,7 +56,6 @@
     src_of_slot = jnp.argmax(slot_match, axis=1).astype(jnp.int32)
     slot_filled = jnp.any(slot_match, axis=1)
     slot_of_src = jnp.argmax(slot_match, axis=0).astype(jnp.int32)
-    src_sent = jnp.any(slot_match, axis=0)
     dest_match = local_owner[None, :] == group_ids[:, None]
     block_of_dest = jnp.argmax(dest_match, axis=1).astype(jnp.int32)
     dest_used = jnp.any(dest_match, axis=1)
@@ -109,12 +108,15 @@
     scale_ratio = jnp.sqrt(adam_sum / entries + eps_mean) / jnp.sqrt(
         precond_sum / entries + eps_mean
     )
-    velocity_new = beta_mom * momentum + (1.0 - beta_mom) * scale_ratio[:, None, None] * precond
-    weight_new = master - learn_rate * velocity_new
-    weight_half = weight_new.astype(jnp.bfloat16)
-    returning = pick(weight_half, slot_of_src, src_sent)
+    velocity_soon = beta_mom * momentum + (1.0 - beta_mom) * scale_ratio[:, None, None] * precond
+    weight_half = (master - learn_rate * velocity_soon).astype(jnp.bfloat16)
+    held = lax.optimization_barrier((momentum, master, precond, scale_ratio, weight_half))
+    velocity_new = beta_mom * held[0] + (1.0 - beta_mom) * held[3][:, None, None] * held[2]
+    weight_new = held[1] - learn_rate * velocity_new
+    weight_half = held[4]
+    returning = jnp.take(weight_half, slot_of_src, axis=0, mode="clip")
     back_rows = lax.all_to_all(returning, "shard", split_axis=0, concat_axis=0, tiled=True)
-    weights_local = jnp.take(back_rows, local_owner, axis=0)
+    weights_local = jnp.take(back_rows, local_owner, axis=0, mode="clip")
     return (left_new, right_new, second_new, velocity_new, weight_new, weights_local)
 
 

time: 113 us -> 110 us (0.973)
  other arithmetic: 19.1 us -> 15.2 us
  waiting for transfers between devices: 44 us -> 42.1 us
  matrix products: 16.1 us -> 17.5 us
  local copies, waits for them, and re-layouts: 6.75 us -> 7.91 us
    all_to_all x1, waiting for transfers between devices: 10.2 us -> 6.98 us  [on_device(): lax.all_to_all(returning, 'shard', split_axis=0, concat_axis=0, tiled=True)]
    select_n x4 -> x3, other arithmetic: 3.7 us -> 1.3 us  [pick(): return jnp.where(valid[:, None, None], taken, jnp.zeros((), source.dtype))]
    gather x1 -> x2, local copies, waits for them, and re-layouts: 1.79 us -> 4.16 us  [the longest x1 2.55 us: on_device(): weights_local = jnp.take(back_rows, local_owner, axis=0, mode='clip')]
    sub x0 -> x1, other arithmetic: none -> 2.28 us  [on_device(): weight_new = held[1] - learn_rate * velocity_new]
    dot_general x1, matrix products: 2.54 us -> 4.81 us  [on_device(): jnp.einsum('kji,kjl->kil', grad_cols, grad_whole, preferred_element_type=...]
    dot_general x1, matrix products: 4.24 us -> 2.2 us  [on_device(): jnp.einsum('kij,klj->kil', grad_piece, grad_whole, preferred_element_type...]
    gather x4 -> x3, local copies, waits for them, and re-layouts: 3.65 us -> 1.75 us  [pick(): taken = jnp.take(source, index, axis=0, mode='clip')]
    dot_general x2, matrix products: 9.33 us -> 10.5 us  [on_device(): jnp.einsum('kij,kjl->kil', mixed, root_right[lo:lo + half], precision=thr...]
  transfers between devices with their start and end apart: 10 -> 10, of which waited for: 8 -> 8; matrix products, arithmetic and copies ran while one was open for 18% -> 20% of each run, Pallas kernels for 0% -> 0%
where the time goes in v7:
time: 110 us; the launch traced here: 109 us
  waiting for transfers between devices  42.1 us (38%)
  starting transfers between devices  25.7 us (23%)
  matrix products  17.5 us (16%)
  other arithmetic  15.2 us (14%)
  local copies, waits for them, and re-layouts  7.91 us (7%)
    all_to_all x1, waiting for transfers between devices, on_device(): lax.all_to_all(outgoing, 'shard', split_axis=0, concat_axis=0, tiled=True)  15.7 us
    dot_general x2, matrix products, on_device(): jnp.einsum('kij,kjl->kil', mixed, root_right[lo:lo + half], precision=thr...  10.5 us
    all_to_all x1, starting transfers between devices, on_device(): lax.all_to_all(outgoing, 'shard', split_axis=0, concat_axis=0, tiled=True)  8.71 us
    ppermute x2, waiting for transfers between devices, gather_rows(): from_left = lax.ppermute(piece, 'tensor', right)  8.6 us
    all_to_all x1, starting transfers between devices, on_device(): lax.all_to_all(returning, 'shard', split_axis=0, concat_axis=0, tiled=True)  8.23 us
    all_to_all x1, waiting for transfers between devices, on_device(): lax.all_to_all(returning, 'shard', split_axis=0, concat_axis=0, tiled=True)  6.98 us
    ppermute x2, waiting for transfers between devices, on_device(): lax.ppermute(sums, 'tensor', [(i, i ^ step) for i in range(splits)])  6.23 us
    dot_general x1, matrix products, on_device(): jnp.einsum('kji,kjl->kil', grad_cols, grad_whole, preferred_element_type=...  4.81 us
  transfers between devices with their start and end apart: 10, of which 8 were waited for; matrix products, arithmetic and copies ran while one was open for 20% of the time, Pallas kernels for 0%

profile of v7, /device:TPU:1, one launch (start us, length us, event | category | flops | bytes accessed | tf_op | source)
XLA Modules:
  0.0 109.2 jit_solution(2139110529890372973)
XLA Ops:
  0.7 0.8 reshape.55
  2.8 1.1 %broadcast_select_fusion = bf16[32,64,256]{2,1,0:T(8,128)(2,1)} fusion(bf16[32,64,256]{2,1,0:T(8,128)(2,1)S(1)} %gather_fusion, pred[32]{0:T(512)(128)(4,1)S(1)} %fusion.24), kind=kLoop, calls=%fused_computation.36 | loop fusion | flops 524288 | bytes 2097184 | tf_op jit(solution)/shard_map/jit(_where)/select_n | solution.py:33
  3.9 8.7 %all-to-all-start = ((bf16[32,64,256]{2,1,0:T(8,128)(2,1)}), bf16[32,64,256]{2,1,0:T(8,128)(2,1)S(1)}, u32[]{:S(2)}, u32[]{:S(2)}) async-start(bf16[32,64,256]{2,1,0:T(8,128)(2,1)} %broadcast_select_fusion), calls=%async_computation | async-start | bytes 2097152 | tf_op jit(solution)/shard_map/all_to_all | solution.py:64
  13.1 0.6 iota_reduce_fusion.1
  13.9 15.7 %all-to-all-done = bf16[32,64,256]{2,1,0:T(8,128)(2,1)S(1)} async-done(((bf16[32,64,256]{2,1,0:T(8,128)(2,1)}), bf16[32,64,256]{2,1,0:T(8,128)(2,1)S(1)}, u32[]{:S(2)}, u32[]{:S(2)}) %all-to-all-start) | async-done | bytes 1048608 | tf_op jit(solution)/shard_map/all_to_all | solution.py:64
  30.3 1.7 %collective-permute-start.1 = (bf16[12,64,256]{2,1,0:T(8,128)(2,1)S(1)}, bf16[12,64,256]{2,1,0:T(8,128)(2,1)S(1)}, u32[]{:S(2)}, u32[]{:S(2)}) collective-permute-start(bf16[12,64,256]{2,1,0:T(8,128)(2,1)S(1)} %broadcast_select_fusion.2), channel_id=1, source_target_pairs={{0,1},{1,2},{2,3},{3,0},{4,5},{5,6},{6,7},{7,4},{8,9},{9,10},{10,1... | collective-permute-start | bytes 1179656 | tf_op jit(solution)/shard_map/ppermute | solution.py:17
  32.6 2.2 %collective-permute-start.3 = (bf16[12,64,256]{2,1,0:T(8,128)(2,1)S(1)}, bf16[12,64,256]{2,1,0:T(8,128)(2,1)S(1)}, u32[]{:S(2)}, u32[]{:S(2)}) collective-permute-start(bf16[12,64,256]{2,1,0:T(8,128)(2,1)S(1)} %broadcast_select_fusion.1), channel_id=1, source_target_pairs={{0,3},{1,0},{2,1},{3,2},{4,7},{5,4},{6,5},{7,6},{8,11},{9,8},{10,9... | collective-permute-start | bytes 1179656 | tf_op jit(solution)/shard_map/ppermute | solution.py:18
  35.4 1.5 %collective-permute-start = (bf16[12,64,256]{2,1,0:T(8,128)(2,1)S(1)}, bf16[12,64,256]{2,1,0:T(8,128)(2,1)S(1)}, u32[]{:S(2)}, u32[]{:S(2)}) collective-permute-start(bf16[12,64,256]{2,1,0:T(8,128)(2,1)S(1)} %broadcast_select_fusion.2), channel_id=1, source_target_pairs={{0,3},{1,0},{2,1},{3,2},{4,7},{5,4},{6,5},{7,6},{8,11},{9,8},{10,9... | collective-permute-start | bytes 1179656 | tf_op jit(solution)/shard_map/ppermute | solution.py:18
  36.8 6.6 %collective-permute-done.1 = bf16[12,64,256]{2,1,0:T(8,128)(2,1)S(1)} collective-permute-done((bf16[12,64,256]{2,1,0:T(8,128)(2,1)S(1)}, bf16[12,64,256]{2,1,0:T(8,128)(2,1)S(1)}, u32[]{:S(2)}, u32[]{:S(2)}) %collective-permute-start.1) | collective-permute-done | bytes 393248 | tf_op jit(solution)/shard_map/ppermute | solution.py:17
  43.5 0.7 collective-permute-start.5
  44.2 2.4 %collective-permute-start.4 = (bf16[12,64,256]{2,1,0:T(8,128)(2,1)S(1)}, bf16[12,64,256]{2,1,0:T(8,128)(2,1)S(1)}, u32[]{:S(2)}, u32[]{:S(2)}) collective-permute-start(bf16[12,64,256]{2,1,0:T(8,128)(2,1)S(1)} %collective-permute-done.3), channel_id=1, source_target_pairs={{0,3},{1,0},{2,1},{3,2},{4,7},{5,4},{6,5},{7,6},{8,11},{9,8},{10,9... | collective-permute-start | bytes 1179656 | tf_op jit(solution)/shard_map/ppermute | solution.py:22
  46.6 3.4 %fusion.10 = (f32[24]{0:T(128)S(1)}, f32[24,64,256]{2,1,0:T(8,128)}) fusion(bf16[12,64,256]{2,1,0:T(8,128)(2,1)S(1)} %broadcast_select_fusion.1, bf16[12,64,256]{2,1,0:T(8,128)(2,1)S(1)} %broadcast_select_fusion.2, f32[24,64,256]{2,1,0:T(8,128)} %param.25), kind=kLoop, calls=%fused_computation.33 | loop fusion | flops 3932136 | bytes 3932256 | tf_op jit(solution)/shard_map/reduce_sum | solution.py:100
  50.0 1.7 %collective-permute-done = bf16[12,64,256]{2,1,0:T(8,128)(2,1)S(1)} collective-permute-done((bf16[12,64,256]{2,1,0:T(8,128)(2,1)S(1)}, bf16[12,64,256]{2,1,0:T(8,128)(2,1)S(1)}, u32[]{:S(2)}, u32[]{:S(2)}) %collective-permute-start) | collective-permute-done | bytes 393248 | tf_op jit(solution)/shard_map/ppermute | solution.py:18
  51.8 2.9 %collective-permute-done.2 = bf16[12,64,256]{2,1,0:T(8,128)(2,1)S(1)} collective-permute-done((bf16[12,64,256]{2,1,0:T(8,128)(2,1)S(1)}, bf16[12,64,256]{2,1,0:T(8,128)(2,1)S(1)}, u32[]{:S(2)}, u32[]{:S(2)}) %collective-permute-start.2) | collective-permute-done | bytes 393248 | tf_op jit(solution)/shard_map/ppermute | solution.py:20
  54.7 1.3 %conditional.2 = (bf16[12,256,256]{2,1,0:T(8,128)(2,1)}) conditional(s32[]{:T(128)} %clamp.4, (bf16[12,64,256]{2,1,0:T(8,128)(2,1)S(1)}, bf16[12,64,256]{2,1,0:T(8,128)(2,1)S(1)}, bf16[12,64,256]{2,1,0:T(8,128)(2,1)S(1)}, bf16[12,64,256]{2,1,0:T(8,128)(2,1)S(1)}) %tuple.39, (bf16[12,64,256]{2,1,0:T(8,128)(2,1)S(1)}, ...), branch_computations={%region_5.6_spmd, %region_6.7_spmd, %region_7.8_spmd, %region_8.9_... | conditional | flops 6291456 | bytes 3145736 | solution.py:28
  54.7 1.3 %pad_maximum_fusion = bf16[12,256,256]{2,1,0:T(8,128)(2,1)} fusion(bf16[12,64,256]{2,1,0:T(8,128)(2,1)S(1)} %get-tuple-element.72, bf16[12,64,256]{2,1,0:T(8,128)(2,1)S(1)} %get-tuple-element.71, bf16[12,64,256]{2,1,0:T(8,128)(2,1)S(1)} %get-tuple-element.70, bf16[12,64,256]{2,1,0:T(8,128)(2,1)S(1)} %get-tuple-element.64), kind=kLoop, calls=%fused_computation.5 | loop fusion | flops 6291456 | bytes 3145728 | tf_op jit(solution)/shard_map/cond/branch_0_fun/concatenate | solution.py:26
  55.9 5.2 %multiply_reduce_fusion.1 = (f32[12]{0:T(128)S(1)}, f32[12,64,256]{2,1,0:T(8,128)}) fusion(f32[24,256,256]{2,1,0:T(8,128)} %param.24, bf16[12,256,256]{2,1,0:T(8,128)(2,1)} %get-tuple-element.148, f32[24,64,256]{2,1,0:T(8,128)} %param.23), kind=kOutput, calls=%fused_computation.39 | convolution fusion | flops 604372992 | bytes 6291504 | tf_op jit(solution)/shard_map/kij,kjl->kil/dot_general | solution.py:93
  61.1 2.0 %collective-permute-done.5 = bf16[12,64,256]{2,1,0:T(8,128)(2,1)S(1)} collective-permute-done((bf16[12,64,256]{2,1,0:T(8,128)(2,1)S(1)}, bf16[12,64,256]{2,1,0:T(8,128)(2,1)S(1)}, u32[]{:S(2)}, u32[]{:S(2)}) %collective-permute-start.5) | collective-permute-done | bytes 393248 | tf_op jit(solution)/shard_map/ppermute | solution.py:17
  63.1 1.3 %conditional.3 = (bf16[12,256,256]{2,1,0:T(8,128)(2,1)}) conditional(s32[]{:T(128)} %clamp.4, (bf16[12,64,256]{2,1,0:T(8,128)(2,1)S(1)}, bf16[12,64,256]{2,1,0:T(8,128)(2,1)S(1)}, bf16[12,64,256]{2,1,0:T(8,128)(2,1)S(1)}, bf16[12,64,256]{2,1,0:T(8,128)(2,1)S(1)}) %tuple.43, (bf16[12,64,256]{2,1,0:T(8,128)(2,1)S(1)}, ...), branch_computations={%region_9.10_spmd, %region_10.11_spmd, %region_11.12_spmd, %region... | conditional | flops 6291456 | bytes 3145736 | solution.py:28
  63.1 1.3 %pad_maximum_fusion.4 = bf16[12,256,256]{2,1,0:T(8,128)(2,1)} fusion(bf16[12,64,256]{2,1,0:T(8,128)(2,1)S(1)} %get-tuple-element.93, bf16[12,64,256]{2,1,0:T(8,128)(2,1)S(1)} %get-tuple-element.92, bf16[12,64,256]{2,1,0:T(8,128)(2,1)S(1)} %get-tuple-element.91, bf16[12,64,256]{2,1,0:T(8,128)(2,1)S(1)} %get-tuple-element.90), kind=kLoop, calls=%fused_computation.9 | loop fusion | flops 6291456 | bytes 3145728 | tf_op jit(solution)/shard_map/cond/branch_0_fun/concatenate | solution.py:26
  64.3 5.3 %multiply_reduce_fusion = (f32[12]{0:T(128)S(1)}, f32[12,64,256]{2,1,0:T(8,128)}) fusion(f32[24,256,256]{2,1,0:T(8,128)} %param.24, bf16[12,256,256]{2,1,0:T(8,128)(2,1)} %get-tuple-element.149, f32[24,64,256]{2,1,0:T(8,128)} %param.23), kind=kOutput, calls=%fused_computation.38 | convolution fusion | flops 604372992 | bytes 6291504 | tf_op jit(solution)/shard_map/kij,kjl->kil/dot_general | solution.py:93
  69.8 2.4 %collective-permute-done.6 = f32[2,24]{1,0:T(2,128)S(1)} collective-permute-done((f32[2,24]{1,0:T(2,128)S(1)}, f32[2,24]{1,0:T(2,128)S(1)}, u32[]{:S(2)}, u32[]{:S(2)}) %collective-permute-start.6) | collective-permute-done | bytes 224 | tf_op jit(solution)/shard_map/ppermute | solution.py:104
  72.4 3.8 %collective-permute-done.7 = f32[2,24]{1,0:T(2,128)S(1)} collective-permute-done((f32[2,24]{1,0:T(2,128)S(1)}, f32[2,24]{1,0:T(2,128)S(1)}, u32[]{:S(2)}, u32[]{:S(2)}) %collective-permute-start.7) | collective-permute-done | bytes 224 | tf_op jit(solution)/shard_map/ppermute | solution.py:104
  76.3 3.5 %subtract_convert_fusion = (bf16[24,64,256]{2,1,0:T(8,128)(2,1)S(1)}, f32[24,64,256]{2,1,0:T(8,128)}) fusion(f32[24,64,256]{2,1,0:T(8,128)S(1)} %copy-done.3, f32[24,64,256]{2,1,0:T(8,128)} %param.26, f32[24]{0:T(128)S(1)} %get-tuple-element.132, f32[12,64,256]{2,1,0:T(8,128)} %get-tuple-element.143, f32[12,64,256]{2,1,0:T(8,128)} %get-tuple-element.145), kind=kLoop, calls=%fused_computation.30 | loop fusion | flops 2752512 | bytes 7077984 | tf_op jit(solution)/shard_map/convert_element_type | solution.py:112
  79.8 1.6 %gather_fusion.3 = bf16[32,64,256]{2,1,0:T(8,128)(2,1)} fusion(bf16[24,64,256]{2,1,0:T(8,128)(2,1)S(1)} %get-tuple-element.126, s32[1024]{0:T(1024)S(1)} %pad_clamp_fusion.1), kind=kCustom, calls=%fused_computation.3 | custom fusion | bytes 2097280 | tf_op jit(solution)/shard_map/jit(_take)/gather | solution.py:117
  81.4 8.2 %all-to-all-start.1 = ((bf16[32,64,256]{2,1,0:T(8,128)(2,1)}), bf16[32,64,256]{2,1,0:T(8,128)(2,1)}, u32[]{:S(2)}, u32[]{:S(2)}) async-start(bf16[32,64,256]{2,1,0:T(8,128)(2,1)} %gather_fusion.3), calls=%async_computation.1 | async-start | bytes 2097152 | tf_op jit(solution)/shard_map/all_to_all | solution.py:118
  89.7 4.8 %multiply_add_fusion.1 = f32[24,64,256]{2,1,0:T(8,128)} fusion(f32[24,64,256]{2,1,0:T(8,128)} %param.22, bf16[12,256,256]{2,1,0:T(8,128)(2,1)} %get-tuple-element.149, bf16[12,256,256]{2,1,0:T(8,128)(2,1)S(1)} %copy-done.1, s32[]{:T(128)S(6)} %select_n.34), kind=kOutput, calls=%fused_computation.31 | convolution fusion | flops 205651968 | bytes 9437188 | tf_op jit(solution)/shard_map/kji,kjl->kil/dot_general | solution.py:79
  94.5 2.2 %multiply_add_fusion.2 = f32[24,64,256]{2,1,0:T(8,128)} fusion(f32[24,64,256]{2,1,0:T(8,128)S(1)} %copy-done.8, bf16[12,256,256]{2,1,0:T(8,128)(2,1)S(1)} %copy-done.2, bf16[12,256,256]{2,1,0:T(8,128)(2,1)S(1)} %copy-done.1, bf16[12,64,256]{2,1,0:T(8,128)(2,1)S(1)} %broadcast_select_fusion.1, bf16[12,64,256]{2,1,0:T(8,128)(2,1)S(1)} %broadcast_select_fusion.2), kind=kOutput, calls=%fused_computation.32 | convolution fusion | flops 204472320 | bytes 7077888 | tf_op jit(solution)/shard_map/kij,klj->kil/dot_general | solution.py:76
  96.7 0.7 copy-done.6
  97.4 2.3 %multiply_subtract_fusion = (f32[24,64,256]{2,1,0:T(8,128)}, f32[24,64,256]{2,1,0:T(8,128)}) fusion(f32[24,64,256]{2,1,0:T(8,128)S(1)} %copy-done.4, f32[24,64,256]{2,1,0:T(8,128)S(1)} %copy-done.6, f32[24]{0:T(128)S(1)} %broadcast_multiply_fusion, f32[24,64,256]{2,1,0:T(8,128)S(1)} %copy-done.5), kind=kLoop, calls=%fused_computation.28 | loop fusion | flops 1966080 | bytes 7864416 | tf_op jit(solution)/shard_map/sub | solution.py:115
  99.7 7.0 %all-to-all-done.1 = bf16[32,64,256]{2,1,0:T(8,128)(2,1)} async-done(((bf16[32,64,256]{2,1,0:T(8,128)(2,1)}), bf16[32,64,256]{2,1,0:T(8,128)(2,1)}, u32[]{:S(2)}, u32[]{:S(2)}) %all-to-all-start.1) | async-done | bytes 1048608 | tf_op jit(solution)/shard_map/all_to_all | solution.py:118
  106.7 2.6 %gather_fusion.4 = bf16[12,64,256]{2,1,0:T(8,128)(2,1)} fusion(bf16[32,64,256]{2,1,0:T(8,128)(2,1)} %all-to-all-done.1, s32[1024]{0:T(1024)S(1)} %pad_clamp_fusion), kind=kCustom, calls=%fused_computation.4 | custom fusion | bytes 786480 | tf_op jit(solution)/shard_map/jit(_take)/gather | solution.py:119
  (48 shorter events, 4.2 us)
Async XLA Ops:
  0.6 1.6 %copy-start = (bf16[12,64,256]{2,1,0:T(8,128)(2,1)S(1)}, bf16[12,64,256]{2,1,0:T(8,128)(2,1)}, u32[]{:S(2)}) copy-start(bf16[12,64,256]{2,1,0:T(8,128)(2,1)} %param.18) | copy-start | bytes 1179652
  3.9 8.8 %copy-start.7 = (s32[384]{0:T(512)S(1)}, s32[384]{0:T(512)}, u32[]{:S(2)}) copy-start(s32[384]{0:T(512)} %param.20) | copy-start | bytes 4612
  3.9 25.6 %all-to-all-start = ((bf16[32,64,256]{2,1,0:T(8,128)(2,1)}), bf16[32,64,256]{2,1,0:T(8,128)(2,1)S(1)}, u32[]{:S(2)}, u32[]{:S(2)}) async-start(bf16[32,64,256]{2,1,0:T(8,128)(2,1)} %broadcast_select_fusion), calls=%async_computation | async-start | bytes 2097152 | tf_op jit(solution)/shard_map/all_to_all | solution.py:64
  30.3 13.2 %collective-permute-start.1 = (bf16[12,64,256]{2,1,0:T(8,128)(2,1)S(1)}, bf16[12,64,256]{2,1,0:T(8,128)(2,1)S(1)}, u32[]{:S(2)}, u32[]{:S(2)}) collective-permute-start(bf16[12,64,256]{2,1,0:T(8,128)(2,1)S(1)} %broadcast_select_fusion.2), channel_id=1, source_target_pairs={{0,1},{1,2},{2,3},{3,0},{4,5},{5,6},{6,7},{7,4},{8,9},{9,10},{10,1... | collective-permute-start | bytes 1179656 | tf_op jit(solution)/shard_map/ppermute | solution.py:17
  32.6 11.5 %collective-permute-start.3 = (bf16[12,64,256]{2,1,0:T(8,128)(2,1)S(1)}, bf16[12,64,256]{2,1,0:T(8,128)(2,1)S(1)}, u32[]{:S(2)}, u32[]{:S(2)}) collective-permute-start(bf16[12,64,256]{2,1,0:T(8,128)(2,1)S(1)} %broadcast_select_fusion.1), channel_id=1, source_target_pairs={{0,3},{1,0},{2,1},{3,2},{4,7},{5,4},{6,5},{7,6},{8,11},{9,8},{10,9... | collective-permute-start | bytes 1179656 | tf_op jit(solution)/shard_map/ppermute | solution.py:18
  35.4 16.4 %collective-permute-start = (bf16[12,64,256]{2,1,0:T(8,128)(2,1)S(1)}, bf16[12,64,256]{2,1,0:T(8,128)(2,1)S(1)}, u32[]{:S(2)}, u32[]{:S(2)}) collective-permute-start(bf16[12,64,256]{2,1,0:T(8,128)(2,1)S(1)} %broadcast_select_fusion.2), channel_id=1, source_target_pairs={{0,3},{1,0},{2,1},{3,2},{4,7},{5,4},{6,5},{7,6},{8,11},{9,8},{10,9... | collective-permute-start | bytes 1179656 | tf_op jit(solution)/shard_map/ppermute | solution.py:18
  43.5 11.2 %collective-permute-start.2 = (bf16[12,64,256]{2,1,0:T(8,128)(2,1)S(1)}, bf16[12,64,256]{2,1,0:T(8,128)(2,1)S(1)}, u32[]{:S(2)}, u32[]{:S(2)}) collective-permute-start(bf16[12,64,256]{2,1,0:T(8,128)(2,1)S(1)} %collective-permute-done.1), channel_id=1, source_target_pairs={{0,1},{1,2},{2,3},{3,0},{4,5},{5,6},{6,7},{7,4},{8,9},{9,10},{10,1... | collective-permute-start | bytes 1179656 | tf_op jit(solution)/shard_map/ppermute | solution.py:20
  43.5 19.6 %collective-permute-start.5 = (bf16[12,64,256]{2,1,0:T(8,128)(2,1)S(1)}, bf16[12,64,256]{2,1,0:T(8,128)(2,1)S(1)}, u32[]{:S(2)}, u32[]{:S(2)}) collective-permute-start(bf16[12,64,256]{2,1,0:T(8,128)(2,1)S(1)} %broadcast_select_fusion.1), channel_id=1, source_target_pairs={{0,1},{1,2},{2,3},{3,0},{4,5},{5,6},{6,7},{7,4},{8,9},{9,10},{10,1... | collective-permute-start | bytes 1179656 | tf_op jit(solution)/shard_map/ppermute | solution.py:17
  44.2 18.9 %collective-permute-start.4 = (bf16[12,64,256]{2,1,0:T(8,128)(2,1)S(1)}, bf16[12,64,256]{2,1,0:T(8,128)(2,1)S(1)}, u32[]{:S(2)}, u32[]{:S(2)}) collective-permute-start(bf16[12,64,256]{2,1,0:T(8,128)(2,1)S(1)} %collective-permute-done.3), channel_id=1, source_target_pairs={{0,3},{1,0},{2,1},{3,2},{4,7},{5,4},{6,5},{7,6},{8,11},{9,8},{10,9... | collective-permute-start | bytes 1179656 | tf_op jit(solution)/shard_map/ppermute | solution.py:22
  64.3 11.9 %copy-start.3 = (f32[24,64,256]{2,1,0:T(8,128)S(1)}, f32[24,64,256]{2,1,0:T(8,128)}, u32[]{:S(2)}) copy-start(f32[24,64,256]{2,1,0:T(8,128)} %param.27) | copy-start | bytes 4718596
  69.7 2.5 %collective-permute-start.6 = (f32[2,24]{1,0:T(2,128)S(1)}, f32[2,24]{1,0:T(2,128)S(1)}, u32[]{:S(2)}, u32[]{:S(2)}) collective-permute-start(f32[2,24]{1,0:T(2,128)S(1)} %pad_maximum_fusion.18), channel_id=1, source_target_pairs={{0,1},{1,0},{2,3},{3,2},{4,5},{5,4},{6,7},{7,6},{8,9},{9,8},{10,11... | collective-permute-start | bytes 584 | tf_op jit(solution)/shard_map/ppermute | solution.py:104
  72.2 4.0 %collective-permute-start.7 = (f32[2,24]{1,0:T(2,128)S(1)}, f32[2,24]{1,0:T(2,128)S(1)}, u32[]{:S(2)}, u32[]{:S(2)}) collective-permute-start(f32[2,24]{1,0:T(2,128)S(1)} %fusion.29), channel_id=1, source_target_pairs={{0,2},{1,3},{2,0},{3,1},{4,6},{5,7},{6,4},{7,5},{8,10},{9,11},{10,... | collective-permute-start | bytes 584 | tf_op jit(solution)/shard_map/ppermute | solution.py:104
  81.4 8.2 %copy-start.1 = (bf16[12,256,256]{2,1,0:T(8,128)(2,1)S(1)}, bf16[12,256,256]{2,1,0:T(8,128)(2,1)}, u32[]{:S(2)}) copy-start(bf16[12,256,256]{2,1,0:T(8,128)(2,1)} %get-tuple-element.148) | copy-start | bytes 4718596
  81.4 25.3 %all-to-all-start.1 = ((bf16[32,64,256]{2,1,0:T(8,128)(2,1)}), bf16[32,64,256]{2,1,0:T(8,128)(2,1)}, u32[]{:S(2)}, u32[]{:S(2)}) async-start(bf16[32,64,256]{2,1,0:T(8,128)(2,1)} %gather_fusion.3), calls=%async_computation.1 | async-start | bytes 2097152 | tf_op jit(solution)/shard_map/all_to_all | solution.py:118
  89.7 4.8 %copy-start.2 = (bf16[12,256,256]{2,1,0:T(8,128)(2,1)S(1)}, bf16[12,256,256]{2,1,0:T(8,128)(2,1)}, u32[]{:S(2)}) copy-start(bf16[12,256,256]{2,1,0:T(8,128)(2,1)} %get-tuple-element.149) | copy-start | bytes 4718596
  89.7 4.8 %copy-start.8 = (f32[24,64,256]{2,1,0:T(8,128)S(1)}, f32[24,64,256]{2,1,0:T(8,128)}, u32[]{:S(2)}) copy-start(f32[24,64,256]{2,1,0:T(8,128)} %param.21) | copy-start | bytes 4718596
  94.5 2.2 %copy-start.4 = (f32[24,64,256]{2,1,0:T(8,128)S(1)}, f32[24,64,256]{2,1,0:T(8,128)}, u32[]{:S(2)}) copy-start(f32[24,64,256]{2,1,0:T(8,128)} %param.27) | copy-start | bytes 4718596
  94.5 2.2 %copy-start.5 = (f32[24,64,256]{2,1,0:T(8,128)S(1)}, f32[24,64,256]{2,1,0:T(8,128)}, u32[]{:S(2)}) copy-start(f32[24,64,256]{2,1,0:T(8,128)} %param.26) | copy-start | bytes 4718596
  94.5 2.9 %copy-start.6 = (f32[24,64,256]{2,1,0:T(8,128)S(1)}, f32[24,64,256]{2,1,0:T(8,128)}, u32[]{:S(2)}) copy-start(f32[24,64,256]{2,1,0:T(8,128)} %get-tuple-element.124) | copy-start | bytes 4718596

commit v8 on v0

--- a/solution.py
+++ b/solution.py
@@ -56,7 +56,6 @@
     src_of_slot = jnp.argmax(slot_match, axis=1).astype(jnp.int32)
     slot_filled = jnp.any(slot_match, axis=1)
     slot_of_src = jnp.argmax(slot_match, axis=0).astype(jnp.int32)
-    src_sent = jnp.any(slot_match, axis=0)
     dest_match = local_owner[None, :] == group_ids[:, None]
     block_of_dest = jnp.argmax(dest_match, axis=1).astype(jnp.int32)
     dest_used = jnp.any(dest_match, axis=1)
@@ -100,10 +99,10 @@
     sums = jnp.stack(
         [jnp.sum(adam_step * adam_step, axis=(1, 2)), precond_sq]
     )
-    step = 1
-    while step < splits:
+    step = splits // 2
+    while step >= 1:
         sums = sums + lax.ppermute(sums, "tensor", [(i, i ^ step) for i in range(splits)])
-        step *= 2
+        step //= 2
     adam_sum, precond_sum = sums[0], sums[1]
     entries = float(rows_dev * splits * order)
     scale_ratio = jnp.sqrt(adam_sum / entries + eps_mean) / jnp.sqrt(
@@ -112,9 +111,9 @@
     velocity_new = beta_mom * momentum + (1.0 - beta_mom) * scale_ratio[:, None, None] * precond
     weight_new = master - learn_rate * velocity_new
     weight_half = weight_new.astype(jnp.bfloat16)
-    returning = pick(weight_half, slot_of_src, src_sent)
+    returning = jnp.take(weight_half, slot_of_src, axis=0, mode="clip")
     back_rows = lax.all_to_all(returning, "shard", split_axis=0, concat_axis=0, tiled=True)
-    weights_local = jnp.take(back_rows, local_owner, axis=0)
+    weights_local = jnp.take(back_rows, local_owner, axis=0, mode="clip")
     return (left_new, right_new, second_new, velocity_new, weight_new, weights_local)
 
 

time: 113 us -> 110 us (0.973)
  other arithmetic: 19.1 us -> 13.9 us
  waiting for transfers between devices: 44 us -> 45.6 us
    ppermute x2, waiting for transfers between devices: 1.23 us -> 8.88 us  [gather_rows(): from_right = lax.ppermute(piece, 'tensor', left)]
    ppermute x2, waiting for transfers between devices: 9.43 us -> 4.46 us  [gather_rows(): from_left = lax.ppermute(piece, 'tensor', right)]
    select_n x4 -> x3, other arithmetic: 3.7 us -> 1.3 us  [pick(): return jnp.where(valid[:, None, None], taken, jnp.zeros((), source.dtype))]
    gather x1 -> x2, local copies, waits for them, and re-layouts: 1.79 us -> 4.16 us  [the longest x1 2.55 us: on_device(): weights_local = jnp.take(back_rows, local_owner, axis=0, mode='clip')]
    ppermute x2, starting transfers between devices: 2.4 us -> 0.15 us  [gather_rows(): from_left = lax.ppermute(piece, 'tensor', right)]
    gather x4 -> x3, local copies, waits for them, and re-layouts: 3.65 us -> 1.75 us  [pick(): taken = jnp.take(source, index, axis=0, mode='clip')]
    ppermute x1, waiting for transfers between devices: 2.88 us -> 1.39 us  [gather_rows(): far = lax.ppermute(from_left, 'tensor', right)]
  transfers between devices with their start and end apart: 10 -> 10, of which waited for: 8 -> 9; matrix products, arithmetic and copies ran while one was open for 18% -> 17% of each run, Pallas kernels for 0% -> 0%
where the time goes in v8:
time: 110 us
  waiting for transfers between devices  45.6 us (41%)
  starting transfers between devices  26 us (24%)
  matrix products  16.4 us (15%)
  other arithmetic  13.9 us (13%)
  local copies, waits for them, and re-layouts  7.19 us (7%)
    all_to_all x1, waiting for transfers between devices, on_device(): lax.all_to_all(outgoing, 'shard', split_axis=0, concat_axis=0, tiled=True)  15.7 us
    all_to_all x1, waiting for transfers between devices, on_device(): lax.all_to_all(returning, 'shard', split_axis=0, concat_axis=0, tiled=True)  10.2 us
    dot_general x2, matrix products, on_device(): jnp.einsum('kij,kjl->kil', mixed, root_right[lo:lo + half], precision=thr...  9.59 us
    ppermute x2, waiting for transfers between devices, gather_rows(): from_right = lax.ppermute(piece, 'tensor', left)  8.88 us
    all_to_all x1, starting transfers between devices, on_device(): lax.all_to_all(outgoing, 'shard', split_axis=0, concat_axis=0, tiled=True)  8.71 us
    all_to_all x1, starting transfers between devices, on_device(): lax.all_to_all(returning, 'shard', split_axis=0, concat_axis=0, tiled=True)  7.92 us
    ppermute x2, waiting for transfers between devices, on_device(): lax.ppermute(sums, 'tensor', [(i, i ^ step) for i in range(splits)])  4.98 us
    convert_element_type x1, other arithmetic, on_device(): weight_half = weight_new.astype(jnp.bfloat16)  4.49 us
  transfers between devices with their start and end apart: 10, of which 9 were waited for; matrix products, arithmetic and copies ran while one was open for 17% of the time, Pallas kernels for 0%

profile of v8, /device:TPU:1, one launch (start us, length us, event | category | flops | bytes accessed | tf_op | source)
XLA Modules:
  0.0 109.9 jit_solution(9923162400664072301)
XLA Ops:
  0.7 0.8 reshape.53
  1.5 0.6 iota_reduce_fusion.2
  2.2 0.6 gather_fusion
  2.8 1.1 %broadcast_select_fusion = bf16[32,64,256]{2,1,0:T(8,128)(2,1)} fusion(bf16[32,64,256]{2,1,0:T(8,128)(2,1)S(1)} %gather_fusion, pred[32]{0:T(512)(128)(4,1)S(1)} %fusion.25), kind=kLoop, calls=%fused_computation.35 | loop fusion | flops 524288 | bytes 2097184 | tf_op jit(solution)/shard_map/jit(_where)/select_n | solution.py:33
  4.0 8.7 %all-to-all-start = ((bf16[32,64,256]{2,1,0:T(8,128)(2,1)}), bf16[32,64,256]{2,1,0:T(8,128)(2,1)S(1)}, u32[]{:S(2)}, u32[]{:S(2)}) async-start(bf16[32,64,256]{2,1,0:T(8,128)(2,1)} %broadcast_select_fusion), calls=%async_computation | async-start | bytes 2097152 | tf_op jit(solution)/shard_map/all_to_all | solution.py:64
  13.1 0.6 iota_reduce_fusion.1
  13.9 15.7 %all-to-all-done = bf16[32,64,256]{2,1,0:T(8,128)(2,1)S(1)} async-done(((bf16[32,64,256]{2,1,0:T(8,128)(2,1)}), bf16[32,64,256]{2,1,0:T(8,128)(2,1)S(1)}, u32[]{:S(2)}, u32[]{:S(2)}) %all-to-all-start) | async-done | bytes 1048608 | tf_op jit(solution)/shard_map/all_to_all | solution.py:64
  29.6 0.6 gather_fusion.2
  30.3 3.8 %collective-permute-start.3 = (bf16[12,64,256]{2,1,0:T(8,128)(2,1)S(1)}, bf16[12,64,256]{2,1,0:T(8,128)(2,1)S(1)}, u32[]{:S(2)}, u32[]{:S(2)}) collective-permute-start(bf16[12,64,256]{2,1,0:T(8,128)(2,1)S(1)} %broadcast_select_fusion.1), channel_id=1, source_target_pairs={{0,3},{1,0},{2,1},{3,2},{4,7},{5,4},{6,5},{7,6},{8,11},{9,8},{10,9... | collective-permute-start | bytes 1179656 | tf_op jit(solution)/shard_map/ppermute | solution.py:18
  34.9 7.5 %collective-permute-done.3 = bf16[12,64,256]{2,1,0:T(8,128)(2,1)S(1)} collective-permute-done((bf16[12,64,256]{2,1,0:T(8,128)(2,1)S(1)}, bf16[12,64,256]{2,1,0:T(8,128)(2,1)S(1)}, u32[]{:S(2)}, u32[]{:S(2)}) %collective-permute-start.3) | collective-permute-done | bytes 393248 | tf_op jit(solution)/shard_map/ppermute | solution.py:18
  42.4 3.4 %collective-permute-start.4 = (bf16[12,64,256]{2,1,0:T(8,128)(2,1)S(1)}, bf16[12,64,256]{2,1,0:T(8,128)(2,1)S(1)}, u32[]{:S(2)}, u32[]{:S(2)}) collective-permute-start(bf16[12,64,256]{2,1,0:T(8,128)(2,1)S(1)} %collective-permute-done.3), channel_id=1, source_target_pairs={{0,3},{1,0},{2,1},{3,2},{4,7},{5,4},{6,5},{7,6},{8,11},{9,8},{10,9... | collective-permute-start | bytes 1179656 | tf_op jit(solution)/shard_map/ppermute | solution.py:22
  46.3 1.0 collective-permute-start.2
  47.3 3.4 %fusion.11 = (f32[24]{0:T(128)S(1)}, f32[24,64,256]{2,1,0:T(8,128)}) fusion(bf16[12,64,256]{2,1,0:T(8,128)(2,1)S(1)} %broadcast_select_fusion.1, bf16[12,64,256]{2,1,0:T(8,128)(2,1)S(1)} %broadcast_select_fusion.2, f32[24,64,256]{2,1,0:T(8,128)} %param.25), kind=kLoop, calls=%fused_computation.32 | loop fusion | flops 3932136 | bytes 3932256 | tf_op jit(solution)/shard_map/reduce_sum | solution.py:100
  50.7 4.0 %collective-permute-done.5 = bf16[12,64,256]{2,1,0:T(8,128)(2,1)S(1)} collective-permute-done((bf16[12,64,256]{2,1,0:T(8,128)(2,1)S(1)}, bf16[12,64,256]{2,1,0:T(8,128)(2,1)S(1)}, u32[]{:S(2)}, u32[]{:S(2)}) %collective-permute-start.5) | collective-permute-done | bytes 393248 | tf_op jit(solution)/shard_map/ppermute | solution.py:17
  54.8 1.3 %conditional.3 = (bf16[12,256,256]{2,1,0:T(8,128)(2,1)}) conditional(s32[]{:T(128)} %clamp.4, (bf16[12,64,256]{2,1,0:T(8,128)(2,1)S(1)}, bf16[12,64,256]{2,1,0:T(8,128)(2,1)S(1)}, bf16[12,64,256]{2,1,0:T(8,128)(2,1)S(1)}, bf16[12,64,256]{2,1,0:T(8,128)(2,1)S(1)}) %tuple.42, (bf16[12,64,256]{2,1,0:T(8,128)(2,1)S(1)}, ...), branch_computations={%region_9.10_spmd, %region_10.11_spmd, %region_11.12_spmd, %region... | conditional | flops 6291456 | bytes 3145736 | solution.py:28
  54.8 1.3 %pad_maximum_fusion.4 = bf16[12,256,256]{2,1,0:T(8,128)(2,1)} fusion(bf16[12,64,256]{2,1,0:T(8,128)(2,1)S(1)} %get-tuple-element.93, bf16[12,64,256]{2,1,0:T(8,128)(2,1)S(1)} %get-tuple-element.92, bf16[12,64,256]{2,1,0:T(8,128)(2,1)S(1)} %get-tuple-element.91, bf16[12,64,256]{2,1,0:T(8,128)(2,1)S(1)} %get-tuple-element.90), kind=kLoop, calls=%fused_computation.9 | loop fusion | flops 6291456 | bytes 3145728 | tf_op jit(solution)/shard_map/cond/branch_0_fun/concatenate | solution.py:26
  56.0 4.4 %multiply_reduce_fusion = (f32[12]{0:T(128)S(1)}, f32[12,64,256]{2,1,0:T(8,128)S(1)}) fusion(f32[24,256,256]{2,1,0:T(8,128)} %param.24, bf16[12,256,256]{2,1,0:T(8,128)(2,1)} %get-tuple-element.136, f32[24,64,256]{2,1,0:T(8,128)} %param.23), kind=kOutput, calls=%fused_computation.37 | convolution fusion | flops 604372992 | bytes 6291504 | tf_op jit(solution)/shard_map/kij,kjl->kil/dot_general | solution.py:93
  60.4 1.4 %collective-permute-done = bf16[12,64,256]{2,1,0:T(8,128)(2,1)S(1)} collective-permute-done((bf16[12,64,256]{2,1,0:T(8,128)(2,1)S(1)}, bf16[12,64,256]{2,1,0:T(8,128)(2,1)S(1)}, u32[]{:S(2)}, u32[]{:S(2)}) %collective-permute-start) | collective-permute-done | bytes 393248 | tf_op jit(solution)/shard_map/ppermute | solution.py:18
  61.8 1.4 %collective-permute-done.2 = bf16[12,64,256]{2,1,0:T(8,128)(2,1)S(1)} collective-permute-done((bf16[12,64,256]{2,1,0:T(8,128)(2,1)S(1)}, bf16[12,64,256]{2,1,0:T(8,128)(2,1)S(1)}, u32[]{:S(2)}, u32[]{:S(2)}) %collective-permute-start.2) | collective-permute-done | bytes 393248 | tf_op jit(solution)/shard_map/ppermute | solution.py:20
  63.2 1.3 %conditional.2 = (bf16[12,256,256]{2,1,0:T(8,128)(2,1)}) conditional(s32[]{:T(128)} %clamp.4, (bf16[12,64,256]{2,1,0:T(8,128)(2,1)S(1)}, bf16[12,64,256]{2,1,0:T(8,128)(2,1)S(1)}, bf16[12,64,256]{2,1,0:T(8,128)(2,1)S(1)}, bf16[12,64,256]{2,1,0:T(8,128)(2,1)S(1)}) %tuple.38, (bf16[12,64,256]{2,1,0:T(8,128)(2,1)S(1)}, ...), branch_computations={%region_5.6_spmd, %region_6.7_spmd, %region_7.8_spmd, %region_8.9_... | conditional | flops 6291456 | bytes 3145736 | solution.py:28
  63.2 1.3 %pad_maximum_fusion = bf16[12,256,256]{2,1,0:T(8,128)(2,1)} fusion(bf16[12,64,256]{2,1,0:T(8,128)(2,1)S(1)} %get-tuple-element.72, bf16[12,64,256]{2,1,0:T(8,128)(2,1)S(1)} %get-tuple-element.71, bf16[12,64,256]{2,1,0:T(8,128)(2,1)S(1)} %get-tuple-element.70, bf16[12,64,256]{2,1,0:T(8,128)(2,1)S(1)} %get-tuple-element.64), kind=kLoop, calls=%fused_computation.5 | loop fusion | flops 6291456 | bytes 3145728 | tf_op jit(solution)/shard_map/cond/branch_0_fun/concatenate | solution.py:26
  64.4 5.2 %multiply_reduce_fusion.1 = (f32[12]{0:T(128)S(1)}, f32[12,64,256]{2,1,0:T(8,128)}) fusion(f32[24,256,256]{2,1,0:T(8,128)} %param.24, bf16[12,256,256]{2,1,0:T(8,128)(2,1)} %get-tuple-element.135, f32[24,64,256]{2,1,0:T(8,128)} %param.23), kind=kOutput, calls=%fused_computation.39 | convolution fusion | flops 604372992 | bytes 6291504 | tf_op jit(solution)/shard_map/kij,kjl->kil/dot_general | solution.py:93
  69.7 0.9 collective-permute-start.6
  71.1 2.6 %collective-permute-done.6 = f32[2,24]{1,0:T(2,128)S(1)} collective-permute-done((f32[2,24]{1,0:T(2,128)S(1)}, f32[2,24]{1,0:T(2,128)S(1)}, u32[]{:S(2)}, u32[]{:S(2)}) %collective-permute-start.6) | collective-permute-done | bytes 224 | tf_op jit(solution)/shard_map/ppermute | solution.py:104
  73.8 2.4 %collective-permute-done.7 = f32[2,24]{1,0:T(2,128)S(1)} collective-permute-done((f32[2,24]{1,0:T(2,128)S(1)}, f32[2,24]{1,0:T(2,128)S(1)}, u32[]{:S(2)}, u32[]{:S(2)}) %collective-permute-start.7) | collective-permute-done | bytes 224 | tf_op jit(solution)/shard_map/ppermute | solution.py:104
  76.3 4.5 %fusion.31 = (bf16[24,64,256]{2,1,0:T(8,128)(2,1)S(1)}, f32[24,64,256]{2,1,0:T(8,128)}, f32[24,64,256]{2,1,0:T(8,128)}) fusion(f32[24,64,256]{2,1,0:T(8,128)} %param.27, f32[12,64,256]{2,1,0:T(8,128)S(1)} %get-tuple-element.130, f32[12,64,256]{2,1,0:T(8,128)} %get-tuple-element.132, f32[24]{0:T(128)S(1)} %multiply_bitcast_fusion, f32[24,64,256]{2,1,0:T(8,128)} %param.26), kind=kLoop, calls=%fused_computation.67 | loop fusion | flops 2752512 | bytes 8650848 | tf_op jit(solution)/shard_map/convert_element_type | solution.py:113
  80.7 1.6 %gather_fusion.3 = bf16[32,64,256]{2,1,0:T(8,128)(2,1)} fusion(bf16[24,64,256]{2,1,0:T(8,128)(2,1)S(1)} %get-tuple-element.120, s32[1024]{0:T(1024)S(1)} %pad_clamp_fusion.1), kind=kCustom, calls=%fused_computation.3 | custom fusion | bytes 2097280 | tf_op jit(solution)/shard_map/jit(_take)/gather | solution.py:114
  82.4 7.9 %all-to-all-start.1 = ((bf16[32,64,256]{2,1,0:T(8,128)(2,1)}), bf16[32,64,256]{2,1,0:T(8,128)(2,1)}, u32[]{:S(2)}, u32[]{:S(2)}) async-start(bf16[32,64,256]{2,1,0:T(8,128)(2,1)} %gather_fusion.3), calls=%async_computation.1 | async-start | bytes 2097152 | tf_op jit(solution)/shard_map/all_to_all | solution.py:115
  90.3 4.2 %multiply_add_fusion.1 = f32[24,64,256]{2,1,0:T(8,128)} fusion(f32[24,64,256]{2,1,0:T(8,128)} %param.21, bf16[12,256,256]{2,1,0:T(8,128)(2,1)S(1)} %copy-done.1, bf16[12,256,256]{2,1,0:T(8,128)(2,1)} %get-tuple-element.135, bf16[12,64,256]{2,1,0:T(8,128)(2,1)S(1)} %broadcast_select_fusion.1, bf16[12,64,256]{2,1,0:T(8,128)(2,1)S(1)} %broadcast_select_fusion.2), kind=kOutput, calls=%fused_computation.31 | convolution fusion | flops 204472320 | bytes 7077888 | tf_op jit(solution)/shard_map/kij,klj->kil/dot_general | solution.py:76
  94.6 2.5 %multiply_add_fusion = f32[24,64,256]{2,1,0:T(8,128)} fusion(f32[24,64,256]{2,1,0:T(8,128)S(1)} %copy-done.4, bf16[12,256,256]{2,1,0:T(8,128)(2,1)S(1)} %copy-done.1, bf16[12,256,256]{2,1,0:T(8,128)(2,1)S(1)} %copy-done.2, s32[]{:T(128)S(6)} %select_n.34), kind=kOutput, calls=%fused_computation.30 | convolution fusion | flops 205651968 | bytes 9437188 | tf_op jit(solution)/shard_map/kji,kjl->kil/dot_general | solution.py:79
  97.1 10.2 %all-to-all-done.1 = bf16[32,64,256]{2,1,0:T(8,128)(2,1)} async-done(((bf16[32,64,256]{2,1,0:T(8,128)(2,1)}), bf16[32,64,256]{2,1,0:T(8,128)(2,1)}, u32[]{:S(2)}, u32[]{:S(2)}) %all-to-all-start.1) | async-done | bytes 1048608 | tf_op jit(solution)/shard_map/all_to_all | solution.py:115
  107.3 2.6 %gather_fusion.4 = bf16[12,64,256]{2,1,0:T(8,128)(2,1)} fusion(bf16[32,64,256]{2,1,0:T(8,128)(2,1)} %all-to-all-done.1, s32[1024]{0:T(1024)S(1)} %pad_clamp_fusion), kind=kCustom, calls=%fused_computation.4 | custom fusion | bytes 786480 | tf_op jit(solution)/shard_map/jit(_take)/gather | solution.py:116
  (38 shorter events, 2.9 us)
Async XLA Ops:
  0.6 1.6 %copy-start = (bf16[12,64,256]{2,1,0:T(8,128)(2,1)S(1)}, bf16[12,64,256]{2,1,0:T(8,128)(2,1)}, u32[]{:S(2)}) copy-start(bf16[12,64,256]{2,1,0:T(8,128)(2,1)} %param.18) | copy-start | bytes 1179652
  4.0 8.7 %copy-start.3 = (s32[384]{0:T(512)S(1)}, s32[384]{0:T(512)}, u32[]{:S(2)}) copy-start(s32[384]{0:T(512)} %param.20) | copy-start | bytes 4612
  4.0 25.6 %all-to-all-start = ((bf16[32,64,256]{2,1,0:T(8,128)(2,1)}), bf16[32,64,256]{2,1,0:T(8,128)(2,1)S(1)}, u32[]{:S(2)}, u32[]{:S(2)}) async-start(bf16[32,64,256]{2,1,0:T(8,128)(2,1)} %broadcast_select_fusion), calls=%async_computation | async-start | bytes 2097152 | tf_op jit(solution)/shard_map/all_to_all | solution.py:64
  30.3 12.2 %collective-permute-start.3 = (bf16[12,64,256]{2,1,0:T(8,128)(2,1)S(1)}, bf16[12,64,256]{2,1,0:T(8,128)(2,1)S(1)}, u32[]{:S(2)}, u32[]{:S(2)}) collective-permute-start(bf16[12,64,256]{2,1,0:T(8,128)(2,1)S(1)} %broadcast_select_fusion.1), channel_id=1, source_target_pairs={{0,3},{1,0},{2,1},{3,2},{4,7},{5,4},{6,5},{7,6},{8,11},{9,8},{10,9... | collective-permute-start | bytes 1179656 | tf_op jit(solution)/shard_map/ppermute | solution.py:18
  34.8 11.6 %collective-permute-start.1 = (bf16[12,64,256]{2,1,0:T(8,128)(2,1)S(1)}, bf16[12,64,256]{2,1,0:T(8,128)(2,1)S(1)}, u32[]{:S(2)}, u32[]{:S(2)}) collective-permute-start(bf16[12,64,256]{2,1,0:T(8,128)(2,1)S(1)} %broadcast_select_fusion.2), channel_id=1, source_target_pairs={{0,1},{1,2},{2,3},{3,0},{4,5},{5,6},{6,7},{7,4},{8,9},{9,10},{10,1... | collective-permute-start | bytes 1179656 | tf_op jit(solution)/shard_map/ppermute | solution.py:17
  34.9 19.9 %collective-permute-start.5 = (bf16[12,64,256]{2,1,0:T(8,128)(2,1)S(1)}, bf16[12,64,256]{2,1,0:T(8,128)(2,1)S(1)}, u32[]{:S(2)}, u32[]{:S(2)}) collective-permute-start(bf16[12,64,256]{2,1,0:T(8,128)(2,1)S(1)} %broadcast_select_fusion.1), channel_id=1, source_target_pairs={{0,1},{1,2},{2,3},{3,0},{4,5},{5,6},{6,7},{7,4},{8,9},{9,10},{10,1... | collective-permute-start | bytes 1179656 | tf_op jit(solution)/shard_map/ppermute | solution.py:17
  42.4 12.3 %collective-permute-start.4 = (bf16[12,64,256]{2,1,0:T(8,128)(2,1)S(1)}, bf16[12,64,256]{2,1,0:T(8,128)(2,1)S(1)}, u32[]{:S(2)}, u32[]{:S(2)}) collective-permute-start(bf16[12,64,256]{2,1,0:T(8,128)(2,1)S(1)} %collective-permute-done.3), channel_id=1, source_target_pairs={{0,3},{1,0},{2,1},{3,2},{4,7},{5,4},{6,5},{7,6},{8,11},{9,8},{10,9... | collective-permute-start | bytes 1179656 | tf_op jit(solution)/shard_map/ppermute | solution.py:22
  45.9 15.9 %collective-permute-start = (bf16[12,64,256]{2,1,0:T(8,128)(2,1)S(1)}, bf16[12,64,256]{2,1,0:T(8,128)(2,1)S(1)}, u32[]{:S(2)}, u32[]{:S(2)}) collective-permute-start(bf16[12,64,256]{2,1,0:T(8,128)(2,1)S(1)} %broadcast_select_fusion.2), channel_id=1, source_target_pairs={{0,3},{1,0},{2,1},{3,2},{4,7},{5,4},{6,5},{7,6},{8,11},{9,8},{10,9... | collective-permute-start | bytes 1179656 | tf_op jit(solution)/shard_map/ppermute | solution.py:18
  46.3 16.9 %collective-permute-start.2 = (bf16[12,64,256]{2,1,0:T(8,128)(2,1)S(1)}, bf16[12,64,256]{2,1,0:T(8,128)(2,1)S(1)}, u32[]{:S(2)}, u32[]{:S(2)}) collective-permute-start(bf16[12,64,256]{2,1,0:T(8,128)(2,1)S(1)} %collective-permute-done.1), channel_id=1, source_target_pairs={{0,1},{1,2},{2,3},{3,0},{4,5},{5,6},{6,7},{7,4},{8,9},{9,10},{10,1... | collective-permute-start | bytes 1179656 | tf_op jit(solution)/shard_map/ppermute | solution.py:20
  69.7 4.0 %collective-permute-start.6 = (f32[2,24]{1,0:T(2,128)S(1)}, f32[2,24]{1,0:T(2,128)S(1)}, u32[]{:S(2)}, u32[]{:S(2)}) collective-permute-start(f32[2,24]{1,0:T(2,128)S(1)} %pad_maximum_fusion.17), channel_id=1, source_target_pairs={{0,2},{1,3},{2,0},{3,1},{4,6},{5,7},{6,4},{7,5},{8,10},{9,11},{10,... | collective-permute-start | bytes 584 | tf_op jit(solution)/shard_map/ppermute | solution.py:104
  73.7 2.5 %collective-permute-start.7 = (f32[2,24]{1,0:T(2,128)S(1)}, f32[2,24]{1,0:T(2,128)S(1)}, u32[]{:S(2)}, u32[]{:S(2)}) collective-permute-start(f32[2,24]{1,0:T(2,128)S(1)} %fusion.30), channel_id=1, source_target_pairs={{0,1},{1,0},{2,3},{3,2},{4,5},{5,4},{6,7},{7,6},{8,9},{9,8},{10,11... | collective-permute-start | bytes 584 | tf_op jit(solution)/shard_map/ppermute | solution.py:104
  82.3 7.9 %copy-start.1 = (bf16[12,256,256]{2,1,0:T(8,128)(2,1)S(1)}, bf16[12,256,256]{2,1,0:T(8,128)(2,1)}, u32[]{:S(2)}) copy-start(bf16[12,256,256]{2,1,0:T(8,128)(2,1)} %get-tuple-element.136) | copy-start | bytes 4718596
  82.4 25.0 %all-to-all-start.1 = ((bf16[32,64,256]{2,1,0:T(8,128)(2,1)}), bf16[32,64,256]{2,1,0:T(8,128)(2,1)}, u32[]{:S(2)}, u32[]{:S(2)}) async-start(bf16[32,64,256]{2,1,0:T(8,128)(2,1)} %gather_fusion.3), calls=%async_computation.1 | async-start | bytes 2097152 | tf_op jit(solution)/shard_map/all_to_all | solution.py:115
  90.3 4.3 %copy-start.2 = (bf16[12,256,256]{2,1,0:T(8,128)(2,1)S(1)}, bf16[12,256,256]{2,1,0:T(8,128)(2,1)}, u32[]{:S(2)}) copy-start(bf16[12,256,256]{2,1,0:T(8,128)(2,1)} %get-tuple-element.135) | copy-start | bytes 4718596
  90.3 4.3 %copy-start.4 = (f32[24,64,256]{2,1,0:T(8,128)S(1)}, f32[24,64,256]{2,1,0:T(8,128)}, u32[]{:S(2)}) copy-start(f32[24,64,256]{2,1,0:T(8,128)} %param.22) | copy-start | bytes 4718596
